TPU v7x, 1024 devices: a whole 4x4x32 slice. The times are simulated.
1024 devices in a mesh: gx: 4 (over y), gy: 8 (over x, core), gz: 32 (over z).
Axes of the slice: x: 4, y: 4, z: 32, core: 2. Of those that a mesh axis runs over, the one named last changes fastest.
Arguments:
- element_load: float32 [160, 136, 512], P('gz', 'gy', 'gx'), may hold values from -6 to 6
- conductivity: float32 [64, 64, 256], P('gz', 'gy', 'gx'), may hold values from 0.2 to 5
Outputs:
- corrected: float32 [160, 136, 512], P('gz', 'gy', 'gx')
All inputs are finite; a program needn't handle non-finite values.
Results may differ from a plain program's by a relative error of at most 0.00002.
Values sent between devices are 32-bit elements; how exact they have to be, the bound alone decides.
No kernel may reach another device: no remote copies, remote signals or barrier semaphores. Data moves between devices by JAX's collectives and lax.ppermute only.
A program may use at most 32 MiB of HBM per device.

v0:
```python
import jax
import jax.numpy as jnp
import numpy as np
from jax import lax
from jax.sharding import PartitionSpec as P

DEG1 = 3
DEG2 = 4


reaction_rate = 0.05
lower_bound = 0.25
upper_bound = 2.5
mass_table = [
    [4.0 / 30.0, 2.0 / 30.0, -1.0 / 30.0],
    [2.0 / 30.0, 16.0 / 30.0, 2.0 / 30.0],
    [-1.0 / 30.0, 2.0 / 30.0, 4.0 / 30.0],
]
stiff_table = [
    [7.0 / 3.0, -8.0 / 3.0, 1.0 / 3.0],
    [-8.0 / 3.0, 16.0 / 3.0, -8.0 / 3.0],
    [1.0 / 3.0, -8.0 / 3.0, 7.0 / 3.0],
]


def padded(cells, sides, width):
    for axis, dim in sides:
        count = lax.axis_size(axis)
        head = lax.slice_in_dim(cells, 0, width, axis=dim)
        tail = lax.slice_in_dim(cells, cells.shape[dim] - width, cells.shape[dim], axis=dim)
        cells = jnp.concatenate(
            [
                lax.ppermute(tail, axis, [(i, (i + 1) % count) for i in range(count)]),
                cells,
                lax.ppermute(head, axis, [((i + 1) % count, i) for i in range(count)]),
            ],
            axis=dim,
        )
    return cells


def pad_axis(values, which_axis, before, after):
    widths = [(0, 0)] * values.ndim
    widths[which_axis] = (before, after)
    return jnp.pad(values, widths)


def contract(values, matrix, which_axis):
    pieces = [lax.index_in_dim(values, a, which_axis, keepdims=False) for a in range(3)]
    results = [
        matrix[b][0] * pieces[0] + matrix[b][1] * pieces[1] + matrix[b][2] * pieces[2]
        for b in range(3)
    ]
    return jnp.stack(results, axis=which_axis)


def node_slices(node_field, which_axis):
    elements = (node_field.shape[which_axis] - 1) // 2
    return [
        lax.slice_in_dim(node_field, a, a + 2 * elements - 1, 2, axis=which_axis) for a in range(3)
    ]


def spread(node_field):
    length_x = node_field.shape[2]
    elements_x = (length_x - 1) // 2
    even_x = lax.slice_in_dim(node_field, 0, length_x, 2, axis=2)
    odd_x = lax.slice_in_dim(node_field, 1, length_x, 2, axis=2)
    along_x = jnp.stack(
        [
            lax.slice_in_dim(even_x, 0, elements_x, axis=2),
            odd_x,
            lax.slice_in_dim(even_x, 1, elements_x + 1, axis=2),
        ],
        0,
    )
    along_y = jnp.stack(node_slices(along_x, 2), 1)
    return jnp.stack(node_slices(along_y, 2), 2)


def fold_back(stacked, which_axis):
    lower_part = stacked[0]
    middle_part = stacked[1]
    upper_part = stacked[2]
    target = which_axis - 1
    elements = lower_part.shape[target]
    even_full = pad_axis(lower_part, target, 0, 1) + pad_axis(upper_part, target, 1, 0)
    even_nodes = lax.slice_in_dim(even_full, 0, elements, axis=target)
    tail_node = lax.slice_in_dim(even_full, elements, elements + 1, axis=target)
    woven_nodes = jnp.stack([even_nodes, middle_part], axis=target + 1)
    node_shape = list(even_nodes.shape)
    node_shape[target] = 2 * elements
    woven_nodes = woven_nodes.reshape(node_shape)
    return jnp.concatenate([woven_nodes, tail_node], axis=target)


def fold_local(stacked, local_dim, target):
    parts = [lax.index_in_dim(stacked, a, local_dim, keepdims=False) for a in range(3)]
    return fold_back(parts, target + 1)


def gather_elements(product):
    folded = fold_local(product, 2, 2)
    folded = fold_local(folded, 1, 2)
    return fold_local(folded, 0, 2)


def apply_local(node_field, conduct, stiff_scale, mass_scale):
    node_values = spread(node_field)
    mass_depth = contract(node_values, mass_table, 2)
    mass_plane = contract(mass_depth, mass_table, 1)
    stiffness = contract(mass_plane, stiff_table, 0)
    mass_width = contract(node_values, mass_table, 0)
    stiffness = stiffness + contract(contract(mass_width, stiff_table, 1), mass_table, 2)
    mass_face = contract(mass_width, mass_table, 1)
    stiffness = stiffness + contract(mass_face, stiff_table, 2)
    product = stiff_scale * conduct * stiffness + mass_scale * contract(mass_face, mass_table, 2)
    return gather_elements(product)


def diag_tables():
    stiff_line = np.array([stiff_table[a][a] for a in range(3)])
    mass_line = np.array([mass_table[a][a] for a in range(3)])
    stiff_part = (
        stiff_line[:, None, None] * mass_line[None, :, None] * mass_line[None, None, :]
        + mass_line[:, None, None] * stiff_line[None, :, None] * mass_line[None, None, :]
        + mass_line[:, None, None] * mass_line[None, :, None] * stiff_line[None, None, :]
    )
    mass_part = mass_line[:, None, None] * mass_line[None, :, None] * mass_line[None, None, :]
    return (stiff_part.reshape(3, 3, 3, 1, 1, 1), mass_part.reshape(3, 3, 3, 1, 1, 1))


def diag_local(conduct, stiff_scale, mass_scale):
    stiff_part, mass_part = diag_tables()
    product = stiff_scale * conduct * jnp.asarray(
        stiff_part, conduct.dtype
    ) + mass_scale * jnp.asarray(mass_part, conduct.dtype)
    return gather_elements(product)


def coarse_conduct(conduct):
    layers_z, rows_y, cols_x = conduct.shape
    shaped = conduct.reshape(layers_z // 2, 2, rows_y // 2, 2, cols_x // 2, 2)
    return jnp.sum(shaped, axis=(1, 3, 5)) * 0.125


def prolong_axis(coarse, which_axis):
    pieces = node_slices(coarse, which_axis)
    fine_parts = [
        pieces[0],
        0.375 * pieces[0] + 0.75 * pieces[1] - 0.125 * pieces[2],
        pieces[1],
        -0.125 * pieces[0] + 0.75 * pieces[1] + 0.375 * pieces[2],
    ]
    woven_nodes = jnp.stack(fine_parts, axis=which_axis + 1)
    node_shape = list(pieces[0].shape)
    node_shape[which_axis] = 4 * pieces[0].shape[which_axis]
    woven_nodes = woven_nodes.reshape(node_shape)
    length_here = coarse.shape[which_axis]
    tail_node = lax.slice_in_dim(coarse, length_here - 1, length_here, axis=which_axis)
    return jnp.concatenate([woven_nodes, tail_node], axis=which_axis)


def prolong_all(coarse):
    result = prolong_axis(coarse, 0)
    result = prolong_axis(result, 1)
    return prolong_axis(result, 2)


def restrict_axis(fine, which_axis):
    length_here = fine.shape[which_axis]
    elements = (length_here - 1) // 4
    quarters = [
        lax.slice_in_dim(fine, q, q + 4 * elements - 3, 4, axis=which_axis) for q in range(4)
    ]
    coarse_parts = [
        quarters[0] + 0.375 * quarters[1] - 0.125 * quarters[3],
        0.75 * quarters[1] + quarters[2] + 0.75 * quarters[3],
        -0.125 * quarters[1] + 0.375 * quarters[3],
    ]
    folded = fold_back(jnp.stack(coarse_parts, 0), which_axis + 1)
    tail_node = lax.slice_in_dim(fine, length_here - 1, length_here, axis=which_axis)
    return folded + pad_axis(tail_node, which_axis, 2 * elements, 0)


def restrict_all(fine):
    result = restrict_axis(fine, 0)
    result = restrict_axis(result, 1)
    return restrict_axis(result, 2)


def chebyshev(right_side, diagonal, operate, degree):
    centre = 0.5 * (upper_bound + lower_bound)
    half_width = 0.5 * (upper_bound - lower_bound)
    sharpness = centre / half_width
    factor = 1.0 / sharpness
    scaled = 1.0 / diagonal
    update = scaled * right_side * (1.0 / centre)
    solution = update
    for k in range(1, degree):
        residual = right_side - operate(solution)
        next_factor = 1.0 / (2.0 * sharpness - factor)
        update = next_factor * factor * update + 2.0 * next_factor / half_width * (
            scaled * residual
        )
        solution = solution + update
        factor = next_factor
    return solution


def merge_rims(extended, which_axis):
    length_here = extended.shape[which_axis]
    inner_part = lax.slice_in_dim(extended, 1, length_here - 1, axis=which_axis)
    below_rim = lax.slice_in_dim(extended, 0, 1, axis=which_axis)
    above_rim = lax.slice_in_dim(extended, length_here - 1, length_here, axis=which_axis)
    return (
        inner_part
        + pad_axis(below_rim, which_axis, 0, length_here - 3)
        + pad_axis(above_rim, which_axis, length_here - 3, 0)
    )


def merge_all(extended, axes_list):
    for which_axis in axes_list:
        extended = merge_rims(extended, which_axis)
    return extended


def faces_fine(stacked):
    extended = padded(stacked, (("gx", 3), ("gy", 2), ("gz", 1)), 1)
    return merge_all(extended, (1, 2, 3))


def coarse_sums(stacked):
    extended = padded(stacked, (("gx", 3), ("gy", 2), ("gz", 1)), 1)
    return merge_all(extended, (1, 2, 3))


def widened(stacked, sides, width):
    for axis, dim in sides:
        count = lax.axis_size(axis)
        length_here = stacked.shape[dim]
        head = lax.slice_in_dim(stacked, 0, width, axis=dim)
        tail = lax.slice_in_dim(stacked, length_here - width, length_here, axis=dim)
        below = lax.ppermute(tail, axis, [(i, (i + 1) % count) for i in range(count)])
        above = lax.ppermute(head, axis, [((i + 1) % count, i) for i in range(count)])
        stacked = jnp.concatenate(
            [
                lax.slice_in_dim(below, 0, width - 1, axis=dim),
                lax.slice_in_dim(below, width - 1, width, axis=dim)
                + lax.slice_in_dim(stacked, 0, 1, axis=dim),
                lax.slice_in_dim(stacked, 1, length_here - 1, axis=dim),
                lax.slice_in_dim(stacked, length_here - 1, length_here, axis=dim)
                + lax.slice_in_dim(above, 0, 1, axis=dim),
                lax.slice_in_dim(above, 1, width, axis=dim),
            ],
            axis=dim,
        )
    return stacked


def on_device(element_load, conductivity):
    load_full = pad_axis(element_load, 2, 0, 1)
    cond_nodes = jnp.zeros(load_full.shape, conductivity.dtype)
    cond_nodes = cond_nodes.at[:-1:2, :-1:2, :-1:2].set(conductivity)
    ring = 2
    wide = widened(
        jnp.stack([load_full, diag_local(conductivity, 1.0, reaction_rate), cond_nodes], 0),
        (("gx", 3), ("gy", 2), ("gz", 1)),
        ring + 1,
    )
    inner = wide[:, ring:-ring, ring:-ring, ring:-ring]
    right_side = inner[0]
    diagonal = inner[1]
    cells = conductivity.shape
    cond_wide = wide[2, : 2 * cells[0] + 3 : 2, : 2 * cells[1] + 3 : 2, : 2 * cells[2] + 3 : 2]

    def operate_fine(node_field):
        return faces_fine(apply_local(node_field, conductivity, 1.0, reaction_rate)[None])[0]

    centre = 0.5 * (upper_bound + lower_bound)
    half_width = 0.5 * (upper_bound - lower_bound)
    sharpness = centre / half_width
    factor = 1.0 / sharpness
    scaled = 1.0 / diagonal
    update = scaled * right_side * (1.0 / centre)
    smooth = update
    first_wide = 1.0 / wide[1] * wide[0] * (1.0 / centre)
    applied_first = apply_local(first_wide, cond_wide, 1.0, reaction_rate)[
        ring:-ring, ring:-ring, ring:-ring
    ]
    for k in range(1, DEG1):
        if k == 1:
            residual = right_side - applied_first
        else:
            residual = right_side - operate_fine(smooth)
        next_factor = 1.0 / (2.0 * sharpness - factor)
        update = next_factor * factor * update + 2.0 * next_factor / half_width * (
            scaled * residual
        )
        smooth = smooth + update
        factor = next_factor
    partial_value = load_full - apply_local(smooth, conductivity, 1.0, reaction_rate)
    coarse_load = restrict_all(partial_value)
    coarse_cond = coarse_conduct(conductivity)
    coarse_mass = 8.0 * reaction_rate
    coarse_diag = diag_local(coarse_cond, 2.0, coarse_mass)
    coarse_both = coarse_sums(jnp.stack([coarse_load, coarse_diag], 0))

    def operate_coarse(node_field):
        return coarse_sums(apply_local(node_field, coarse_cond, 2.0, coarse_mass)[None])[0]

    correction = chebyshev(coarse_both[0], coarse_both[1], operate_coarse, DEG2)
    corrected = smooth + prolong_all(correction)
    return corrected[:, :, : corrected.shape[2] - 1]


def solution(mesh):
    in_specs = (P("gz", "gy", "gx"), P("gz", "gy", "gx"))
    out_specs = P("gz", "gy", "gx")
    return jax.shard_map(
        on_device, mesh=mesh, in_specs=in_specs, out_specs=out_specs, check_vma=False
    )
```

profile of v0, /device:TPU:24, one launch (start us, length us, event | category | flops | bytes accessed | tf_op | source)
XLA Modules:
  0.0 206.0 jit_solution(14538310438539352286)
XLA Ops:
  0.0 0.8 reshape.1397
  1.6 0.6 copy-done.12
  3.0 4.3 %scatter_custom_fusion = f32[10965]{0:T(1024)S(1)} fusion(s32[1024]{0:T(1024)S(1)} %reshape.1395, f32[1024]{0:T(1024)S(1)} %reshape.1397, f32[]{:T(128)} %constant.32.clone.1), kind=kCustom, calls=%fused_computation.593 | custom fusion | bytes 43864
  8.0 0.7 copy-done.1
  8.8 2.7 %collective-permute-start.1 = (f32[3,5,17,3]{3,2,1,0:T(8,128)S(1)}, f32[3,5,17,3]{3,2,1,0:T(8,128)S(1)}, u32[]{:S(2)}, u32[]{:S(2)}) collective-permute-start(f32[3,5,17,3]{3,2,1,0:T(8,128)S(1)} %get-tuple-element.58), channel_id=1, source_target_pairs={{256,0},{512,256},{768,512},{0,768},{257,1},{513,257},{769,513},{1... | collective-permute-start | bytes 9188 | tf_op jit(solution)/shard_map/ppermute | solution.py:246
  11.5 14.0 %collective-permute-start = (f32[3,5,17,3]{3,2,1,0:T(8,128)S(1)}, f32[3,5,17,3]{3,2,1,0:T(8,128)S(1)}, u32[]{:S(2)}, u32[]{:S(2)}) collective-permute-start(f32[3,5,17,3]{3,2,1,0:T(8,128)S(1)} %get-tuple-element.59), channel_id=1, source_target_pairs={{0,256},{256,512},{512,768},{768,0},{1,257},{257,513},{513,769},{7... | collective-permute-start | bytes 9188 | tf_op jit(solution)/shard_map/ppermute | solution.py:245
  27.2 1.3 collective-permute-done
  29.6 1.3 collective-permute-done.3
  30.9 3.0 %collective-permute-done.2 = f32[3,5,3,133]{3,2,1,0:T(4,128)S(1)} collective-permute-done((f32[3,5,3,133]{3,2,1,0:T(4,128)S(1)}, f32[3,5,3,133]{3,2,1,0:T(4,128)S(1)}, u32[]{:S(2)}, u32[]{:S(2)}) %collective-permute-start.2) | collective-permute-done | bytes 23972 | tf_op jit(solution)/shard_map/ppermute | solution.py:245
  34.4 1.9 collective-permute-start.4
  36.4 12.6 %collective-permute-done.4 = f32[3,3,21,133]{3,2,1,0:T(8,128)S(1)} collective-permute-done((f32[3,3,21,133]{3,2,1,0:T(8,128)S(1)}, f32[3,3,21,133]{3,2,1,0:T(8,128)S(1)}, u32[]{:S(2)}, u32[]{:S(2)}) %collective-permute-start.4) | collective-permute-done | bytes 100580 | tf_op jit(solution)/shard_map/ppermute | solution.py:245
  49.1 4.1 %collective-permute-start.5 = (f32[3,3,21,133]{3,2,1,0:T(8,128)S(1)}, f32[3,3,21,133]{3,2,1,0:T(8,128)S(1)}, u32[]{:S(2)}, u32[]{:S(2)}) collective-permute-start(f32[3,3,21,133]{3,2,1,0:T(8,128)S(1)} %get-tuple-element.51), channel_id=1, source_target_pairs={{1,0},{2,1},{3,2},{4,3},{5,4},{6,5},{7,6},{8,7},{9,8},{10,9},{11,1... | collective-permute-start | bytes 301652 | tf_op jit(solution)/shard_map/ppermute | solution.py:246
  53.3 3.6 %collective-permute-done.5 = f32[3,3,21,133]{3,2,1,0:T(8,128)S(1)} collective-permute-done((f32[3,3,21,133]{3,2,1,0:T(8,128)S(1)}, f32[3,3,21,133]{3,2,1,0:T(8,128)S(1)}, u32[]{:S(2)}, u32[]{:S(2)}) %collective-permute-start.5) | collective-permute-done | bytes 100580 | tf_op jit(solution)/shard_map/ppermute | solution.py:246
  56.9 0.9 slice.1356
  57.9 1.8 slice.1361
  59.6 1.8 slice.1359
  67.3 0.8 slice.1404
  68.1 0.8 slice.1402
  71.0 5.6 %collective-permute-start.6 = (f32[1,5,17,1]{3,2,1,0:T(8,128)S(1)}, f32[1,5,17,1]{3,2,1,0:T(8,128)S(1)}, u32[]{:S(2)}, u32[]{:S(2)}) collective-permute-start(f32[1,5,17,1]{3,2,1,0:T(8,128)S(1)} %get-tuple-element.165), channel_id=1, source_target_pairs={{0,256},{256,512},{512,768},{768,0},{1,257},{257,513},{513,769},{7... | collective-permute-start | bytes 1028 | tf_op jit(solution)/shard_map/ppermute | solution.py:33
  76.7 2.1 %collective-permute-start.7 = (f32[1,5,17,1]{3,2,1,0:T(8,128)S(1)}, f32[1,5,17,1]{3,2,1,0:T(8,128)S(1)}, u32[]{:S(2)}, u32[]{:S(2)}) collective-permute-start(f32[1,5,17,1]{3,2,1,0:T(8,128)S(1)} %get-tuple-element.166), channel_id=1, source_target_pairs={{256,0},{512,256},{768,512},{0,768},{257,1},{513,257},{769,513},{1... | collective-permute-start | bytes 1028 | tf_op jit(solution)/shard_map/ppermute | solution.py:35
  78.8 5.2 %collective-permute-done.7 = f32[1,5,17,1]{3,2,1,0:T(8,128)S(1)} collective-permute-done((f32[1,5,17,1]{3,2,1,0:T(8,128)S(1)}, f32[1,5,17,1]{3,2,1,0:T(8,128)S(1)}, u32[]{:S(2)}, u32[]{:S(2)}) %collective-permute-start.7) | collective-permute-done | bytes 372 | tf_op jit(solution)/shard_map/ppermute | solution.py:35
  84.1 2.9 %collective-permute-start.9 = (f32[1,5,1,131]{3,2,1,0:T(1,128)S(1)}, f32[1,5,1,131]{3,2,1,0:T(1,128)S(1)}, u32[]{:S(2)}, u32[]{:S(2)}) collective-permute-start(f32[1,5,1,131]{3,2,1,0:T(1,128)S(1)} %get-tuple-element.64), channel_id=1, source_target_pairs={{32,0},{64,32},{96,64},{128,96},{160,128},{192,160},{224,192},{0,2... | collective-permute-start | bytes 7868 | tf_op jit(solution)/shard_map/ppermute | solution.py:35
  87.3 1.0 collective-permute-done.8
  88.5 1.9 collective-permute-start.10
  90.5 5.1 %collective-permute-start.11 = (f32[1,1,19,131]{3,2,1,0:T(8,128)S(1)}, f32[1,1,19,131]{3,2,1,0:T(8,128)S(1)}, u32[]{:S(2)}, u32[]{:S(2)}) collective-permute-start(f32[1,1,19,131]{3,2,1,0:T(8,128)S(1)} %get-tuple-element.164), channel_id=1, source_target_pairs={{1,0},{2,1},{3,2},{4,3},{5,4},{6,5},{7,6},{8,7},{9,8},{10,9},{11,1... | collective-permute-start | bytes 29876 | tf_op jit(solution)/shard_map/ppermute | solution.py:35
  95.7 1.4 collective-permute-done.11
  97.2 0.6 copy-done.10
  98.8 0.8 slice.1459
  99.6 0.8 slice.1457
  104.1 0.6 slice-done
  104.9 1.9 collective-permute-start.12
  106.9 3.9 %collective-permute-start.13 = (f32[2,3,9,1]{3,2,1,0:T(8,128)S(1)}, f32[2,3,9,1]{3,2,1,0:T(8,128)S(1)}, u32[]{:S(2)}, u32[]{:S(2)}) collective-permute-start(f32[2,3,9,1]{3,2,1,0:T(8,128)S(1)} %get-tuple-element.296), channel_id=1, source_target_pairs={{256,0},{512,256},{768,512},{0,768},{257,1},{513,257},{769,513},{1... | collective-permute-start | bytes 656 | tf_op jit(solution)/shard_map/ppermute | solution.py:35
  110.9 3.1 %collective-permute-done.13 = f32[2,3,9,1]{3,2,1,0:T(8,128)S(1)} collective-permute-done((f32[2,3,9,1]{3,2,1,0:T(8,128)S(1)}, f32[2,3,9,1]{3,2,1,0:T(8,128)S(1)}, u32[]{:S(2)}, u32[]{:S(2)}) %collective-permute-start.13) | collective-permute-done | bytes 248 | tf_op jit(solution)/shard_map/ppermute | solution.py:35
  114.2 2.9 %collective-permute-start.15 = (f32[2,3,1,67]{3,2,1,0:T(1,128)S(1)}, f32[2,3,1,67]{3,2,1,0:T(1,128)S(1)}, u32[]{:S(2)}, u32[]{:S(2)}) collective-permute-start(f32[2,3,1,67]{3,2,1,0:T(1,128)S(1)} %get-tuple-element.149), channel_id=1, source_target_pairs={{32,0},{64,32},{96,64},{128,96},{160,128},{192,160},{224,192},{0,2... | collective-permute-start | bytes 4832 | tf_op jit(solution)/shard_map/ppermute | solution.py:35
  117.1 1.3 collective-permute-done.14
  118.6 1.9 collective-permute-start.16
  120.5 5.4 %collective-permute-start.17 = (f32[2,1,11,67]{3,2,1,0:T(8,128)S(1)}, f32[2,1,11,67]{3,2,1,0:T(8,128)S(1)}, u32[]{:S(2)}, u32[]{:S(2)}) collective-permute-start(f32[2,1,11,67]{3,2,1,0:T(8,128)S(1)} %get-tuple-element.294), channel_id=1, source_target_pairs={{1,0},{2,1},{3,2},{4,3},{5,4},{6,5},{7,6},{8,7},{9,8},{10,9},{11,1... | collective-permute-start | bytes 17696 | tf_op jit(solution)/shard_map/ppermute | solution.py:35
  125.9 1.4 collective-permute-done.17
  127.5 0.6 copy-done.4
  131.0 1.9 collective-permute-start.18
  133.0 3.9 %collective-permute-start.19 = (f32[1,3,9,1]{3,2,1,0:T(8,128)S(1)}, f32[1,3,9,1]{3,2,1,0:T(8,128)S(1)}, u32[]{:S(2)}, u32[]{:S(2)}) collective-permute-start(f32[1,3,9,1]{3,2,1,0:T(8,128)S(1)} %get-tuple-element.344), channel_id=1, source_target_pairs={{256,0},{512,256},{768,512},{0,768},{257,1},{513,257},{769,513},{1... | collective-permute-start | bytes 332 | tf_op jit(solution)/shard_map/ppermute | solution.py:35
  136.9 3.0 %collective-permute-done.19 = f32[1,3,9,1]{3,2,1,0:T(8,128)S(1)} collective-permute-done((f32[1,3,9,1]{3,2,1,0:T(8,128)S(1)}, f32[1,3,9,1]{3,2,1,0:T(8,128)S(1)}, u32[]{:S(2)}, u32[]{:S(2)}) %collective-permute-start.19) | collective-permute-done | bytes 140 | tf_op jit(solution)/shard_map/ppermute | solution.py:35
  140.0 3.0 %collective-permute-start.21 = (f32[1,3,1,67]{3,2,1,0:T(1,128)S(1)}, f32[1,3,1,67]{3,2,1,0:T(1,128)S(1)}, u32[]{:S(2)}, u32[]{:S(2)}) collective-permute-start(f32[1,3,1,67]{3,2,1,0:T(1,128)S(1)} %get-tuple-element.174), channel_id=1, source_target_pairs={{32,0},{64,32},{96,64},{128,96},{160,128},{192,160},{224,192},{0,2... | collective-permute-start | bytes 2420 | tf_op jit(solution)/shard_map/ppermute | solution.py:35
  142.9 1.3 collective-permute-done.20
  144.3 1.9 collective-permute-start.22
  146.3 5.4 %collective-permute-start.23 = (f32[1,1,11,67]{3,2,1,0:T(8,128)S(1)}, f32[1,1,11,67]{3,2,1,0:T(8,128)S(1)}, u32[]{:S(2)}, u32[]{:S(2)}) collective-permute-start(f32[1,1,11,67]{3,2,1,0:T(8,128)S(1)} %get-tuple-element.342), channel_id=1, source_target_pairs={{1,0},{2,1},{3,2},{4,3},{5,4},{6,5},{7,6},{8,7},{9,8},{10,9},{11,1... | collective-permute-start | bytes 8852 | tf_op jit(solution)/shard_map/ppermute | solution.py:35
  151.7 1.3 collective-permute-done.23
  155.5 2.1 %collective-permute-start.24 = (f32[1,3,9,1]{3,2,1,0:T(8,128)S(1)}, f32[1,3,9,1]{3,2,1,0:T(8,128)S(1)}, u32[]{:S(2)}, u32[]{:S(2)}) collective-permute-start(f32[1,3,9,1]{3,2,1,0:T(8,128)S(1)} %get-tuple-element.337), channel_id=1, source_target_pairs={{0,256},{256,512},{512,768},{768,0},{1,257},{257,513},{513,769},{7... | collective-permute-start | bytes 332 | tf_op jit(solution)/shard_map/ppermute | solution.py:33
  157.6 3.7 %collective-permute-start.25 = (f32[1,3,9,1]{3,2,1,0:T(8,128)S(1)}, f32[1,3,9,1]{3,2,1,0:T(8,128)S(1)}, u32[]{:S(2)}, u32[]{:S(2)}) collective-permute-start(f32[1,3,9,1]{3,2,1,0:T(8,128)S(1)} %get-tuple-element.338), channel_id=1, source_target_pairs={{256,0},{512,256},{768,512},{0,768},{257,1},{513,257},{769,513},{1... | collective-permute-start | bytes 332 | tf_op jit(solution)/shard_map/ppermute | solution.py:35
  161.4 3.2 %collective-permute-done.25 = f32[1,3,9,1]{3,2,1,0:T(8,128)S(1)} collective-permute-done((f32[1,3,9,1]{3,2,1,0:T(8,128)S(1)}, f32[1,3,9,1]{3,2,1,0:T(8,128)S(1)}, u32[]{:S(2)}, u32[]{:S(2)}) %collective-permute-start.25) | collective-permute-done | bytes 140 | tf_op jit(solution)/shard_map/ppermute | solution.py:35
  164.6 3.0 %collective-permute-start.27 = (f32[1,3,1,67]{3,2,1,0:T(1,128)S(1)}, f32[1,3,1,67]{3,2,1,0:T(1,128)S(1)}, u32[]{:S(2)}, u32[]{:S(2)}) collective-permute-start(f32[1,3,1,67]{3,2,1,0:T(1,128)S(1)} %get-tuple-element.172), channel_id=1, source_target_pairs={{32,0},{64,32},{96,64},{128,96},{160,128},{192,160},{224,192},{0,2... | collective-permute-start | bytes 2420 | tf_op jit(solution)/shard_map/ppermute | solution.py:35
  167.6 1.3 collective-permute-done.26
  169.0 1.9 collective-permute-start.28
  170.9 5.4 %collective-permute-start.29 = (f32[1,1,11,67]{3,2,1,0:T(8,128)S(1)}, f32[1,1,11,67]{3,2,1,0:T(8,128)S(1)}, u32[]{:S(2)}, u32[]{:S(2)}) collective-permute-start(f32[1,1,11,67]{3,2,1,0:T(8,128)S(1)} %get-tuple-element.336), channel_id=1, source_target_pairs={{1,0},{2,1},{3,2},{4,3},{5,4},{6,5},{7,6},{8,7},{9,8},{10,9},{11,1... | collective-permute-start | bytes 8852 | tf_op jit(solution)/shard_map/ppermute | solution.py:35
  176.3 1.3 collective-permute-done.29
  180.1 2.7 %collective-permute-start.30 = (f32[1,3,9,1]{3,2,1,0:T(8,128)S(1)}, f32[1,3,9,1]{3,2,1,0:T(8,128)S(1)}, u32[]{:S(2)}, u32[]{:S(2)}) collective-permute-start(f32[1,3,9,1]{3,2,1,0:T(8,128)S(1)} %get-tuple-element.331), channel_id=1, source_target_pairs={{0,256},{256,512},{512,768},{768,0},{1,257},{257,513},{513,769},{7... | collective-permute-start | bytes 332 | tf_op jit(solution)/shard_map/ppermute | solution.py:33
  182.8 3.1 %collective-permute-start.31 = (f32[1,3,9,1]{3,2,1,0:T(8,128)S(1)}, f32[1,3,9,1]{3,2,1,0:T(8,128)S(1)}, u32[]{:S(2)}, u32[]{:S(2)}) collective-permute-start(f32[1,3,9,1]{3,2,1,0:T(8,128)S(1)} %get-tuple-element.332), channel_id=1, source_target_pairs={{256,0},{512,256},{768,512},{0,768},{257,1},{513,257},{769,513},{1... | collective-permute-start | bytes 332 | tf_op jit(solution)/shard_map/ppermute | solution.py:35
  186.0 3.8 %collective-permute-done.31 = f32[1,3,9,1]{3,2,1,0:T(8,128)S(1)} collective-permute-done((f32[1,3,9,1]{3,2,1,0:T(8,128)S(1)}, f32[1,3,9,1]{3,2,1,0:T(8,128)S(1)}, u32[]{:S(2)}, u32[]{:S(2)}) %collective-permute-start.31) | collective-permute-done | bytes 140 | tf_op jit(solution)/shard_map/ppermute | solution.py:35
  189.9 3.0 %collective-permute-start.33 = (f32[1,3,1,67]{3,2,1,0:T(1,128)S(1)}, f32[1,3,1,67]{3,2,1,0:T(1,128)S(1)}, u32[]{:S(2)}, u32[]{:S(2)}) collective-permute-start(f32[1,3,1,67]{3,2,1,0:T(1,128)S(1)} %get-tuple-element.170), channel_id=1, source_target_pairs={{32,0},{64,32},{96,64},{128,96},{160,128},{192,160},{224,192},{0,2... | collective-permute-start | bytes 2420 | tf_op jit(solution)/shard_map/ppermute | solution.py:35
  192.8 1.3 collective-permute-done.32
  194.2 1.9 collective-permute-start.34
  196.1 5.4 %collective-permute-start.35 = (f32[1,1,11,67]{3,2,1,0:T(8,128)S(1)}, f32[1,1,11,67]{3,2,1,0:T(8,128)S(1)}, u32[]{:S(2)}, u32[]{:S(2)}) collective-permute-start(f32[1,1,11,67]{3,2,1,0:T(8,128)S(1)} %get-tuple-element.330), channel_id=1, source_target_pairs={{1,0},{2,1},{3,2},{4,3},{5,4},{6,5},{7,6},{8,7},{9,8},{10,9},{11,1... | collective-permute-start | bytes 8852 | tf_op jit(solution)/shard_map/ppermute | solution.py:35
  201.6 1.3 collective-permute-done.35
  205.3 0.7 slice_add_fusion.4
  (432 shorter events, 28.8 us)
Async XLA Ops:
  0.0 0.8 copy-start.8
  0.0 0.8 copy-start.2
  0.0 0.8 copy-start.7
  1.6 0.7 copy-start.12
  2.2 0.7 copy-start.11
  7.8 0.8 copy-start.1
  8.8 18.3 %collective-permute-start.1 = (f32[3,5,17,3]{3,2,1,0:T(8,128)S(1)}, f32[3,5,17,3]{3,2,1,0:T(8,128)S(1)}, u32[]{:S(2)}, u32[]{:S(2)}) collective-permute-start(f32[3,5,17,3]{3,2,1,0:T(8,128)S(1)} %get-tuple-element.58), channel_id=1, source_target_pairs={{256,0},{512,256},{768,512},{0,768},{257,1},{513,257},{769,513},{1... | collective-permute-start | bytes 9188 | tf_op jit(solution)/shard_map/ppermute | solution.py:246
  11.5 17.1 %collective-permute-start = (f32[3,5,17,3]{3,2,1,0:T(8,128)S(1)}, f32[3,5,17,3]{3,2,1,0:T(8,128)S(1)}, u32[]{:S(2)}, u32[]{:S(2)}) collective-permute-start(f32[3,5,17,3]{3,2,1,0:T(8,128)S(1)} %get-tuple-element.59), channel_id=1, source_target_pairs={{0,256},{256,512},{512,768},{768,0},{1,257},{257,513},{513,769},{7... | collective-permute-start | bytes 9188 | tf_op jit(solution)/shard_map/ppermute | solution.py:245
  25.7 0.7 copy-start.5
  25.7 0.7 copy-start.6
  29.0 1.9 collective-permute-start.3
  29.1 4.9 %collective-permute-start.2 = (f32[3,5,3,133]{3,2,1,0:T(4,128)S(1)}, f32[3,5,3,133]{3,2,1,0:T(4,128)S(1)}, u32[]{:S(2)}, u32[]{:S(2)}) collective-permute-start(f32[3,5,3,133]{3,2,1,0:T(4,128)S(1)} %get-tuple-element.55), channel_id=1, source_target_pairs={{0,32},{32,64},{64,96},{96,128},{128,160},{160,192},{192,224},{224... | collective-permute-start | bytes 71828 | tf_op jit(solution)/shard_map/ppermute | solution.py:245
  34.4 14.6 %collective-permute-start.4 = (f32[3,3,21,133]{3,2,1,0:T(8,128)S(1)}, f32[3,3,21,133]{3,2,1,0:T(8,128)S(1)}, u32[]{:S(2)}, u32[]{:S(2)}) collective-permute-start(f32[3,3,21,133]{3,2,1,0:T(8,128)S(1)} %slice.1762), channel_id=1, source_target_pairs={{0,1},{1,2},{2,3},{3,4},{4,5},{5,6},{6,7},{7,8},{8,9},{9,10},{10,1... | collective-permute-start | bytes 301652 | tf_op jit(solution)/shard_map/ppermute | solution.py:245
  49.1 7.8 %collective-permute-start.5 = (f32[3,3,21,133]{3,2,1,0:T(8,128)S(1)}, f32[3,3,21,133]{3,2,1,0:T(8,128)S(1)}, u32[]{:S(2)}, u32[]{:S(2)}) collective-permute-start(f32[3,3,21,133]{3,2,1,0:T(8,128)S(1)} %get-tuple-element.51), channel_id=1, source_target_pairs={{1,0},{2,1},{3,2},{4,3},{5,4},{6,5},{7,6},{8,7},{9,8},{10,9},{11,1... | collective-permute-start | bytes 301652 | tf_op jit(solution)/shard_map/ppermute | solution.py:246
  71.0 7.8 %collective-permute-start.6 = (f32[1,5,17,1]{3,2,1,0:T(8,128)S(1)}, f32[1,5,17,1]{3,2,1,0:T(8,128)S(1)}, u32[]{:S(2)}, u32[]{:S(2)}) collective-permute-start(f32[1,5,17,1]{3,2,1,0:T(8,128)S(1)} %get-tuple-element.165), channel_id=1, source_target_pairs={{0,256},{256,512},{512,768},{768,0},{1,257},{257,513},{513,769},{7... | collective-permute-start | bytes 1028 | tf_op jit(solution)/shard_map/ppermute | solution.py:33
  76.7 7.3 %collective-permute-start.7 = (f32[1,5,17,1]{3,2,1,0:T(8,128)S(1)}, f32[1,5,17,1]{3,2,1,0:T(8,128)S(1)}, u32[]{:S(2)}, u32[]{:S(2)}) collective-permute-start(f32[1,5,17,1]{3,2,1,0:T(8,128)S(1)} %get-tuple-element.166), channel_id=1, source_target_pairs={{256,0},{512,256},{768,512},{0,768},{257,1},{513,257},{769,513},{1... | collective-permute-start | bytes 1028 | tf_op jit(solution)/shard_map/ppermute | solution.py:35
  84.1 4.3 %collective-permute-start.8 = (f32[1,5,1,131]{3,2,1,0:T(1,128)S(1)}, f32[1,5,1,131]{3,2,1,0:T(1,128)S(1)}, u32[]{:S(2)}, u32[]{:S(2)}) collective-permute-start(f32[1,5,1,131]{3,2,1,0:T(1,128)S(1)} %get-tuple-element.63), channel_id=1, source_target_pairs={{0,32},{32,64},{64,96},{96,128},{128,160},{160,192},{192,224},{224... | collective-permute-start | bytes 7868 | tf_op jit(solution)/shard_map/ppermute | solution.py:33
  84.1 4.3 %collective-permute-start.9 = (f32[1,5,1,131]{3,2,1,0:T(1,128)S(1)}, f32[1,5,1,131]{3,2,1,0:T(1,128)S(1)}, u32[]{:S(2)}, u32[]{:S(2)}) collective-permute-start(f32[1,5,1,131]{3,2,1,0:T(1,128)S(1)} %get-tuple-element.64), channel_id=1, source_target_pairs={{32,0},{64,32},{96,64},{128,96},{160,128},{192,160},{224,192},{0,2... | collective-permute-start | bytes 7868 | tf_op jit(solution)/shard_map/ppermute | solution.py:35
  88.5 7.2 %collective-permute-start.10 = (f32[1,1,19,131]{3,2,1,0:T(8,128)S(1)}, f32[1,1,19,131]{3,2,1,0:T(8,128)S(1)}, u32[]{:S(2)}, u32[]{:S(2)}) collective-permute-start(f32[1,1,19,131]{3,2,1,0:T(8,128)S(1)} %get-tuple-element.163), channel_id=1, source_target_pairs={{0,1},{1,2},{2,3},{3,4},{4,5},{5,6},{6,7},{7,8},{8,9},{9,10},{10,1... | collective-permute-start | bytes 29876 | tf_op jit(solution)/shard_map/ppermute | solution.py:33
  90.5 6.6 %collective-permute-start.11 = (f32[1,1,19,131]{3,2,1,0:T(8,128)S(1)}, f32[1,1,19,131]{3,2,1,0:T(8,128)S(1)}, u32[]{:S(2)}, u32[]{:S(2)}) collective-permute-start(f32[1,1,19,131]{3,2,1,0:T(8,128)S(1)} %get-tuple-element.164), channel_id=1, source_target_pairs={{1,0},{2,1},{3,2},{4,3},{5,4},{6,5},{7,6},{8,7},{9,8},{10,9},{11,1... | collective-permute-start | bytes 29876 | tf_op jit(solution)/shard_map/ppermute | solution.py:35
  97.2 0.7 copy-start.10
  98.0 0.7 copy-start.9
  102.8 0.7 copy-start
  104.0 0.7 slice-start
  104.9 6.0 %collective-permute-start.12 = (f32[2,3,9,1]{3,2,1,0:T(8,128)S(1)}, f32[2,3,9,1]{3,2,1,0:T(8,128)S(1)}, u32[]{:S(2)}, u32[]{:S(2)}) collective-permute-start(f32[2,3,9,1]{3,2,1,0:T(8,128)S(1)} %get-tuple-element.295), channel_id=1, source_target_pairs={{0,256},{256,512},{512,768},{768,0},{1,257},{257,513},{513,769},{7... | collective-permute-start | bytes 656 | tf_op jit(solution)/shard_map/ppermute | solution.py:33
  106.9 7.2 %collective-permute-start.13 = (f32[2,3,9,1]{3,2,1,0:T(8,128)S(1)}, f32[2,3,9,1]{3,2,1,0:T(8,128)S(1)}, u32[]{:S(2)}, u32[]{:S(2)}) collective-permute-start(f32[2,3,9,1]{3,2,1,0:T(8,128)S(1)} %get-tuple-element.296), channel_id=1, source_target_pairs={{256,0},{512,256},{768,512},{0,768},{257,1},{513,257},{769,513},{1... | collective-permute-start | bytes 656 | tf_op jit(solution)/shard_map/ppermute | solution.py:35
  114.2 4.2 %collective-permute-start.14 = (f32[2,3,1,67]{3,2,1,0:T(1,128)S(1)}, f32[2,3,1,67]{3,2,1,0:T(1,128)S(1)}, u32[]{:S(2)}, u32[]{:S(2)}) collective-permute-start(f32[2,3,1,67]{3,2,1,0:T(1,128)S(1)} %get-tuple-element.148), channel_id=1, source_target_pairs={{0,32},{32,64},{64,96},{96,128},{128,160},{160,192},{192,224},{224... | collective-permute-start | bytes 4832 | tf_op jit(solution)/shard_map/ppermute | solution.py:33
  114.2 4.3 %collective-permute-start.15 = (f32[2,3,1,67]{3,2,1,0:T(1,128)S(1)}, f32[2,3,1,67]{3,2,1,0:T(1,128)S(1)}, u32[]{:S(2)}, u32[]{:S(2)}) collective-permute-start(f32[2,3,1,67]{3,2,1,0:T(1,128)S(1)} %get-tuple-element.149), channel_id=1, source_target_pairs={{32,0},{64,32},{96,64},{128,96},{160,128},{192,160},{224,192},{0,2... | collective-permute-start | bytes 4832 | tf_op jit(solution)/shard_map/ppermute | solution.py:35
  118.6 7.4 %collective-permute-start.16 = (f32[2,1,11,67]{3,2,1,0:T(8,128)S(1)}, f32[2,1,11,67]{3,2,1,0:T(8,128)S(1)}, u32[]{:S(2)}, u32[]{:S(2)}) collective-permute-start(f32[2,1,11,67]{3,2,1,0:T(8,128)S(1)} %get-tuple-element.293), channel_id=1, source_target_pairs={{0,1},{1,2},{2,3},{3,4},{4,5},{5,6},{6,7},{7,8},{8,9},{9,10},{10,1... | collective-permute-start | bytes 17696 | tf_op jit(solution)/shard_map/ppermute | solution.py:33
  120.5 6.9 %collective-permute-start.17 = (f32[2,1,11,67]{3,2,1,0:T(8,128)S(1)}, f32[2,1,11,67]{3,2,1,0:T(8,128)S(1)}, u32[]{:S(2)}, u32[]{:S(2)}) collective-permute-start(f32[2,1,11,67]{3,2,1,0:T(8,128)S(1)} %get-tuple-element.294), channel_id=1, source_target_pairs={{1,0},{2,1},{3,2},{4,3},{5,4},{6,5},{7,6},{8,7},{9,8},{10,9},{11,1... | collective-permute-start | bytes 17696 | tf_op jit(solution)/shard_map/ppermute | solution.py:35
  127.4 0.7 copy-start.4
  128.2 0.7 copy-start.3
  131.0 5.9 %collective-permute-start.18 = (f32[1,3,9,1]{3,2,1,0:T(8,128)S(1)}, f32[1,3,9,1]{3,2,1,0:T(8,128)S(1)}, u32[]{:S(2)}, u32[]{:S(2)}) collective-permute-start(f32[1,3,9,1]{3,2,1,0:T(8,128)S(1)} %get-tuple-element.343), channel_id=1, source_target_pairs={{0,256},{256,512},{512,768},{768,0},{1,257},{257,513},{513,769},{7... | collective-permute-start | bytes 332 | tf_op jit(solution)/shard_map/ppermute | solution.py:33
  133.0 6.9 %collective-permute-start.19 = (f32[1,3,9,1]{3,2,1,0:T(8,128)S(1)}, f32[1,3,9,1]{3,2,1,0:T(8,128)S(1)}, u32[]{:S(2)}, u32[]{:S(2)}) collective-permute-start(f32[1,3,9,1]{3,2,1,0:T(8,128)S(1)} %get-tuple-element.344), channel_id=1, source_target_pairs={{256,0},{512,256},{768,512},{0,768},{257,1},{513,257},{769,513},{1... | collective-permute-start | bytes 332 | tf_op jit(solution)/shard_map/ppermute | solution.py:35
  140.0 4.2 %collective-permute-start.20 = (f32[1,3,1,67]{3,2,1,0:T(1,128)S(1)}, f32[1,3,1,67]{3,2,1,0:T(1,128)S(1)}, u32[]{:S(2)}, u32[]{:S(2)}) collective-permute-start(f32[1,3,1,67]{3,2,1,0:T(1,128)S(1)} %get-tuple-element.173), channel_id=1, source_target_pairs={{0,32},{32,64},{64,96},{96,128},{128,160},{160,192},{192,224},{224... | collective-permute-start | bytes 2420 | tf_op jit(solution)/shard_map/ppermute | solution.py:33
  140.0 4.3 %collective-permute-start.21 = (f32[1,3,1,67]{3,2,1,0:T(1,128)S(1)}, f32[1,3,1,67]{3,2,1,0:T(1,128)S(1)}, u32[]{:S(2)}, u32[]{:S(2)}) collective-permute-start(f32[1,3,1,67]{3,2,1,0:T(1,128)S(1)} %get-tuple-element.174), channel_id=1, source_target_pairs={{32,0},{64,32},{96,64},{128,96},{160,128},{192,160},{224,192},{0,2... | collective-permute-start | bytes 2420 | tf_op jit(solution)/shard_map/ppermute | solution.py:35
  144.3 7.3 %collective-permute-start.22 = (f32[1,1,11,67]{3,2,1,0:T(8,128)S(1)}, f32[1,1,11,67]{3,2,1,0:T(8,128)S(1)}, u32[]{:S(2)}, u32[]{:S(2)}) collective-permute-start(f32[1,1,11,67]{3,2,1,0:T(8,128)S(1)} %get-tuple-element.341), channel_id=1, source_target_pairs={{0,1},{1,2},{2,3},{3,4},{4,5},{5,6},{6,7},{7,8},{8,9},{9,10},{10,1... | collective-permute-start | bytes 8852 | tf_op jit(solution)/shard_map/ppermute | solution.py:33
  146.3 6.8 %collective-permute-start.23 = (f32[1,1,11,67]{3,2,1,0:T(8,128)S(1)}, f32[1,1,11,67]{3,2,1,0:T(8,128)S(1)}, u32[]{:S(2)}, u32[]{:S(2)}) collective-permute-start(f32[1,1,11,67]{3,2,1,0:T(8,128)S(1)} %get-tuple-element.342), channel_id=1, source_target_pairs={{1,0},{2,1},{3,2},{4,3},{5,4},{6,5},{7,6},{8,7},{9,8},{10,9},{11,1... | collective-permute-start | bytes 8852 | tf_op jit(solution)/shard_map/ppermute | solution.py:35
  155.5 5.9 %collective-permute-start.24 = (f32[1,3,9,1]{3,2,1,0:T(8,128)S(1)}, f32[1,3,9,1]{3,2,1,0:T(8,128)S(1)}, u32[]{:S(2)}, u32[]{:S(2)}) collective-permute-start(f32[1,3,9,1]{3,2,1,0:T(8,128)S(1)} %get-tuple-element.337), channel_id=1, source_target_pairs={{0,256},{256,512},{512,768},{768,0},{1,257},{257,513},{513,769},{7... | collective-permute-start | bytes 332 | tf_op jit(solution)/shard_map/ppermute | solution.py:33
  157.6 6.9 %collective-permute-start.25 = (f32[1,3,9,1]{3,2,1,0:T(8,128)S(1)}, f32[1,3,9,1]{3,2,1,0:T(8,128)S(1)}, u32[]{:S(2)}, u32[]{:S(2)}) collective-permute-start(f32[1,3,9,1]{3,2,1,0:T(8,128)S(1)} %get-tuple-element.338), channel_id=1, source_target_pairs={{256,0},{512,256},{768,512},{0,768},{257,1},{513,257},{769,513},{1... | collective-permute-start | bytes 332 | tf_op jit(solution)/shard_map/ppermute | solution.py:35
  164.6 4.2 %collective-permute-start.26 = (f32[1,3,1,67]{3,2,1,0:T(1,128)S(1)}, f32[1,3,1,67]{3,2,1,0:T(1,128)S(1)}, u32[]{:S(2)}, u32[]{:S(2)}) collective-permute-start(f32[1,3,1,67]{3,2,1,0:T(1,128)S(1)} %get-tuple-element.171), channel_id=1, source_target_pairs={{0,32},{32,64},{64,96},{96,128},{128,160},{160,192},{192,224},{224... | collective-permute-start | bytes 2420 | tf_op jit(solution)/shard_map/ppermute | solution.py:33
  164.6 4.3 %collective-permute-start.27 = (f32[1,3,1,67]{3,2,1,0:T(1,128)S(1)}, f32[1,3,1,67]{3,2,1,0:T(1,128)S(1)}, u32[]{:S(2)}, u32[]{:S(2)}) collective-permute-start(f32[1,3,1,67]{3,2,1,0:T(1,128)S(1)} %get-tuple-element.172), channel_id=1, source_target_pairs={{32,0},{64,32},{96,64},{128,96},{160,128},{192,160},{224,192},{0,2... | collective-permute-start | bytes 2420 | tf_op jit(solution)/shard_map/ppermute | solution.py:35
  169.0 7.3 %collective-permute-start.28 = (f32[1,1,11,67]{3,2,1,0:T(8,128)S(1)}, f32[1,1,11,67]{3,2,1,0:T(8,128)S(1)}, u32[]{:S(2)}, u32[]{:S(2)}) collective-permute-start(f32[1,1,11,67]{3,2,1,0:T(8,128)S(1)} %get-tuple-element.335), channel_id=1, source_target_pairs={{0,1},{1,2},{2,3},{3,4},{4,5},{5,6},{6,7},{7,8},{8,9},{9,10},{10,1... | collective-permute-start | bytes 8852 | tf_op jit(solution)/shard_map/ppermute | solution.py:33
  170.9 6.8 %collective-permute-start.29 = (f32[1,1,11,67]{3,2,1,0:T(8,128)S(1)}, f32[1,1,11,67]{3,2,1,0:T(8,128)S(1)}, u32[]{:S(2)}, u32[]{:S(2)}) collective-permute-start(f32[1,1,11,67]{3,2,1,0:T(8,128)S(1)} %get-tuple-element.336), channel_id=1, source_target_pairs={{1,0},{2,1},{3,2},{4,3},{5,4},{6,5},{7,6},{8,7},{9,8},{10,9},{11,1... | collective-permute-start | bytes 8852 | tf_op jit(solution)/shard_map/ppermute | solution.py:35
  180.1 5.9 %collective-permute-start.30 = (f32[1,3,9,1]{3,2,1,0:T(8,128)S(1)}, f32[1,3,9,1]{3,2,1,0:T(8,128)S(1)}, u32[]{:S(2)}, u32[]{:S(2)}) collective-permute-start(f32[1,3,9,1]{3,2,1,0:T(8,128)S(1)} %get-tuple-element.331), channel_id=1, source_target_pairs={{0,256},{256,512},{512,768},{768,0},{1,257},{257,513},{513,769},{7... | collective-permute-start | bytes 332 | tf_op jit(solution)/shard_map/ppermute | solution.py:33
  182.8 6.9 %collective-permute-start.31 = (f32[1,3,9,1]{3,2,1,0:T(8,128)S(1)}, f32[1,3,9,1]{3,2,1,0:T(8,128)S(1)}, u32[]{:S(2)}, u32[]{:S(2)}) collective-permute-start(f32[1,3,9,1]{3,2,1,0:T(8,128)S(1)} %get-tuple-element.332), channel_id=1, source_target_pairs={{256,0},{512,256},{768,512},{0,768},{257,1},{513,257},{769,513},{1... | collective-permute-start | bytes 332 | tf_op jit(solution)/shard_map/ppermute | solution.py:35
  189.8 4.2 %collective-permute-start.32 = (f32[1,3,1,67]{3,2,1,0:T(1,128)S(1)}, f32[1,3,1,67]{3,2,1,0:T(1,128)S(1)}, u32[]{:S(2)}, u32[]{:S(2)}) collective-permute-start(f32[1,3,1,67]{3,2,1,0:T(1,128)S(1)} %get-tuple-element.169), channel_id=1, source_target_pairs={{0,32},{32,64},{64,96},{96,128},{128,160},{160,192},{192,224},{224... | collective-permute-start | bytes 2420 | tf_op jit(solution)/shard_map/ppermute | solution.py:33
  189.9 4.3 %collective-permute-start.33 = (f32[1,3,1,67]{3,2,1,0:T(1,128)S(1)}, f32[1,3,1,67]{3,2,1,0:T(1,128)S(1)}, u32[]{:S(2)}, u32[]{:S(2)}) collective-permute-start(f32[1,3,1,67]{3,2,1,0:T(1,128)S(1)} %get-tuple-element.170), channel_id=1, source_target_pairs={{32,0},{64,32},{96,64},{128,96},{160,128},{192,160},{224,192},{0,2... | collective-permute-start | bytes 2420 | tf_op jit(solution)/shard_map/ppermute | solution.py:35
  194.2 7.3 %collective-permute-start.34 = (f32[1,1,11,67]{3,2,1,0:T(8,128)S(1)}, f32[1,1,11,67]{3,2,1,0:T(8,128)S(1)}, u32[]{:S(2)}, u32[]{:S(2)}) collective-permute-start(f32[1,1,11,67]{3,2,1,0:T(8,128)S(1)} %get-tuple-element.329), channel_id=1, source_target_pairs={{0,1},{1,2},{2,3},{3,4},{4,5},{5,6},{6,7},{7,8},{8,9},{9,10},{10,1... | collective-permute-start | bytes 8852 | tf_op jit(solution)/shard_map/ppermute | solution.py:33
  196.1 6.8 %collective-permute-start.35 = (f32[1,1,11,67]{3,2,1,0:T(8,128)S(1)}, f32[1,1,11,67]{3,2,1,0:T(8,128)S(1)}, u32[]{:S(2)}, u32[]{:S(2)}) collective-permute-start(f32[1,1,11,67]{3,2,1,0:T(8,128)S(1)} %get-tuple-element.330), channel_id=1, source_target_pairs={{1,0},{2,1},{3,2},{4,3},{5,4},{6,5},{7,6},{8,7},{9,8},{10,9},{11,1... | collective-permute-start | bytes 8852 | tf_op jit(solution)/shard_map/ppermute | solution.py:35
where the time goes:
time: 207 us; the launch traced here: 206 us
  starting transfers between devices  105 us (51%)
  waiting for transfers between devices  53.7 us (26%)
  local copies, waits for them, and re-layouts  31.7 us (15%)
  other arithmetic  12.5 us (6%)
  between operations  2.61 us (1%)
    ppermute x15, starting transfers between devices, padded(): lax.ppermute(head, axis, [((i + 1) % count, i) for i in range(count)])  58.4 us
    ppermute x15, waiting for transfers between devices, padded(): lax.ppermute(head, axis, [((i + 1) % count, i) for i in range(count)])  25.3 us
    ppermute x15, starting transfers between devices, padded(): lax.ppermute(tail, axis, [(i, (i + 1) % count) for i in range(count)])  23.9 us
    ppermute x3, waiting for transfers between devices, widened(): lax.ppermute(tail, axis, [(i, (i + 1) % count) for i in range(count)])  17 us
    ppermute x3, starting transfers between devices, widened(): lax.ppermute(tail, axis, [(i, (i + 1) % count) for i in range(count)])  16.4 us
    unnamed x31, local copies, waits for them, and re-layouts  10.3 us
    ppermute x3, starting transfers between devices, widened(): lax.ppermute(head, axis, [((i + 1) % count, i) for i in range(count)])  6.77 us
    ppermute x15, waiting for transfers between devices, padded(): lax.ppermute(tail, axis, [(i, (i + 1) % count) for i in range(count)])  6.21 us
  transfers between devices with their start and end apart: 36, of which 22 were waited for; matrix products, arithmetic and copies ran while one was open for 1% of the time, Pallas kernels for 0%

commit v1 on v0

--- a/solution.py
+++ b/solution.py
@@ -261,8 +261,9 @@
 
 def on_device(element_load, conductivity):
     load_full = pad_axis(element_load, 2, 0, 1)
-    cond_nodes = jnp.zeros(load_full.shape, conductivity.dtype)
-    cond_nodes = cond_nodes.at[:-1:2, :-1:2, :-1:2].set(conductivity)
+    cond_nodes = lax.pad(
+        conductivity, jnp.zeros((), conductivity.dtype), [(0, 2, 1), (0, 2, 1), (0, 2, 1)]
+    )
     ring = 2
     wide = widened(
         jnp.stack([load_full, diag_local(conductivity, 1.0, reaction_rate), cond_nodes], 0),

time: 207 us -> 202 us (0.976)
  local copies, waits for them, and re-layouts: 31.7 us -> 26.5 us
    unnamed x31 -> x24, local copies, waits for them, and re-layouts: 10.3 us -> 5.25 us
where the time goes in v1:
time: 202 us; the launch traced here: 201 us
  starting transfers between devices  105 us (52%)
  waiting for transfers between devices  53.7 us (27%)
  local copies, waits for them, and re-layouts  26.5 us (13%)
  other arithmetic  13 us (6%)
  between operations  2.57 us (1%)
    ppermute x15, starting transfers between devices, padded(): lax.ppermute(head, axis, [((i + 1) % count, i) for i in range(count)])  58.4 us
    ppermute x15, waiting for transfers between devices, padded(): lax.ppermute(head, axis, [((i + 1) % count, i) for i in range(count)])  25.3 us
    ppermute x15, starting transfers between devices, padded(): lax.ppermute(tail, axis, [(i, (i + 1) % count) for i in range(count)])  23.9 us
    ppermute x3, waiting for transfers between devices, widened(): lax.ppermute(tail, axis, [(i, (i + 1) % count) for i in range(count)])  17 us
    ppermute x3, starting transfers between devices, widened(): lax.ppermute(tail, axis, [(i, (i + 1) % count) for i in range(count)])  16.4 us
    ppermute x3, starting transfers between devices, widened(): lax.ppermute(head, axis, [((i + 1) % count, i) for i in range(count)])  6.77 us
    ppermute x15, waiting for transfers between devices, padded(): lax.ppermute(tail, axis, [(i, (i + 1) % count) for i in range(count)])  6.21 us
    ppermute x3, waiting for transfers between devices, widened(): lax.ppermute(head, axis, [((i + 1) % count, i) for i in range(count)])  5.29 us
  transfers between devices with their start and end apart: 36, of which 22 were waited for; matrix products, arithmetic and copies ran while one was open for 1% of the time, Pallas kernels for 0%

profile of v1, /device:TPU:24, one launch (start us, length us, event | category | flops | bytes accessed | tf_op | source)
XLA Modules:
  0.0 201.3 jit_solution(18240074026318416932)
XLA Ops:
  0.0 0.7 copy-done.8
  0.7 0.8 multiply_add_fusion.24
  2.0 0.6 copy-done.2
  3.3 0.7 copy-done.1
  4.1 2.7 %collective-permute-start.1 = (f32[3,5,17,3]{3,2,1,0:T(8,128)S(1)}, f32[3,5,17,3]{3,2,1,0:T(8,128)S(1)}, u32[]{:S(2)}, u32[]{:S(2)}) collective-permute-start(f32[3,5,17,3]{3,2,1,0:T(8,128)S(1)} %get-tuple-element.58), channel_id=1, source_target_pairs={{256,0},{512,256},{768,512},{0,768},{257,1},{513,257},{769,513},{1... | collective-permute-start | bytes 9188 | tf_op jit(solution)/shard_map/ppermute | solution.py:246
  6.8 14.0 %collective-permute-start = (f32[3,5,17,3]{3,2,1,0:T(8,128)S(1)}, f32[3,5,17,3]{3,2,1,0:T(8,128)S(1)}, u32[]{:S(2)}, u32[]{:S(2)}) collective-permute-start(f32[3,5,17,3]{3,2,1,0:T(8,128)S(1)} %get-tuple-element.59), channel_id=1, source_target_pairs={{0,256},{256,512},{512,768},{768,0},{1,257},{257,513},{513,769},{7... | collective-permute-start | bytes 9188 | tf_op jit(solution)/shard_map/ppermute | solution.py:245
  22.5 1.3 collective-permute-done
  24.9 1.3 collective-permute-done.3
  26.2 3.0 %collective-permute-done.2 = f32[3,5,3,133]{3,2,1,0:T(4,128)S(1)} collective-permute-done((f32[3,5,3,133]{3,2,1,0:T(4,128)S(1)}, f32[3,5,3,133]{3,2,1,0:T(4,128)S(1)}, u32[]{:S(2)}, u32[]{:S(2)}) %collective-permute-start.2) | collective-permute-done | bytes 23972 | tf_op jit(solution)/shard_map/ppermute | solution.py:245
  29.7 1.9 collective-permute-start.4
  31.7 12.6 %collective-permute-done.4 = f32[3,3,21,133]{3,2,1,0:T(8,128)S(1)} collective-permute-done((f32[3,3,21,133]{3,2,1,0:T(8,128)S(1)}, f32[3,3,21,133]{3,2,1,0:T(8,128)S(1)}, u32[]{:S(2)}, u32[]{:S(2)}) %collective-permute-start.4) | collective-permute-done | bytes 100580 | tf_op jit(solution)/shard_map/ppermute | solution.py:245
  44.4 4.1 %collective-permute-start.5 = (f32[3,3,21,133]{3,2,1,0:T(8,128)S(1)}, f32[3,3,21,133]{3,2,1,0:T(8,128)S(1)}, u32[]{:S(2)}, u32[]{:S(2)}) collective-permute-start(f32[3,3,21,133]{3,2,1,0:T(8,128)S(1)} %get-tuple-element.51), channel_id=1, source_target_pairs={{1,0},{2,1},{3,2},{4,3},{5,4},{6,5},{7,6},{8,7},{9,8},{10,9},{11,1... | collective-permute-start | bytes 301652 | tf_op jit(solution)/shard_map/ppermute | solution.py:246
  48.6 3.6 %collective-permute-done.5 = f32[3,3,21,133]{3,2,1,0:T(8,128)S(1)} collective-permute-done((f32[3,3,21,133]{3,2,1,0:T(8,128)S(1)}, f32[3,3,21,133]{3,2,1,0:T(8,128)S(1)}, u32[]{:S(2)}, u32[]{:S(2)}) %collective-permute-start.5) | collective-permute-done | bytes 100580 | tf_op jit(solution)/shard_map/ppermute | solution.py:246
  52.2 0.9 slice.1356
  53.2 1.8 slice.1361
  55.0 1.8 slice.1359
  62.6 0.8 slice.1404
  63.4 0.8 slice.1402
  66.4 5.6 %collective-permute-start.6 = (f32[1,5,17,1]{3,2,1,0:T(8,128)S(1)}, f32[1,5,17,1]{3,2,1,0:T(8,128)S(1)}, u32[]{:S(2)}, u32[]{:S(2)}) collective-permute-start(f32[1,5,17,1]{3,2,1,0:T(8,128)S(1)} %get-tuple-element.165), channel_id=1, source_target_pairs={{0,256},{256,512},{512,768},{768,0},{1,257},{257,513},{513,769},{7... | collective-permute-start | bytes 1028 | tf_op jit(solution)/shard_map/ppermute | solution.py:33
  72.0 2.1 %collective-permute-start.7 = (f32[1,5,17,1]{3,2,1,0:T(8,128)S(1)}, f32[1,5,17,1]{3,2,1,0:T(8,128)S(1)}, u32[]{:S(2)}, u32[]{:S(2)}) collective-permute-start(f32[1,5,17,1]{3,2,1,0:T(8,128)S(1)} %get-tuple-element.166), channel_id=1, source_target_pairs={{256,0},{512,256},{768,512},{0,768},{257,1},{513,257},{769,513},{1... | collective-permute-start | bytes 1028 | tf_op jit(solution)/shard_map/ppermute | solution.py:35
  74.1 5.2 %collective-permute-done.7 = f32[1,5,17,1]{3,2,1,0:T(8,128)S(1)} collective-permute-done((f32[1,5,17,1]{3,2,1,0:T(8,128)S(1)}, f32[1,5,17,1]{3,2,1,0:T(8,128)S(1)}, u32[]{:S(2)}, u32[]{:S(2)}) %collective-permute-start.7) | collective-permute-done | bytes 372 | tf_op jit(solution)/shard_map/ppermute | solution.py:35
  79.4 2.9 %collective-permute-start.9 = (f32[1,5,1,131]{3,2,1,0:T(1,128)S(1)}, f32[1,5,1,131]{3,2,1,0:T(1,128)S(1)}, u32[]{:S(2)}, u32[]{:S(2)}) collective-permute-start(f32[1,5,1,131]{3,2,1,0:T(1,128)S(1)} %get-tuple-element.64), channel_id=1, source_target_pairs={{32,0},{64,32},{96,64},{128,96},{160,128},{192,160},{224,192},{0,2... | collective-permute-start | bytes 7868 | tf_op jit(solution)/shard_map/ppermute | solution.py:35
  82.6 1.0 collective-permute-done.8
  83.8 1.9 collective-permute-start.10
  85.8 5.1 %collective-permute-start.11 = (f32[1,1,19,131]{3,2,1,0:T(8,128)S(1)}, f32[1,1,19,131]{3,2,1,0:T(8,128)S(1)}, u32[]{:S(2)}, u32[]{:S(2)}) collective-permute-start(f32[1,1,19,131]{3,2,1,0:T(8,128)S(1)} %get-tuple-element.164), channel_id=1, source_target_pairs={{1,0},{2,1},{3,2},{4,3},{5,4},{6,5},{7,6},{8,7},{9,8},{10,9},{11,1... | collective-permute-start | bytes 29876 | tf_op jit(solution)/shard_map/ppermute | solution.py:35
  91.0 1.4 collective-permute-done.11
  92.6 0.6 copy-done.10
  94.1 0.8 slice.1459
  94.9 0.8 slice.1457
  99.4 0.6 slice-done
  100.2 1.9 collective-permute-start.12
  102.2 3.9 %collective-permute-start.13 = (f32[2,3,9,1]{3,2,1,0:T(8,128)S(1)}, f32[2,3,9,1]{3,2,1,0:T(8,128)S(1)}, u32[]{:S(2)}, u32[]{:S(2)}) collective-permute-start(f32[2,3,9,1]{3,2,1,0:T(8,128)S(1)} %get-tuple-element.296), channel_id=1, source_target_pairs={{256,0},{512,256},{768,512},{0,768},{257,1},{513,257},{769,513},{1... | collective-permute-start | bytes 656 | tf_op jit(solution)/shard_map/ppermute | solution.py:35
  106.2 3.1 %collective-permute-done.13 = f32[2,3,9,1]{3,2,1,0:T(8,128)S(1)} collective-permute-done((f32[2,3,9,1]{3,2,1,0:T(8,128)S(1)}, f32[2,3,9,1]{3,2,1,0:T(8,128)S(1)}, u32[]{:S(2)}, u32[]{:S(2)}) %collective-permute-start.13) | collective-permute-done | bytes 248 | tf_op jit(solution)/shard_map/ppermute | solution.py:35
  109.5 2.9 %collective-permute-start.15 = (f32[2,3,1,67]{3,2,1,0:T(1,128)S(1)}, f32[2,3,1,67]{3,2,1,0:T(1,128)S(1)}, u32[]{:S(2)}, u32[]{:S(2)}) collective-permute-start(f32[2,3,1,67]{3,2,1,0:T(1,128)S(1)} %get-tuple-element.149), channel_id=1, source_target_pairs={{32,0},{64,32},{96,64},{128,96},{160,128},{192,160},{224,192},{0,2... | collective-permute-start | bytes 4832 | tf_op jit(solution)/shard_map/ppermute | solution.py:35
  112.4 1.3 collective-permute-done.14
  113.9 1.9 collective-permute-start.16
  115.8 5.4 %collective-permute-start.17 = (f32[2,1,11,67]{3,2,1,0:T(8,128)S(1)}, f32[2,1,11,67]{3,2,1,0:T(8,128)S(1)}, u32[]{:S(2)}, u32[]{:S(2)}) collective-permute-start(f32[2,1,11,67]{3,2,1,0:T(8,128)S(1)} %get-tuple-element.294), channel_id=1, source_target_pairs={{1,0},{2,1},{3,2},{4,3},{5,4},{6,5},{7,6},{8,7},{9,8},{10,9},{11,1... | collective-permute-start | bytes 17696 | tf_op jit(solution)/shard_map/ppermute | solution.py:35
  121.2 1.4 collective-permute-done.17
  122.8 0.6 copy-done.4
  126.3 1.9 collective-permute-start.18
  128.3 3.9 %collective-permute-start.19 = (f32[1,3,9,1]{3,2,1,0:T(8,128)S(1)}, f32[1,3,9,1]{3,2,1,0:T(8,128)S(1)}, u32[]{:S(2)}, u32[]{:S(2)}) collective-permute-start(f32[1,3,9,1]{3,2,1,0:T(8,128)S(1)} %get-tuple-element.344), channel_id=1, source_target_pairs={{256,0},{512,256},{768,512},{0,768},{257,1},{513,257},{769,513},{1... | collective-permute-start | bytes 332 | tf_op jit(solution)/shard_map/ppermute | solution.py:35
  132.2 3.0 %collective-permute-done.19 = f32[1,3,9,1]{3,2,1,0:T(8,128)S(1)} collective-permute-done((f32[1,3,9,1]{3,2,1,0:T(8,128)S(1)}, f32[1,3,9,1]{3,2,1,0:T(8,128)S(1)}, u32[]{:S(2)}, u32[]{:S(2)}) %collective-permute-start.19) | collective-permute-done | bytes 140 | tf_op jit(solution)/shard_map/ppermute | solution.py:35
  135.3 3.0 %collective-permute-start.21 = (f32[1,3,1,67]{3,2,1,0:T(1,128)S(1)}, f32[1,3,1,67]{3,2,1,0:T(1,128)S(1)}, u32[]{:S(2)}, u32[]{:S(2)}) collective-permute-start(f32[1,3,1,67]{3,2,1,0:T(1,128)S(1)} %get-tuple-element.174), channel_id=1, source_target_pairs={{32,0},{64,32},{96,64},{128,96},{160,128},{192,160},{224,192},{0,2... | collective-permute-start | bytes 2420 | tf_op jit(solution)/shard_map/ppermute | solution.py:35
  138.2 1.3 collective-permute-done.20
  139.6 1.9 collective-permute-start.22
  141.6 5.4 %collective-permute-start.23 = (f32[1,1,11,67]{3,2,1,0:T(8,128)S(1)}, f32[1,1,11,67]{3,2,1,0:T(8,128)S(1)}, u32[]{:S(2)}, u32[]{:S(2)}) collective-permute-start(f32[1,1,11,67]{3,2,1,0:T(8,128)S(1)} %get-tuple-element.342), channel_id=1, source_target_pairs={{1,0},{2,1},{3,2},{4,3},{5,4},{6,5},{7,6},{8,7},{9,8},{10,9},{11,1... | collective-permute-start | bytes 8852 | tf_op jit(solution)/shard_map/ppermute | solution.py:35
  147.0 1.3 collective-permute-done.23
  150.8 2.1 %collective-permute-start.24 = (f32[1,3,9,1]{3,2,1,0:T(8,128)S(1)}, f32[1,3,9,1]{3,2,1,0:T(8,128)S(1)}, u32[]{:S(2)}, u32[]{:S(2)}) collective-permute-start(f32[1,3,9,1]{3,2,1,0:T(8,128)S(1)} %get-tuple-element.337), channel_id=1, source_target_pairs={{0,256},{256,512},{512,768},{768,0},{1,257},{257,513},{513,769},{7... | collective-permute-start | bytes 332 | tf_op jit(solution)/shard_map/ppermute | solution.py:33
  152.9 3.7 %collective-permute-start.25 = (f32[1,3,9,1]{3,2,1,0:T(8,128)S(1)}, f32[1,3,9,1]{3,2,1,0:T(8,128)S(1)}, u32[]{:S(2)}, u32[]{:S(2)}) collective-permute-start(f32[1,3,9,1]{3,2,1,0:T(8,128)S(1)} %get-tuple-element.338), channel_id=1, source_target_pairs={{256,0},{512,256},{768,512},{0,768},{257,1},{513,257},{769,513},{1... | collective-permute-start | bytes 332 | tf_op jit(solution)/shard_map/ppermute | solution.py:35
  156.7 3.2 %collective-permute-done.25 = f32[1,3,9,1]{3,2,1,0:T(8,128)S(1)} collective-permute-done((f32[1,3,9,1]{3,2,1,0:T(8,128)S(1)}, f32[1,3,9,1]{3,2,1,0:T(8,128)S(1)}, u32[]{:S(2)}, u32[]{:S(2)}) %collective-permute-start.25) | collective-permute-done | bytes 140 | tf_op jit(solution)/shard_map/ppermute | solution.py:35
  159.9 3.0 %collective-permute-start.27 = (f32[1,3,1,67]{3,2,1,0:T(1,128)S(1)}, f32[1,3,1,67]{3,2,1,0:T(1,128)S(1)}, u32[]{:S(2)}, u32[]{:S(2)}) collective-permute-start(f32[1,3,1,67]{3,2,1,0:T(1,128)S(1)} %get-tuple-element.172), channel_id=1, source_target_pairs={{32,0},{64,32},{96,64},{128,96},{160,128},{192,160},{224,192},{0,2... | collective-permute-start | bytes 2420 | tf_op jit(solution)/shard_map/ppermute | solution.py:35
  162.9 1.3 collective-permute-done.26
  164.3 1.9 collective-permute-start.28
  166.2 5.4 %collective-permute-start.29 = (f32[1,1,11,67]{3,2,1,0:T(8,128)S(1)}, f32[1,1,11,67]{3,2,1,0:T(8,128)S(1)}, u32[]{:S(2)}, u32[]{:S(2)}) collective-permute-start(f32[1,1,11,67]{3,2,1,0:T(8,128)S(1)} %get-tuple-element.336), channel_id=1, source_target_pairs={{1,0},{2,1},{3,2},{4,3},{5,4},{6,5},{7,6},{8,7},{9,8},{10,9},{11,1... | collective-permute-start | bytes 8852 | tf_op jit(solution)/shard_map/ppermute | solution.py:35
  171.6 1.3 collective-permute-done.29
  175.4 2.7 %collective-permute-start.30 = (f32[1,3,9,1]{3,2,1,0:T(8,128)S(1)}, f32[1,3,9,1]{3,2,1,0:T(8,128)S(1)}, u32[]{:S(2)}, u32[]{:S(2)}) collective-permute-start(f32[1,3,9,1]{3,2,1,0:T(8,128)S(1)} %get-tuple-element.331), channel_id=1, source_target_pairs={{0,256},{256,512},{512,768},{768,0},{1,257},{257,513},{513,769},{7... | collective-permute-start | bytes 332 | tf_op jit(solution)/shard_map/ppermute | solution.py:33
  178.1 3.1 %collective-permute-start.31 = (f32[1,3,9,1]{3,2,1,0:T(8,128)S(1)}, f32[1,3,9,1]{3,2,1,0:T(8,128)S(1)}, u32[]{:S(2)}, u32[]{:S(2)}) collective-permute-start(f32[1,3,9,1]{3,2,1,0:T(8,128)S(1)} %get-tuple-element.332), channel_id=1, source_target_pairs={{256,0},{512,256},{768,512},{0,768},{257,1},{513,257},{769,513},{1... | collective-permute-start | bytes 332 | tf_op jit(solution)/shard_map/ppermute | solution.py:35
  181.3 3.8 %collective-permute-done.31 = f32[1,3,9,1]{3,2,1,0:T(8,128)S(1)} collective-permute-done((f32[1,3,9,1]{3,2,1,0:T(8,128)S(1)}, f32[1,3,9,1]{3,2,1,0:T(8,128)S(1)}, u32[]{:S(2)}, u32[]{:S(2)}) %collective-permute-start.31) | collective-permute-done | bytes 140 | tf_op jit(solution)/shard_map/ppermute | solution.py:35
  185.2 3.0 %collective-permute-start.33 = (f32[1,3,1,67]{3,2,1,0:T(1,128)S(1)}, f32[1,3,1,67]{3,2,1,0:T(1,128)S(1)}, u32[]{:S(2)}, u32[]{:S(2)}) collective-permute-start(f32[1,3,1,67]{3,2,1,0:T(1,128)S(1)} %get-tuple-element.170), channel_id=1, source_target_pairs={{32,0},{64,32},{96,64},{128,96},{160,128},{192,160},{224,192},{0,2... | collective-permute-start | bytes 2420 | tf_op jit(solution)/shard_map/ppermute | solution.py:35
  188.1 1.3 collective-permute-done.32
  189.5 1.9 collective-permute-start.34
  191.4 5.4 %collective-permute-start.35 = (f32[1,1,11,67]{3,2,1,0:T(8,128)S(1)}, f32[1,1,11,67]{3,2,1,0:T(8,128)S(1)}, u32[]{:S(2)}, u32[]{:S(2)}) collective-permute-start(f32[1,1,11,67]{3,2,1,0:T(8,128)S(1)} %get-tuple-element.330), channel_id=1, source_target_pairs={{1,0},{2,1},{3,2},{4,3},{5,4},{6,5},{7,6},{8,7},{9,8},{10,9},{11,1... | collective-permute-start | bytes 8852 | tf_op jit(solution)/shard_map/ppermute | solution.py:35
  196.9 1.3 collective-permute-done.35
  200.6 0.7 slice_add_fusion.4
  (416 shorter events, 27.7 us)
Async XLA Ops:
  0.0 0.7 copy-start.8
  0.0 0.7 copy-start.7
  1.9 0.7 copy-start.2
  3.1 0.8 copy-start.1
  4.1 18.3 %collective-permute-start.1 = (f32[3,5,17,3]{3,2,1,0:T(8,128)S(1)}, f32[3,5,17,3]{3,2,1,0:T(8,128)S(1)}, u32[]{:S(2)}, u32[]{:S(2)}) collective-permute-start(f32[3,5,17,3]{3,2,1,0:T(8,128)S(1)} %get-tuple-element.58), channel_id=1, source_target_pairs={{256,0},{512,256},{768,512},{0,768},{257,1},{513,257},{769,513},{1... | collective-permute-start | bytes 9188 | tf_op jit(solution)/shard_map/ppermute | solution.py:246
  6.8 17.1 %collective-permute-start = (f32[3,5,17,3]{3,2,1,0:T(8,128)S(1)}, f32[3,5,17,3]{3,2,1,0:T(8,128)S(1)}, u32[]{:S(2)}, u32[]{:S(2)}) collective-permute-start(f32[3,5,17,3]{3,2,1,0:T(8,128)S(1)} %get-tuple-element.59), channel_id=1, source_target_pairs={{0,256},{256,512},{512,768},{768,0},{1,257},{257,513},{513,769},{7... | collective-permute-start | bytes 9188 | tf_op jit(solution)/shard_map/ppermute | solution.py:245
  21.0 0.7 copy-start.5
  21.0 0.7 copy-start.6
  24.3 1.9 collective-permute-start.3
  24.4 4.9 %collective-permute-start.2 = (f32[3,5,3,133]{3,2,1,0:T(4,128)S(1)}, f32[3,5,3,133]{3,2,1,0:T(4,128)S(1)}, u32[]{:S(2)}, u32[]{:S(2)}) collective-permute-start(f32[3,5,3,133]{3,2,1,0:T(4,128)S(1)} %get-tuple-element.55), channel_id=1, source_target_pairs={{0,32},{32,64},{64,96},{96,128},{128,160},{160,192},{192,224},{224... | collective-permute-start | bytes 71828 | tf_op jit(solution)/shard_map/ppermute | solution.py:245
  29.7 14.6 %collective-permute-start.4 = (f32[3,3,21,133]{3,2,1,0:T(8,128)S(1)}, f32[3,3,21,133]{3,2,1,0:T(8,128)S(1)}, u32[]{:S(2)}, u32[]{:S(2)}) collective-permute-start(f32[3,3,21,133]{3,2,1,0:T(8,128)S(1)} %slice.1762), channel_id=1, source_target_pairs={{0,1},{1,2},{2,3},{3,4},{4,5},{5,6},{6,7},{7,8},{8,9},{9,10},{10,1... | collective-permute-start | bytes 301652 | tf_op jit(solution)/shard_map/ppermute | solution.py:245
  44.4 7.8 %collective-permute-start.5 = (f32[3,3,21,133]{3,2,1,0:T(8,128)S(1)}, f32[3,3,21,133]{3,2,1,0:T(8,128)S(1)}, u32[]{:S(2)}, u32[]{:S(2)}) collective-permute-start(f32[3,3,21,133]{3,2,1,0:T(8,128)S(1)} %get-tuple-element.51), channel_id=1, source_target_pairs={{1,0},{2,1},{3,2},{4,3},{5,4},{6,5},{7,6},{8,7},{9,8},{10,9},{11,1... | collective-permute-start | bytes 301652 | tf_op jit(solution)/shard_map/ppermute | solution.py:246
  66.4 7.8 %collective-permute-start.6 = (f32[1,5,17,1]{3,2,1,0:T(8,128)S(1)}, f32[1,5,17,1]{3,2,1,0:T(8,128)S(1)}, u32[]{:S(2)}, u32[]{:S(2)}) collective-permute-start(f32[1,5,17,1]{3,2,1,0:T(8,128)S(1)} %get-tuple-element.165), channel_id=1, source_target_pairs={{0,256},{256,512},{512,768},{768,0},{1,257},{257,513},{513,769},{7... | collective-permute-start | bytes 1028 | tf_op jit(solution)/shard_map/ppermute | solution.py:33
  72.0 7.3 %collective-permute-start.7 = (f32[1,5,17,1]{3,2,1,0:T(8,128)S(1)}, f32[1,5,17,1]{3,2,1,0:T(8,128)S(1)}, u32[]{:S(2)}, u32[]{:S(2)}) collective-permute-start(f32[1,5,17,1]{3,2,1,0:T(8,128)S(1)} %get-tuple-element.166), channel_id=1, source_target_pairs={{256,0},{512,256},{768,512},{0,768},{257,1},{513,257},{769,513},{1... | collective-permute-start | bytes 1028 | tf_op jit(solution)/shard_map/ppermute | solution.py:35
  79.4 4.3 %collective-permute-start.8 = (f32[1,5,1,131]{3,2,1,0:T(1,128)S(1)}, f32[1,5,1,131]{3,2,1,0:T(1,128)S(1)}, u32[]{:S(2)}, u32[]{:S(2)}) collective-permute-start(f32[1,5,1,131]{3,2,1,0:T(1,128)S(1)} %get-tuple-element.63), channel_id=1, source_target_pairs={{0,32},{32,64},{64,96},{96,128},{128,160},{160,192},{192,224},{224... | collective-permute-start | bytes 7868 | tf_op jit(solution)/shard_map/ppermute | solution.py:33
  79.4 4.3 %collective-permute-start.9 = (f32[1,5,1,131]{3,2,1,0:T(1,128)S(1)}, f32[1,5,1,131]{3,2,1,0:T(1,128)S(1)}, u32[]{:S(2)}, u32[]{:S(2)}) collective-permute-start(f32[1,5,1,131]{3,2,1,0:T(1,128)S(1)} %get-tuple-element.64), channel_id=1, source_target_pairs={{32,0},{64,32},{96,64},{128,96},{160,128},{192,160},{224,192},{0,2... | collective-permute-start | bytes 7868 | tf_op jit(solution)/shard_map/ppermute | solution.py:35
  83.8 7.2 %collective-permute-start.10 = (f32[1,1,19,131]{3,2,1,0:T(8,128)S(1)}, f32[1,1,19,131]{3,2,1,0:T(8,128)S(1)}, u32[]{:S(2)}, u32[]{:S(2)}) collective-permute-start(f32[1,1,19,131]{3,2,1,0:T(8,128)S(1)} %get-tuple-element.163), channel_id=1, source_target_pairs={{0,1},{1,2},{2,3},{3,4},{4,5},{5,6},{6,7},{7,8},{8,9},{9,10},{10,1... | collective-permute-start | bytes 29876 | tf_op jit(solution)/shard_map/ppermute | solution.py:33
  85.8 6.6 %collective-permute-start.11 = (f32[1,1,19,131]{3,2,1,0:T(8,128)S(1)}, f32[1,1,19,131]{3,2,1,0:T(8,128)S(1)}, u32[]{:S(2)}, u32[]{:S(2)}) collective-permute-start(f32[1,1,19,131]{3,2,1,0:T(8,128)S(1)} %get-tuple-element.164), channel_id=1, source_target_pairs={{1,0},{2,1},{3,2},{4,3},{5,4},{6,5},{7,6},{8,7},{9,8},{10,9},{11,1... | collective-permute-start | bytes 29876 | tf_op jit(solution)/shard_map/ppermute | solution.py:35
  92.5 0.7 copy-start.10
  93.3 0.7 copy-start.9
  98.1 0.7 copy-start
  99.3 0.7 slice-start
  100.2 6.0 %collective-permute-start.12 = (f32[2,3,9,1]{3,2,1,0:T(8,128)S(1)}, f32[2,3,9,1]{3,2,1,0:T(8,128)S(1)}, u32[]{:S(2)}, u32[]{:S(2)}) collective-permute-start(f32[2,3,9,1]{3,2,1,0:T(8,128)S(1)} %get-tuple-element.295), channel_id=1, source_target_pairs={{0,256},{256,512},{512,768},{768,0},{1,257},{257,513},{513,769},{7... | collective-permute-start | bytes 656 | tf_op jit(solution)/shard_map/ppermute | solution.py:33
  102.2 7.2 %collective-permute-start.13 = (f32[2,3,9,1]{3,2,1,0:T(8,128)S(1)}, f32[2,3,9,1]{3,2,1,0:T(8,128)S(1)}, u32[]{:S(2)}, u32[]{:S(2)}) collective-permute-start(f32[2,3,9,1]{3,2,1,0:T(8,128)S(1)} %get-tuple-element.296), channel_id=1, source_target_pairs={{256,0},{512,256},{768,512},{0,768},{257,1},{513,257},{769,513},{1... | collective-permute-start | bytes 656 | tf_op jit(solution)/shard_map/ppermute | solution.py:35
  109.5 4.2 %collective-permute-start.14 = (f32[2,3,1,67]{3,2,1,0:T(1,128)S(1)}, f32[2,3,1,67]{3,2,1,0:T(1,128)S(1)}, u32[]{:S(2)}, u32[]{:S(2)}) collective-permute-start(f32[2,3,1,67]{3,2,1,0:T(1,128)S(1)} %get-tuple-element.148), channel_id=1, source_target_pairs={{0,32},{32,64},{64,96},{96,128},{128,160},{160,192},{192,224},{224... | collective-permute-start | bytes 4832 | tf_op jit(solution)/shard_map/ppermute | solution.py:33
  109.5 4.3 %collective-permute-start.15 = (f32[2,3,1,67]{3,2,1,0:T(1,128)S(1)}, f32[2,3,1,67]{3,2,1,0:T(1,128)S(1)}, u32[]{:S(2)}, u32[]{:S(2)}) collective-permute-start(f32[2,3,1,67]{3,2,1,0:T(1,128)S(1)} %get-tuple-element.149), channel_id=1, source_target_pairs={{32,0},{64,32},{96,64},{128,96},{160,128},{192,160},{224,192},{0,2... | collective-permute-start | bytes 4832 | tf_op jit(solution)/shard_map/ppermute | solution.py:35
  113.9 7.4 %collective-permute-start.16 = (f32[2,1,11,67]{3,2,1,0:T(8,128)S(1)}, f32[2,1,11,67]{3,2,1,0:T(8,128)S(1)}, u32[]{:S(2)}, u32[]{:S(2)}) collective-permute-start(f32[2,1,11,67]{3,2,1,0:T(8,128)S(1)} %get-tuple-element.293), channel_id=1, source_target_pairs={{0,1},{1,2},{2,3},{3,4},{4,5},{5,6},{6,7},{7,8},{8,9},{9,10},{10,1... | collective-permute-start | bytes 17696 | tf_op jit(solution)/shard_map/ppermute | solution.py:33
  115.8 6.9 %collective-permute-start.17 = (f32[2,1,11,67]{3,2,1,0:T(8,128)S(1)}, f32[2,1,11,67]{3,2,1,0:T(8,128)S(1)}, u32[]{:S(2)}, u32[]{:S(2)}) collective-permute-start(f32[2,1,11,67]{3,2,1,0:T(8,128)S(1)} %get-tuple-element.294), channel_id=1, source_target_pairs={{1,0},{2,1},{3,2},{4,3},{5,4},{6,5},{7,6},{8,7},{9,8},{10,9},{11,1... | collective-permute-start | bytes 17696 | tf_op jit(solution)/shard_map/ppermute | solution.py:35
  122.7 0.7 copy-start.4
  123.5 0.7 copy-start.3
  126.3 5.9 %collective-permute-start.18 = (f32[1,3,9,1]{3,2,1,0:T(8,128)S(1)}, f32[1,3,9,1]{3,2,1,0:T(8,128)S(1)}, u32[]{:S(2)}, u32[]{:S(2)}) collective-permute-start(f32[1,3,9,1]{3,2,1,0:T(8,128)S(1)} %get-tuple-element.343), channel_id=1, source_target_pairs={{0,256},{256,512},{512,768},{768,0},{1,257},{257,513},{513,769},{7... | collective-permute-start | bytes 332 | tf_op jit(solution)/shard_map/ppermute | solution.py:33
  128.3 6.9 %collective-permute-start.19 = (f32[1,3,9,1]{3,2,1,0:T(8,128)S(1)}, f32[1,3,9,1]{3,2,1,0:T(8,128)S(1)}, u32[]{:S(2)}, u32[]{:S(2)}) collective-permute-start(f32[1,3,9,1]{3,2,1,0:T(8,128)S(1)} %get-tuple-element.344), channel_id=1, source_target_pairs={{256,0},{512,256},{768,512},{0,768},{257,1},{513,257},{769,513},{1... | collective-permute-start | bytes 332 | tf_op jit(solution)/shard_map/ppermute | solution.py:35
  135.3 4.2 %collective-permute-start.20 = (f32[1,3,1,67]{3,2,1,0:T(1,128)S(1)}, f32[1,3,1,67]{3,2,1,0:T(1,128)S(1)}, u32[]{:S(2)}, u32[]{:S(2)}) collective-permute-start(f32[1,3,1,67]{3,2,1,0:T(1,128)S(1)} %get-tuple-element.173), channel_id=1, source_target_pairs={{0,32},{32,64},{64,96},{96,128},{128,160},{160,192},{192,224},{224... | collective-permute-start | bytes 2420 | tf_op jit(solution)/shard_map/ppermute | solution.py:33
  135.3 4.3 %collective-permute-start.21 = (f32[1,3,1,67]{3,2,1,0:T(1,128)S(1)}, f32[1,3,1,67]{3,2,1,0:T(1,128)S(1)}, u32[]{:S(2)}, u32[]{:S(2)}) collective-permute-start(f32[1,3,1,67]{3,2,1,0:T(1,128)S(1)} %get-tuple-element.174), channel_id=1, source_target_pairs={{32,0},{64,32},{96,64},{128,96},{160,128},{192,160},{224,192},{0,2... | collective-permute-start | bytes 2420 | tf_op jit(solution)/shard_map/ppermute | solution.py:35
  139.6 7.3 %collective-permute-start.22 = (f32[1,1,11,67]{3,2,1,0:T(8,128)S(1)}, f32[1,1,11,67]{3,2,1,0:T(8,128)S(1)}, u32[]{:S(2)}, u32[]{:S(2)}) collective-permute-start(f32[1,1,11,67]{3,2,1,0:T(8,128)S(1)} %get-tuple-element.341), channel_id=1, source_target_pairs={{0,1},{1,2},{2,3},{3,4},{4,5},{5,6},{6,7},{7,8},{8,9},{9,10},{10,1... | collective-permute-start | bytes 8852 | tf_op jit(solution)/shard_map/ppermute | solution.py:33
  141.6 6.8 %collective-permute-start.23 = (f32[1,1,11,67]{3,2,1,0:T(8,128)S(1)}, f32[1,1,11,67]{3,2,1,0:T(8,128)S(1)}, u32[]{:S(2)}, u32[]{:S(2)}) collective-permute-start(f32[1,1,11,67]{3,2,1,0:T(8,128)S(1)} %get-tuple-element.342), channel_id=1, source_target_pairs={{1,0},{2,1},{3,2},{4,3},{5,4},{6,5},{7,6},{8,7},{9,8},{10,9},{11,1... | collective-permute-start | bytes 8852 | tf_op jit(solution)/shard_map/ppermute | solution.py:35
  150.8 5.9 %collective-permute-start.24 = (f32[1,3,9,1]{3,2,1,0:T(8,128)S(1)}, f32[1,3,9,1]{3,2,1,0:T(8,128)S(1)}, u32[]{:S(2)}, u32[]{:S(2)}) collective-permute-start(f32[1,3,9,1]{3,2,1,0:T(8,128)S(1)} %get-tuple-element.337), channel_id=1, source_target_pairs={{0,256},{256,512},{512,768},{768,0},{1,257},{257,513},{513,769},{7... | collective-permute-start | bytes 332 | tf_op jit(solution)/shard_map/ppermute | solution.py:33
  152.9 6.9 %collective-permute-start.25 = (f32[1,3,9,1]{3,2,1,0:T(8,128)S(1)}, f32[1,3,9,1]{3,2,1,0:T(8,128)S(1)}, u32[]{:S(2)}, u32[]{:S(2)}) collective-permute-start(f32[1,3,9,1]{3,2,1,0:T(8,128)S(1)} %get-tuple-element.338), channel_id=1, source_target_pairs={{256,0},{512,256},{768,512},{0,768},{257,1},{513,257},{769,513},{1... | collective-permute-start | bytes 332 | tf_op jit(solution)/shard_map/ppermute | solution.py:35
  159.9 4.2 %collective-permute-start.26 = (f32[1,3,1,67]{3,2,1,0:T(1,128)S(1)}, f32[1,3,1,67]{3,2,1,0:T(1,128)S(1)}, u32[]{:S(2)}, u32[]{:S(2)}) collective-permute-start(f32[1,3,1,67]{3,2,1,0:T(1,128)S(1)} %get-tuple-element.171), channel_id=1, source_target_pairs={{0,32},{32,64},{64,96},{96,128},{128,160},{160,192},{192,224},{224... | collective-permute-start | bytes 2420 | tf_op jit(solution)/shard_map/ppermute | solution.py:33
  159.9 4.3 %collective-permute-start.27 = (f32[1,3,1,67]{3,2,1,0:T(1,128)S(1)}, f32[1,3,1,67]{3,2,1,0:T(1,128)S(1)}, u32[]{:S(2)}, u32[]{:S(2)}) collective-permute-start(f32[1,3,1,67]{3,2,1,0:T(1,128)S(1)} %get-tuple-element.172), channel_id=1, source_target_pairs={{32,0},{64,32},{96,64},{128,96},{160,128},{192,160},{224,192},{0,2... | collective-permute-start | bytes 2420 | tf_op jit(solution)/shard_map/ppermute | solution.py:35
  164.3 7.3 %collective-permute-start.28 = (f32[1,1,11,67]{3,2,1,0:T(8,128)S(1)}, f32[1,1,11,67]{3,2,1,0:T(8,128)S(1)}, u32[]{:S(2)}, u32[]{:S(2)}) collective-permute-start(f32[1,1,11,67]{3,2,1,0:T(8,128)S(1)} %get-tuple-element.335), channel_id=1, source_target_pairs={{0,1},{1,2},{2,3},{3,4},{4,5},{5,6},{6,7},{7,8},{8,9},{9,10},{10,1... | collective-permute-start | bytes 8852 | tf_op jit(solution)/shard_map/ppermute | solution.py:33
  166.2 6.8 %collective-permute-start.29 = (f32[1,1,11,67]{3,2,1,0:T(8,128)S(1)}, f32[1,1,11,67]{3,2,1,0:T(8,128)S(1)}, u32[]{:S(2)}, u32[]{:S(2)}) collective-permute-start(f32[1,1,11,67]{3,2,1,0:T(8,128)S(1)} %get-tuple-element.336), channel_id=1, source_target_pairs={{1,0},{2,1},{3,2},{4,3},{5,4},{6,5},{7,6},{8,7},{9,8},{10,9},{11,1... | collective-permute-start | bytes 8852 | tf_op jit(solution)/shard_map/ppermute | solution.py:35
  175.4 5.9 %collective-permute-start.30 = (f32[1,3,9,1]{3,2,1,0:T(8,128)S(1)}, f32[1,3,9,1]{3,2,1,0:T(8,128)S(1)}, u32[]{:S(2)}, u32[]{:S(2)}) collective-permute-start(f32[1,3,9,1]{3,2,1,0:T(8,128)S(1)} %get-tuple-element.331), channel_id=1, source_target_pairs={{0,256},{256,512},{512,768},{768,0},{1,257},{257,513},{513,769},{7... | collective-permute-start | bytes 332 | tf_op jit(solution)/shard_map/ppermute | solution.py:33
  178.1 6.9 %collective-permute-start.31 = (f32[1,3,9,1]{3,2,1,0:T(8,128)S(1)}, f32[1,3,9,1]{3,2,1,0:T(8,128)S(1)}, u32[]{:S(2)}, u32[]{:S(2)}) collective-permute-start(f32[1,3,9,1]{3,2,1,0:T(8,128)S(1)} %get-tuple-element.332), channel_id=1, source_target_pairs={{256,0},{512,256},{768,512},{0,768},{257,1},{513,257},{769,513},{1... | collective-permute-start | bytes 332 | tf_op jit(solution)/shard_map/ppermute | solution.py:35
  185.2 4.2 %collective-permute-start.32 = (f32[1,3,1,67]{3,2,1,0:T(1,128)S(1)}, f32[1,3,1,67]{3,2,1,0:T(1,128)S(1)}, u32[]{:S(2)}, u32[]{:S(2)}) collective-permute-start(f32[1,3,1,67]{3,2,1,0:T(1,128)S(1)} %get-tuple-element.169), channel_id=1, source_target_pairs={{0,32},{32,64},{64,96},{96,128},{128,160},{160,192},{192,224},{224... | collective-permute-start | bytes 2420 | tf_op jit(solution)/shard_map/ppermute | solution.py:33
  185.2 4.3 %collective-permute-start.33 = (f32[1,3,1,67]{3,2,1,0:T(1,128)S(1)}, f32[1,3,1,67]{3,2,1,0:T(1,128)S(1)}, u32[]{:S(2)}, u32[]{:S(2)}) collective-permute-start(f32[1,3,1,67]{3,2,1,0:T(1,128)S(1)} %get-tuple-element.170), channel_id=1, source_target_pairs={{32,0},{64,32},{96,64},{128,96},{160,128},{192,160},{224,192},{0,2... | collective-permute-start | bytes 2420 | tf_op jit(solution)/shard_map/ppermute | solution.py:35
  189.5 7.3 %collective-permute-start.34 = (f32[1,1,11,67]{3,2,1,0:T(8,128)S(1)}, f32[1,1,11,67]{3,2,1,0:T(8,128)S(1)}, u32[]{:S(2)}, u32[]{:S(2)}) collective-permute-start(f32[1,1,11,67]{3,2,1,0:T(8,128)S(1)} %get-tuple-element.329), channel_id=1, source_target_pairs={{0,1},{1,2},{2,3},{3,4},{4,5},{5,6},{6,7},{7,8},{8,9},{9,10},{10,1... | collective-permute-start | bytes 8852 | tf_op jit(solution)/shard_map/ppermute | solution.py:33
  191.4 6.8 %collective-permute-start.35 = (f32[1,1,11,67]{3,2,1,0:T(8,128)S(1)}, f32[1,1,11,67]{3,2,1,0:T(8,128)S(1)}, u32[]{:S(2)}, u32[]{:S(2)}) collective-permute-start(f32[1,1,11,67]{3,2,1,0:T(8,128)S(1)} %get-tuple-element.330), channel_id=1, source_target_pairs={{1,0},{2,1},{3,2},{4,3},{5,4},{6,5},{7,6},{8,7},{9,8},{10,9},{11,1... | collective-permute-start | bytes 8852 | tf_op jit(solution)/shard_map/ppermute | solution.py:35

commit v2 on v1

--- a/solution.py
+++ b/solution.py
@@ -64,8 +64,14 @@
 def spread(node_field):
     length_x = node_field.shape[2]
     elements_x = (length_x - 1) // 2
-    even_x = lax.slice_in_dim(node_field, 0, length_x, 2, axis=2)
-    odd_x = lax.slice_in_dim(node_field, 1, length_x, 2, axis=2)
+    order = np.concatenate([np.arange(0, length_x, 2), np.arange(1, length_x, 2)])
+    chooser = np.zeros((length_x, length_x), np.float32)
+    chooser[order, np.arange(length_x)] = 1.0
+    sorted_x = jnp.einsum(
+        "zyx,xk->zyk", node_field, jnp.asarray(chooser), precision=lax.Precision.HIGHEST
+    )
+    even_x = lax.slice_in_dim(sorted_x, 0, elements_x + 1, axis=2)
+    odd_x = lax.slice_in_dim(sorted_x, elements_x + 1, length_x, axis=2)
     along_x = jnp.stack(
         [
             lax.slice_in_dim(even_x, 0, elements_x, axis=2),

time: 202 us -> 207 us (1.025)
  waiting for transfers between devices: 53.7 us -> 62.8 us
  starting transfers between devices: 105 us -> 101 us
  local copies, waits for them, and re-layouts: 26.5 us -> 24.3 us
    ppermute x15, waiting for transfers between devices: 6.21 us -> 23.6 us  [padded(): lax.ppermute(tail, axis, [(i, (i + 1) % count) for i in range(count)])]
    ppermute x15, starting transfers between devices: 58.4 us -> 45.2 us  [padded(): lax.ppermute(head, axis, [((i + 1) % count, i) for i in range(count)])]
    slice x12 -> x1, local copies, waits for them, and re-layouts: 8.09 us -> 0.01 us  [widened(): lax.slice_in_dim(stacked, length_here - 1, length_here, axis=dim)]
    ppermute x15, waiting for transfers between devices: 25.3 us -> 18.1 us  [padded(): lax.ppermute(head, axis, [((i + 1) % count, i) for i in range(count)])]
    ppermute x15, starting transfers between devices: 23.9 us -> 30.5 us  [padded(): lax.ppermute(tail, axis, [(i, (i + 1) % count) for i in range(count)])]
    ppermute x3, starting transfers between devices: 6.77 us -> 9.24 us  [widened(): lax.ppermute(head, axis, [((i + 1) % count, i) for i in range(count)])]
    unnamed x24 -> x47, local copies, waits for them, and re-layouts: 5.25 us -> 7.46 us
  transfers between devices with their start and end apart: 36 -> 36, of which waited for: 22 -> 20; matrix products, arithmetic and copies ran while one was open for 1% -> 1% of each run, Pallas kernels for 0% -> 0%
where the time goes in v2:
time: 207 us; the launch traced here: 206 us
  starting transfers between devices  101 us (49%)
  waiting for transfers between devices  62.8 us (30%)
  local copies, waits for them, and re-layouts  24.3 us (12%)
  other arithmetic  13.3 us (6%)
  between operations  3.08 us (1%)
    ppermute x15, starting transfers between devices, padded(): lax.ppermute(head, axis, [((i + 1) % count, i) for i in range(count)])  45.2 us
    ppermute x15, starting transfers between devices, padded(): lax.ppermute(tail, axis, [(i, (i + 1) % count) for i in range(count)])  30.5 us
    ppermute x15, waiting for transfers between devices, padded(): lax.ppermute(tail, axis, [(i, (i + 1) % count) for i in range(count)])  23.6 us
    ppermute x15, waiting for transfers between devices, padded(): lax.ppermute(head, axis, [((i + 1) % count, i) for i in range(count)])  18.1 us
    ppermute x3, waiting for transfers between devices, widened(): lax.ppermute(tail, axis, [(i, (i + 1) % count) for i in range(count)])  16.1 us
    ppermute x3, starting transfers between devices, widened(): lax.ppermute(tail, axis, [(i, (i + 1) % count) for i in range(count)])  16 us
    ppermute x3, starting transfers between devices, widened(): lax.ppermute(head, axis, [((i + 1) % count, i) for i in range(count)])  9.24 us
    unnamed x47, local copies, waits for them, and re-layouts  7.46 us
  transfers between devices with their start and end apart: 36, of which 20 were waited for; matrix products, arithmetic and copies ran while one was open for 1% of the time, Pallas kernels for 0%

profile of v2, /device:TPU:24, one launch (start us, length us, event | category | flops | bytes accessed | tf_op | source)
XLA Modules:
  0.0 205.8 jit_solution(11722830829237532686)
XLA Ops:
  0.0 0.7 copy-done.10
  0.7 0.8 multiply_add_fusion.24
  2.0 0.7 copy-done.2
  2.9 0.6 copy-done.3
  4.8 2.7 %collective-permute-start.1 = (f32[3,5,17,3]{3,0,2,1:T(4,128)S(1)}, f32[3,5,17,3]{3,0,2,1:T(4,128)S(1)}, u32[]{:S(2)}, u32[]{:S(2)}) collective-permute-start(f32[3,5,17,3]{3,0,2,1:T(4,128)S(1)} %get-tuple-element.58), channel_id=1, source_target_pairs={{256,0},{512,256},{768,512},{0,768},{257,1},{513,257},{769,513},{1... | collective-permute-start | bytes 9188 | tf_op jit(solution)/shard_map/ppermute | solution.py:252
  7.4 14.0 %collective-permute-start = (f32[3,5,17,3]{3,0,2,1:T(4,128)S(1)}, f32[3,5,17,3]{3,0,2,1:T(4,128)S(1)}, u32[]{:S(2)}, u32[]{:S(2)}) collective-permute-start(f32[3,5,17,3]{3,0,2,1:T(4,128)S(1)} %get-tuple-element.59), channel_id=1, source_target_pairs={{0,256},{256,512},{512,768},{768,0},{1,257},{257,513},{513,769},{7... | collective-permute-start | bytes 9188 | tf_op jit(solution)/shard_map/ppermute | solution.py:251
  21.7 0.6 copy-done.9
  23.1 1.3 collective-permute-done
  24.5 2.3 %concatenate.228 = f32[3,5,17,133]{3,0,2,1:T(4,128)S(1)} concatenate(f32[3,5,17,2]{3,0,2,1:T(4,128)S(1)} %bitcast.603, f32[3,5,17,1]{3,0,2,1:T(4,128)S(1)} %get-tuple-element.57, f32[3,5,17,127]{3,0,2,1:T(4,128)S(1)} %slice.1742, f32[3,5,17,1]{3,0,2,1:T(4,128)S(1)} %get-tuple-element.56, f32[3,5,17,2]{3,0,2,1:T(4,128)S(1)} %slice.1746), dimensions={3} | concatenate | bytes 271320 | tf_op jit(solution)/shard_map/concatenate | solution.py:253
  27.1 2.9 %collective-permute-start.3 = (f32[3,5,3,133]{3,2,1,0:T(4,128)S(1)}, f32[3,5,3,133]{3,2,1,0:T(4,128)S(1)}, u32[]{:S(2)}, u32[]{:S(2)}) collective-permute-start(f32[3,5,3,133]{3,2,1,0:T(4,128)S(1)} %copy.793), channel_id=1, source_target_pairs={{32,0},{64,32},{96,64},{128,96},{160,128},{192,160},{224,192},{0,2... | collective-permute-start | bytes 71828 | tf_op jit(solution)/shard_map/ppermute | solution.py:252
  30.0 1.7 collective-permute-done.2
  31.8 0.6 copy-done.5
  32.5 0.7 slice-done.1
  33.6 1.9 collective-permute-start.4
  35.6 13.1 %collective-permute-done.4 = f32[3,3,21,133]{3,2,1,0:T(8,128)S(1)} collective-permute-done((f32[3,3,21,133]{3,2,1,0:T(8,128)S(1)}, f32[3,3,21,133]{3,2,1,0:T(8,128)S(1)}, u32[]{:S(2)}, u32[]{:S(2)}) %collective-permute-start.4) | collective-permute-done | bytes 100580 | tf_op jit(solution)/shard_map/ppermute | solution.py:251
  48.7 3.6 %collective-permute-start.5 = (f32[3,3,21,133]{3,2,1,0:T(8,128)S(1)}, f32[3,3,21,133]{3,2,1,0:T(8,128)S(1)}, u32[]{:S(2)}, u32[]{:S(2)}) collective-permute-start(f32[3,3,21,133]{3,2,1,0:T(8,128)S(1)} %get-tuple-element.51), channel_id=1, source_target_pairs={{1,0},{2,1},{3,2},{4,3},{5,4},{6,5},{7,6},{8,7},{9,8},{10,9},{11,1... | collective-permute-start | bytes 301652 | tf_op jit(solution)/shard_map/ppermute | solution.py:252
  52.5 4.9 %collective-permute-done.5 = f32[3,3,21,133]{3,2,1,0:T(8,128)S(1)} collective-permute-done((f32[3,3,21,133]{3,2,1,0:T(8,128)S(1)}, f32[3,3,21,133]{3,2,1,0:T(8,128)S(1)}, u32[]{:S(2)}, u32[]{:S(2)}) %collective-permute-start.5) | collective-permute-done | bytes 100580 | tf_op jit(solution)/shard_map/ppermute | solution.py:252
  57.4 0.9 slice.1356
  64.5 0.7 copy-done.4
  67.5 5.6 %collective-permute-start.6 = (f32[1,5,17,1]{3,2,1,0:T(8,128)S(1)}, f32[1,5,17,1]{3,2,1,0:T(8,128)S(1)}, u32[]{:S(2)}, u32[]{:S(2)}) collective-permute-start(f32[1,5,17,1]{3,2,1,0:T(8,128)S(1)} %get-tuple-element.164), channel_id=1, source_target_pairs={{0,256},{256,512},{512,768},{768,0},{1,257},{257,513},{513,769},{7... | collective-permute-start | bytes 1028 | tf_op jit(solution)/shard_map/ppermute | solution.py:33
  73.2 1.9 collective-permute-start.7
  75.3 5.2 %collective-permute-done.7 = f32[1,5,17,1]{3,2,1,0:T(8,128)S(1)} collective-permute-done((f32[1,5,17,1]{3,2,1,0:T(8,128)S(1)}, f32[1,5,17,1]{3,2,1,0:T(8,128)S(1)}, u32[]{:S(2)}, u32[]{:S(2)}) %collective-permute-start.7) | collective-permute-done | bytes 372 | tf_op jit(solution)/shard_map/ppermute | solution.py:35
  80.7 2.9 %collective-permute-start.9 = (f32[1,5,1,131]{3,0,2,1:T(1,128)S(1)}, f32[1,5,1,131]{3,0,2,1:T(1,128)S(1)}, u32[]{:S(2)}, u32[]{:S(2)}) collective-permute-start(f32[1,5,1,131]{3,0,2,1:T(1,128)S(1)} %get-tuple-element.147), channel_id=1, source_target_pairs={{32,0},{64,32},{96,64},{128,96},{160,128},{192,160},{224,192},{0,2... | collective-permute-start | bytes 7868 | tf_op jit(solution)/shard_map/ppermute | solution.py:35
  83.9 1.0 collective-permute-done.8
  85.3 4.6 %collective-permute-start.11 = (f32[1,1,19,131]{3,2,1,0:T(8,128)S(1)}, f32[1,1,19,131]{3,2,1,0:T(8,128)S(1)}, u32[]{:S(2)}, u32[]{:S(2)}) collective-permute-start(f32[1,1,19,131]{3,2,1,0:T(8,128)S(1)} %copy.833), channel_id=1, source_target_pairs={{1,0},{2,1},{3,2},{4,3},{5,4},{6,5},{7,6},{8,7},{9,8},{10,9},{11,1... | collective-permute-start | bytes 29876 | tf_op jit(solution)/shard_map/ppermute | solution.py:35
  89.9 2.1 %collective-permute-start.10 = (f32[1,1,19,131]{3,2,1,0:T(8,128)S(1)}, f32[1,1,19,131]{3,2,1,0:T(8,128)S(1)}, u32[]{:S(2)}, u32[]{:S(2)}) collective-permute-start(f32[1,1,19,131]{3,2,1,0:T(8,128)S(1)} %copy.834), channel_id=1, source_target_pairs={{0,1},{1,2},{2,3},{3,4},{4,5},{5,6},{6,7},{7,8},{8,9},{9,10},{10,1... | collective-permute-start | bytes 29876 | tf_op jit(solution)/shard_map/ppermute | solution.py:33
  92.1 4.8 %collective-permute-done.10 = f32[1,1,19,131]{3,2,1,0:T(8,128)S(1)} collective-permute-done((f32[1,1,19,131]{3,2,1,0:T(8,128)S(1)}, f32[1,1,19,131]{3,2,1,0:T(8,128)S(1)}, u32[]{:S(2)}, u32[]{:S(2)}) %collective-permute-start.10) | collective-permute-done | bytes 9988 | tf_op jit(solution)/shard_map/ppermute | solution.py:33
  96.9 0.6 copy-done.12
  102.4 0.6 slice-done
  103.3 1.9 collective-permute-start.12
  105.2 3.9 %collective-permute-start.13 = (f32[2,3,9,1]{3,0,2,1:T(2,128)S(1)}, f32[2,3,9,1]{3,0,2,1:T(2,128)S(1)}, u32[]{:S(2)}, u32[]{:S(2)}) collective-permute-start(f32[2,3,9,1]{3,0,2,1:T(2,128)S(1)} %get-tuple-element.325), channel_id=1, source_target_pairs={{256,0},{512,256},{768,512},{0,768},{257,1},{513,257},{769,513},{1... | collective-permute-start | bytes 656 | tf_op jit(solution)/shard_map/ppermute | solution.py:35
  109.2 3.0 %collective-permute-done.13 = f32[2,3,9,1]{3,0,2,1:T(2,128)S(1)} collective-permute-done((f32[2,3,9,1]{3,0,2,1:T(2,128)S(1)}, f32[2,3,9,1]{3,0,2,1:T(2,128)S(1)}, u32[]{:S(2)}, u32[]{:S(2)}) %collective-permute-start.13) | collective-permute-done | bytes 248 | tf_op jit(solution)/shard_map/ppermute | solution.py:35
  112.3 2.9 %collective-permute-start.15 = (f32[2,3,1,67]{3,0,2,1:T(2,128)S(1)}, f32[2,3,1,67]{3,0,2,1:T(2,128)S(1)}, u32[]{:S(2)}, u32[]{:S(2)}) collective-permute-start(f32[2,3,1,67]{3,0,2,1:T(2,128)S(1)} %get-tuple-element.172), channel_id=1, source_target_pairs={{32,0},{64,32},{96,64},{128,96},{160,128},{192,160},{224,192},{0,2... | collective-permute-start | bytes 4832 | tf_op jit(solution)/shard_map/ppermute | solution.py:35
  115.2 1.3 collective-permute-done.14
  116.8 1.9 collective-permute-start.17
  118.7 3.9 %collective-permute-start.16 = (f32[2,1,11,67]{3,1,2,0:T(1,128)S(1)}, f32[2,1,11,67]{3,1,2,0:T(1,128)S(1)}, u32[]{:S(2)}, u32[]{:S(2)}) collective-permute-start(f32[2,1,11,67]{3,1,2,0:T(1,128)S(1)} %copy.836), channel_id=1, source_target_pairs={{0,1},{1,2},{2,3},{3,4},{4,5},{5,6},{6,7},{7,8},{8,9},{9,10},{10,1... | collective-permute-start | bytes 17696 | tf_op jit(solution)/shard_map/ppermute | solution.py:33
  122.6 2.8 %collective-permute-done.16 = f32[2,1,11,67]{3,1,2,0:T(1,128)S(1)} collective-permute-done((f32[2,1,11,67]{3,1,2,0:T(1,128)S(1)}, f32[2,1,11,67]{3,1,2,0:T(1,128)S(1)}, u32[]{:S(2)}, u32[]{:S(2)}) %collective-permute-start.16) | collective-permute-done | bytes 5928 | tf_op jit(solution)/shard_map/ppermute | solution.py:33
  125.6 0.6 copy-done.8
  127.1 0.7 copy-done.1
  129.8 1.9 collective-permute-start.18
  131.7 3.9 %collective-permute-start.19 = (f32[1,3,9,1]{3,1,2,0:T(4,128)S(1)}, f32[1,3,9,1]{3,1,2,0:T(4,128)S(1)}, u32[]{:S(2)}, u32[]{:S(2)}) collective-permute-start(f32[1,3,9,1]{3,1,2,0:T(4,128)S(1)} %get-tuple-element.348), channel_id=1, source_target_pairs={{256,0},{512,256},{768,512},{0,768},{257,1},{513,257},{769,513},{1... | collective-permute-start | bytes 332 | tf_op jit(solution)/shard_map/ppermute | solution.py:35
  135.6 2.9 %collective-permute-done.19 = f32[1,3,9,1]{3,1,2,0:T(4,128)S(1)} collective-permute-done((f32[1,3,9,1]{3,1,2,0:T(4,128)S(1)}, f32[1,3,9,1]{3,1,2,0:T(4,128)S(1)}, u32[]{:S(2)}, u32[]{:S(2)}) %collective-permute-start.19) | collective-permute-done | bytes 140 | tf_op jit(solution)/shard_map/ppermute | solution.py:35
  138.7 3.0 %collective-permute-start.21 = (f32[1,3,1,67]{3,0,2,1:T(1,128)S(1)}, f32[1,3,1,67]{3,0,2,1:T(1,128)S(1)}, u32[]{:S(2)}, u32[]{:S(2)}) collective-permute-start(f32[1,3,1,67]{3,0,2,1:T(1,128)S(1)} %get-tuple-element.309), channel_id=1, source_target_pairs={{32,0},{64,32},{96,64},{128,96},{160,128},{192,160},{224,192},{0,2... | collective-permute-start | bytes 2420 | tf_op jit(solution)/shard_map/ppermute | solution.py:35
  141.6 1.3 collective-permute-done.20
  143.1 1.9 collective-permute-start.23
  145.0 3.9 %collective-permute-start.22 = (f32[1,1,11,67]{3,1,2,0:T(1,128)S(1)}, f32[1,1,11,67]{3,1,2,0:T(1,128)S(1)}, u32[]{:S(2)}, u32[]{:S(2)}) collective-permute-start(f32[1,1,11,67]{3,1,2,0:T(1,128)S(1)} %copy.838), channel_id=1, source_target_pairs={{0,1},{1,2},{2,3},{3,4},{4,5},{5,6},{6,7},{7,8},{8,9},{9,10},{10,1... | collective-permute-start | bytes 8852 | tf_op jit(solution)/shard_map/ppermute | solution.py:33
  149.0 2.8 %collective-permute-done.22 = f32[1,1,11,67]{3,1,2,0:T(1,128)S(1)} collective-permute-done((f32[1,1,11,67]{3,1,2,0:T(1,128)S(1)}, f32[1,1,11,67]{3,1,2,0:T(1,128)S(1)}, u32[]{:S(2)}, u32[]{:S(2)}) %collective-permute-start.22) | collective-permute-done | bytes 2980 | tf_op jit(solution)/shard_map/ppermute | solution.py:33
  154.0 2.1 %collective-permute-start.24 = (f32[1,3,9,1]{3,1,2,0:T(4,128)S(1)}, f32[1,3,9,1]{3,1,2,0:T(4,128)S(1)}, u32[]{:S(2)}, u32[]{:S(2)}) collective-permute-start(f32[1,3,9,1]{3,1,2,0:T(4,128)S(1)} %get-tuple-element.345), channel_id=1, source_target_pairs={{0,256},{256,512},{512,768},{768,0},{1,257},{257,513},{513,769},{7... | collective-permute-start | bytes 332 | tf_op jit(solution)/shard_map/ppermute | solution.py:33
  156.1 3.7 %collective-permute-start.25 = (f32[1,3,9,1]{3,1,2,0:T(4,128)S(1)}, f32[1,3,9,1]{3,1,2,0:T(4,128)S(1)}, u32[]{:S(2)}, u32[]{:S(2)}) collective-permute-start(f32[1,3,9,1]{3,1,2,0:T(4,128)S(1)} %get-tuple-element.346), channel_id=1, source_target_pairs={{256,0},{512,256},{768,512},{0,768},{257,1},{513,257},{769,513},{1... | collective-permute-start | bytes 332 | tf_op jit(solution)/shard_map/ppermute | solution.py:35
  159.9 3.1 %collective-permute-done.25 = f32[1,3,9,1]{3,1,2,0:T(4,128)S(1)} collective-permute-done((f32[1,3,9,1]{3,1,2,0:T(4,128)S(1)}, f32[1,3,9,1]{3,1,2,0:T(4,128)S(1)}, u32[]{:S(2)}, u32[]{:S(2)}) %collective-permute-start.25) | collective-permute-done | bytes 140 | tf_op jit(solution)/shard_map/ppermute | solution.py:35
  163.1 3.0 %collective-permute-start.27 = (f32[1,3,1,67]{3,0,2,1:T(1,128)S(1)}, f32[1,3,1,67]{3,0,2,1:T(1,128)S(1)}, u32[]{:S(2)}, u32[]{:S(2)}) collective-permute-start(f32[1,3,1,67]{3,0,2,1:T(1,128)S(1)} %get-tuple-element.307), channel_id=1, source_target_pairs={{32,0},{64,32},{96,64},{128,96},{160,128},{192,160},{224,192},{0,2... | collective-permute-start | bytes 2420 | tf_op jit(solution)/shard_map/ppermute | solution.py:35
  166.0 1.3 collective-permute-done.26
  167.5 2.7 %collective-permute-start.29 = (f32[1,1,11,67]{3,1,2,0:T(1,128)S(1)}, f32[1,1,11,67]{3,1,2,0:T(1,128)S(1)}, u32[]{:S(2)}, u32[]{:S(2)}) collective-permute-start(f32[1,1,11,67]{3,1,2,0:T(1,128)S(1)} %copy.839), channel_id=1, source_target_pairs={{1,0},{2,1},{3,2},{4,3},{5,4},{6,5},{7,6},{8,7},{9,8},{10,9},{11,1... | collective-permute-start | bytes 8852 | tf_op jit(solution)/shard_map/ppermute | solution.py:35
  170.2 3.1 %collective-permute-start.28 = (f32[1,1,11,67]{3,1,2,0:T(1,128)S(1)}, f32[1,1,11,67]{3,1,2,0:T(1,128)S(1)}, u32[]{:S(2)}, u32[]{:S(2)}) collective-permute-start(f32[1,1,11,67]{3,1,2,0:T(1,128)S(1)} %copy.840), channel_id=1, source_target_pairs={{0,1},{1,2},{2,3},{3,4},{4,5},{5,6},{6,7},{7,8},{8,9},{9,10},{10,1... | collective-permute-start | bytes 8852 | tf_op jit(solution)/shard_map/ppermute | solution.py:33
  173.3 3.6 %collective-permute-done.28 = f32[1,1,11,67]{3,1,2,0:T(1,128)S(1)} collective-permute-done((f32[1,1,11,67]{3,1,2,0:T(1,128)S(1)}, f32[1,1,11,67]{3,1,2,0:T(1,128)S(1)}, u32[]{:S(2)}, u32[]{:S(2)}) %collective-permute-start.28) | collective-permute-done | bytes 2980 | tf_op jit(solution)/shard_map/ppermute | solution.py:33
  179.1 2.7 %collective-permute-start.30 = (f32[1,3,9,1]{3,1,2,0:T(4,128)S(1)}, f32[1,3,9,1]{3,1,2,0:T(4,128)S(1)}, u32[]{:S(2)}, u32[]{:S(2)}) collective-permute-start(f32[1,3,9,1]{3,1,2,0:T(4,128)S(1)} %get-tuple-element.343), channel_id=1, source_target_pairs={{0,256},{256,512},{512,768},{768,0},{1,257},{257,513},{513,769},{7... | collective-permute-start | bytes 332 | tf_op jit(solution)/shard_map/ppermute | solution.py:33
  181.9 3.1 %collective-permute-start.31 = (f32[1,3,9,1]{3,1,2,0:T(4,128)S(1)}, f32[1,3,9,1]{3,1,2,0:T(4,128)S(1)}, u32[]{:S(2)}, u32[]{:S(2)}) collective-permute-start(f32[1,3,9,1]{3,1,2,0:T(4,128)S(1)} %get-tuple-element.344), channel_id=1, source_target_pairs={{256,0},{512,256},{768,512},{0,768},{257,1},{513,257},{769,513},{1... | collective-permute-start | bytes 332 | tf_op jit(solution)/shard_map/ppermute | solution.py:35
  185.0 3.7 %collective-permute-done.31 = f32[1,3,9,1]{3,1,2,0:T(4,128)S(1)} collective-permute-done((f32[1,3,9,1]{3,1,2,0:T(4,128)S(1)}, f32[1,3,9,1]{3,1,2,0:T(4,128)S(1)}, u32[]{:S(2)}, u32[]{:S(2)}) %collective-permute-start.31) | collective-permute-done | bytes 140 | tf_op jit(solution)/shard_map/ppermute | solution.py:35
  188.8 3.0 %collective-permute-start.33 = (f32[1,3,1,67]{3,0,2,1:T(1,128)S(1)}, f32[1,3,1,67]{3,0,2,1:T(1,128)S(1)}, u32[]{:S(2)}, u32[]{:S(2)}) collective-permute-start(f32[1,3,1,67]{3,0,2,1:T(1,128)S(1)} %get-tuple-element.305), channel_id=1, source_target_pairs={{32,0},{64,32},{96,64},{128,96},{160,128},{192,160},{224,192},{0,2... | collective-permute-start | bytes 2420 | tf_op jit(solution)/shard_map/ppermute | solution.py:35
  191.8 1.3 collective-permute-done.32
  193.3 2.7 %collective-permute-start.35 = (f32[1,1,11,67]{3,1,2,0:T(1,128)S(1)}, f32[1,1,11,67]{3,1,2,0:T(1,128)S(1)}, u32[]{:S(2)}, u32[]{:S(2)}) collective-permute-start(f32[1,1,11,67]{3,1,2,0:T(1,128)S(1)} %copy.841), channel_id=1, source_target_pairs={{1,0},{2,1},{3,2},{4,3},{5,4},{6,5},{7,6},{8,7},{9,8},{10,9},{11,1... | collective-permute-start | bytes 8852 | tf_op jit(solution)/shard_map/ppermute | solution.py:35
  196.0 3.1 %collective-permute-start.34 = (f32[1,1,11,67]{3,1,2,0:T(1,128)S(1)}, f32[1,1,11,67]{3,1,2,0:T(1,128)S(1)}, u32[]{:S(2)}, u32[]{:S(2)}) collective-permute-start(f32[1,1,11,67]{3,1,2,0:T(1,128)S(1)} %copy.842), channel_id=1, source_target_pairs={{0,1},{1,2},{2,3},{3,4},{4,5},{5,6},{6,7},{7,8},{8,9},{9,10},{10,1... | collective-permute-start | bytes 8852 | tf_op jit(solution)/shard_map/ppermute | solution.py:33
  199.1 3.6 %collective-permute-done.34 = f32[1,1,11,67]{3,1,2,0:T(1,128)S(1)} collective-permute-done((f32[1,1,11,67]{3,1,2,0:T(1,128)S(1)}, f32[1,1,11,67]{3,1,2,0:T(1,128)S(1)}, u32[]{:S(2)}, u32[]{:S(2)}) %collective-permute-start.34) | collective-permute-done | bytes 2980 | tf_op jit(solution)/shard_map/ppermute | solution.py:33
  205.2 0.7 slice_add_fusion.4
  (454 shorter events, 27.6 us)
Async XLA Ops:
  0.0 0.7 copy-start.10
  0.0 0.7 copy-start.6
  1.9 0.8 copy-start.2
  2.8 0.7 copy-start.3
  4.8 18.2 %collective-permute-start.1 = (f32[3,5,17,3]{3,0,2,1:T(4,128)S(1)}, f32[3,5,17,3]{3,0,2,1:T(4,128)S(1)}, u32[]{:S(2)}, u32[]{:S(2)}) collective-permute-start(f32[3,5,17,3]{3,0,2,1:T(4,128)S(1)} %get-tuple-element.58), channel_id=1, source_target_pairs={{256,0},{512,256},{768,512},{0,768},{257,1},{513,257},{769,513},{1... | collective-permute-start | bytes 9188 | tf_op jit(solution)/shard_map/ppermute | solution.py:252
  7.4 17.0 %collective-permute-start = (f32[3,5,17,3]{3,0,2,1:T(4,128)S(1)}, f32[3,5,17,3]{3,0,2,1:T(4,128)S(1)}, u32[]{:S(2)}, u32[]{:S(2)}) collective-permute-start(f32[3,5,17,3]{3,0,2,1:T(4,128)S(1)} %get-tuple-element.59), channel_id=1, source_target_pairs={{0,256},{256,512},{512,768},{768,0},{1,257},{257,513},{513,769},{7... | collective-permute-start | bytes 9188 | tf_op jit(solution)/shard_map/ppermute | solution.py:251
  21.6 0.7 copy-start.9
  26.9 4.9 %collective-permute-start.2 = (f32[3,5,3,133]{3,2,1,0:T(4,128)S(1)}, f32[3,5,3,133]{3,2,1,0:T(4,128)S(1)}, u32[]{:S(2)}, u32[]{:S(2)}) collective-permute-start(f32[3,5,3,133]{3,2,1,0:T(4,128)S(1)} %copy.790), channel_id=1, source_target_pairs={{0,32},{32,64},{64,96},{96,128},{128,160},{160,192},{192,224},{224... | collective-permute-start | bytes 71828 | tf_op jit(solution)/shard_map/ppermute | solution.py:251
  27.1 5.3 %collective-permute-start.3 = (f32[3,5,3,133]{3,2,1,0:T(4,128)S(1)}, f32[3,5,3,133]{3,2,1,0:T(4,128)S(1)}, u32[]{:S(2)}, u32[]{:S(2)}) collective-permute-start(f32[3,5,3,133]{3,2,1,0:T(4,128)S(1)} %copy.793), channel_id=1, source_target_pairs={{32,0},{64,32},{96,64},{128,96},{160,128},{192,160},{224,192},{0,2... | collective-permute-start | bytes 71828 | tf_op jit(solution)/shard_map/ppermute | solution.py:252
  31.8 0.6 copy-start.5
  32.4 0.8 slice-start.1
  33.6 15.0 %collective-permute-start.4 = (f32[3,3,21,133]{3,2,1,0:T(8,128)S(1)}, f32[3,3,21,133]{3,2,1,0:T(8,128)S(1)}, u32[]{:S(2)}, u32[]{:S(2)}) collective-permute-start(f32[3,3,21,133]{3,2,1,0:T(8,128)S(1)} %slice.1756), channel_id=1, source_target_pairs={{0,1},{1,2},{2,3},{3,4},{4,5},{5,6},{6,7},{7,8},{8,9},{9,10},{10,1... | collective-permute-start | bytes 301652 | tf_op jit(solution)/shard_map/ppermute | solution.py:251
  48.7 8.6 %collective-permute-start.5 = (f32[3,3,21,133]{3,2,1,0:T(8,128)S(1)}, f32[3,3,21,133]{3,2,1,0:T(8,128)S(1)}, u32[]{:S(2)}, u32[]{:S(2)}) collective-permute-start(f32[3,3,21,133]{3,2,1,0:T(8,128)S(1)} %get-tuple-element.51), channel_id=1, source_target_pairs={{1,0},{2,1},{3,2},{4,3},{5,4},{6,5},{7,6},{8,7},{9,8},{10,9},{11,1... | collective-permute-start | bytes 301652 | tf_op jit(solution)/shard_map/ppermute | solution.py:252
  57.3 0.9 copy-start.13
  64.2 0.9 copy-start.4
  67.5 7.7 %collective-permute-start.6 = (f32[1,5,17,1]{3,2,1,0:T(8,128)S(1)}, f32[1,5,17,1]{3,2,1,0:T(8,128)S(1)}, u32[]{:S(2)}, u32[]{:S(2)}) collective-permute-start(f32[1,5,17,1]{3,2,1,0:T(8,128)S(1)} %get-tuple-element.164), channel_id=1, source_target_pairs={{0,256},{256,512},{512,768},{768,0},{1,257},{257,513},{513,769},{7... | collective-permute-start | bytes 1028 | tf_op jit(solution)/shard_map/ppermute | solution.py:33
  73.2 7.3 %collective-permute-start.7 = (f32[1,5,17,1]{3,2,1,0:T(8,128)S(1)}, f32[1,5,17,1]{3,2,1,0:T(8,128)S(1)}, u32[]{:S(2)}, u32[]{:S(2)}) collective-permute-start(f32[1,5,17,1]{3,2,1,0:T(8,128)S(1)} %get-tuple-element.165), channel_id=1, source_target_pairs={{256,0},{512,256},{768,512},{0,768},{257,1},{513,257},{769,513},{1... | collective-permute-start | bytes 1028 | tf_op jit(solution)/shard_map/ppermute | solution.py:35
  80.6 4.3 %collective-permute-start.8 = (f32[1,5,1,131]{3,0,2,1:T(1,128)S(1)}, f32[1,5,1,131]{3,0,2,1:T(1,128)S(1)}, u32[]{:S(2)}, u32[]{:S(2)}) collective-permute-start(f32[1,5,1,131]{3,0,2,1:T(1,128)S(1)} %get-tuple-element.146), channel_id=1, source_target_pairs={{0,32},{32,64},{64,96},{96,128},{128,160},{160,192},{192,224},{224... | collective-permute-start | bytes 7868 | tf_op jit(solution)/shard_map/ppermute | solution.py:33
  80.7 4.3 %collective-permute-start.9 = (f32[1,5,1,131]{3,0,2,1:T(1,128)S(1)}, f32[1,5,1,131]{3,0,2,1:T(1,128)S(1)}, u32[]{:S(2)}, u32[]{:S(2)}) collective-permute-start(f32[1,5,1,131]{3,0,2,1:T(1,128)S(1)} %get-tuple-element.147), channel_id=1, source_target_pairs={{32,0},{64,32},{96,64},{128,96},{160,128},{192,160},{224,192},{0,2... | collective-permute-start | bytes 7868 | tf_op jit(solution)/shard_map/ppermute | solution.py:35
  85.3 6.8 %collective-permute-start.11 = (f32[1,1,19,131]{3,2,1,0:T(8,128)S(1)}, f32[1,1,19,131]{3,2,1,0:T(8,128)S(1)}, u32[]{:S(2)}, u32[]{:S(2)}) collective-permute-start(f32[1,1,19,131]{3,2,1,0:T(8,128)S(1)} %copy.833), channel_id=1, source_target_pairs={{1,0},{2,1},{3,2},{4,3},{5,4},{6,5},{7,6},{8,7},{9,8},{10,9},{11,1... | collective-permute-start | bytes 29876 | tf_op jit(solution)/shard_map/ppermute | solution.py:35
  89.9 7.0 %collective-permute-start.10 = (f32[1,1,19,131]{3,2,1,0:T(8,128)S(1)}, f32[1,1,19,131]{3,2,1,0:T(8,128)S(1)}, u32[]{:S(2)}, u32[]{:S(2)}) collective-permute-start(f32[1,1,19,131]{3,2,1,0:T(8,128)S(1)} %copy.834), channel_id=1, source_target_pairs={{0,1},{1,2},{2,3},{3,4},{4,5},{5,6},{6,7},{7,8},{8,9},{9,10},{10,1... | collective-permute-start | bytes 29876 | tf_op jit(solution)/shard_map/ppermute | solution.py:33
  96.9 0.7 copy-start.12
  97.6 0.7 copy-start.11
  101.1 0.7 copy-start
  102.3 0.7 slice-start
  103.3 5.9 %collective-permute-start.12 = (f32[2,3,9,1]{3,0,2,1:T(2,128)S(1)}, f32[2,3,9,1]{3,0,2,1:T(2,128)S(1)}, u32[]{:S(2)}, u32[]{:S(2)}) collective-permute-start(f32[2,3,9,1]{3,0,2,1:T(2,128)S(1)} %get-tuple-element.324), channel_id=1, source_target_pairs={{0,256},{256,512},{512,768},{768,0},{1,257},{257,513},{513,769},{7... | collective-permute-start | bytes 656 | tf_op jit(solution)/shard_map/ppermute | solution.py:33
  105.2 7.0 %collective-permute-start.13 = (f32[2,3,9,1]{3,0,2,1:T(2,128)S(1)}, f32[2,3,9,1]{3,0,2,1:T(2,128)S(1)}, u32[]{:S(2)}, u32[]{:S(2)}) collective-permute-start(f32[2,3,9,1]{3,0,2,1:T(2,128)S(1)} %get-tuple-element.325), channel_id=1, source_target_pairs={{256,0},{512,256},{768,512},{0,768},{257,1},{513,257},{769,513},{1... | collective-permute-start | bytes 656 | tf_op jit(solution)/shard_map/ppermute | solution.py:35
  112.3 4.2 %collective-permute-start.14 = (f32[2,3,1,67]{3,0,2,1:T(2,128)S(1)}, f32[2,3,1,67]{3,0,2,1:T(2,128)S(1)}, u32[]{:S(2)}, u32[]{:S(2)}) collective-permute-start(f32[2,3,1,67]{3,0,2,1:T(2,128)S(1)} %get-tuple-element.171), channel_id=1, source_target_pairs={{0,32},{32,64},{64,96},{96,128},{128,160},{160,192},{192,224},{224... | collective-permute-start | bytes 4832 | tf_op jit(solution)/shard_map/ppermute | solution.py:33
  112.3 4.3 %collective-permute-start.15 = (f32[2,3,1,67]{3,0,2,1:T(2,128)S(1)}, f32[2,3,1,67]{3,0,2,1:T(2,128)S(1)}, u32[]{:S(2)}, u32[]{:S(2)}) collective-permute-start(f32[2,3,1,67]{3,0,2,1:T(2,128)S(1)} %get-tuple-element.172), channel_id=1, source_target_pairs={{32,0},{64,32},{96,64},{128,96},{160,128},{192,160},{224,192},{0,2... | collective-permute-start | bytes 4832 | tf_op jit(solution)/shard_map/ppermute | solution.py:35
  116.8 5.9 %collective-permute-start.17 = (f32[2,1,11,67]{3,1,2,0:T(1,128)S(1)}, f32[2,1,11,67]{3,1,2,0:T(1,128)S(1)}, u32[]{:S(2)}, u32[]{:S(2)}) collective-permute-start(f32[2,1,11,67]{3,1,2,0:T(1,128)S(1)} %copy.835), channel_id=1, source_target_pairs={{1,0},{2,1},{3,2},{4,3},{5,4},{6,5},{7,6},{8,7},{9,8},{10,9},{11,1... | collective-permute-start | bytes 17696 | tf_op jit(solution)/shard_map/ppermute | solution.py:35
  118.7 6.8 %collective-permute-start.16 = (f32[2,1,11,67]{3,1,2,0:T(1,128)S(1)}, f32[2,1,11,67]{3,1,2,0:T(1,128)S(1)}, u32[]{:S(2)}, u32[]{:S(2)}) collective-permute-start(f32[2,1,11,67]{3,1,2,0:T(1,128)S(1)} %copy.836), channel_id=1, source_target_pairs={{0,1},{1,2},{2,3},{3,4},{4,5},{5,6},{6,7},{7,8},{8,9},{9,10},{10,1... | collective-permute-start | bytes 17696 | tf_op jit(solution)/shard_map/ppermute | solution.py:33
  125.5 0.7 copy-start.8
  126.3 0.7 copy-start.7
  127.0 0.8 copy-start.1
  129.8 5.9 %collective-permute-start.18 = (f32[1,3,9,1]{3,1,2,0:T(4,128)S(1)}, f32[1,3,9,1]{3,1,2,0:T(4,128)S(1)}, u32[]{:S(2)}, u32[]{:S(2)}) collective-permute-start(f32[1,3,9,1]{3,1,2,0:T(4,128)S(1)} %get-tuple-element.347), channel_id=1, source_target_pairs={{0,256},{256,512},{512,768},{768,0},{1,257},{257,513},{513,769},{7... | collective-permute-start | bytes 332 | tf_op jit(solution)/shard_map/ppermute | solution.py:33
  131.7 6.9 %collective-permute-start.19 = (f32[1,3,9,1]{3,1,2,0:T(4,128)S(1)}, f32[1,3,9,1]{3,1,2,0:T(4,128)S(1)}, u32[]{:S(2)}, u32[]{:S(2)}) collective-permute-start(f32[1,3,9,1]{3,1,2,0:T(4,128)S(1)} %get-tuple-element.348), channel_id=1, source_target_pairs={{256,0},{512,256},{768,512},{0,768},{257,1},{513,257},{769,513},{1... | collective-permute-start | bytes 332 | tf_op jit(solution)/shard_map/ppermute | solution.py:35
  138.6 4.2 %collective-permute-start.20 = (f32[1,3,1,67]{3,0,2,1:T(1,128)S(1)}, f32[1,3,1,67]{3,0,2,1:T(1,128)S(1)}, u32[]{:S(2)}, u32[]{:S(2)}) collective-permute-start(f32[1,3,1,67]{3,0,2,1:T(1,128)S(1)} %get-tuple-element.308), channel_id=1, source_target_pairs={{0,32},{32,64},{64,96},{96,128},{128,160},{160,192},{192,224},{224... | collective-permute-start | bytes 2420 | tf_op jit(solution)/shard_map/ppermute | solution.py:33
  138.7 4.3 %collective-permute-start.21 = (f32[1,3,1,67]{3,0,2,1:T(1,128)S(1)}, f32[1,3,1,67]{3,0,2,1:T(1,128)S(1)}, u32[]{:S(2)}, u32[]{:S(2)}) collective-permute-start(f32[1,3,1,67]{3,0,2,1:T(1,128)S(1)} %get-tuple-element.309), channel_id=1, source_target_pairs={{32,0},{64,32},{96,64},{128,96},{160,128},{192,160},{224,192},{0,2... | collective-permute-start | bytes 2420 | tf_op jit(solution)/shard_map/ppermute | solution.py:35
  143.1 5.9 %collective-permute-start.23 = (f32[1,1,11,67]{3,1,2,0:T(1,128)S(1)}, f32[1,1,11,67]{3,1,2,0:T(1,128)S(1)}, u32[]{:S(2)}, u32[]{:S(2)}) collective-permute-start(f32[1,1,11,67]{3,1,2,0:T(1,128)S(1)} %copy.837), channel_id=1, source_target_pairs={{1,0},{2,1},{3,2},{4,3},{5,4},{6,5},{7,6},{8,7},{9,8},{10,9},{11,1... | collective-permute-start | bytes 8852 | tf_op jit(solution)/shard_map/ppermute | solution.py:35
  145.0 6.7 %collective-permute-start.22 = (f32[1,1,11,67]{3,1,2,0:T(1,128)S(1)}, f32[1,1,11,67]{3,1,2,0:T(1,128)S(1)}, u32[]{:S(2)}, u32[]{:S(2)}) collective-permute-start(f32[1,1,11,67]{3,1,2,0:T(1,128)S(1)} %copy.838), channel_id=1, source_target_pairs={{0,1},{1,2},{2,3},{3,4},{4,5},{5,6},{6,7},{7,8},{8,9},{9,10},{10,1... | collective-permute-start | bytes 8852 | tf_op jit(solution)/shard_map/ppermute | solution.py:33
  154.0 5.9 %collective-permute-start.24 = (f32[1,3,9,1]{3,1,2,0:T(4,128)S(1)}, f32[1,3,9,1]{3,1,2,0:T(4,128)S(1)}, u32[]{:S(2)}, u32[]{:S(2)}) collective-permute-start(f32[1,3,9,1]{3,1,2,0:T(4,128)S(1)} %get-tuple-element.345), channel_id=1, source_target_pairs={{0,256},{256,512},{512,768},{768,0},{1,257},{257,513},{513,769},{7... | collective-permute-start | bytes 332 | tf_op jit(solution)/shard_map/ppermute | solution.py:33
  156.1 6.9 %collective-permute-start.25 = (f32[1,3,9,1]{3,1,2,0:T(4,128)S(1)}, f32[1,3,9,1]{3,1,2,0:T(4,128)S(1)}, u32[]{:S(2)}, u32[]{:S(2)}) collective-permute-start(f32[1,3,9,1]{3,1,2,0:T(4,128)S(1)} %get-tuple-element.346), channel_id=1, source_target_pairs={{256,0},{512,256},{768,512},{0,768},{257,1},{513,257},{769,513},{1... | collective-permute-start | bytes 332 | tf_op jit(solution)/shard_map/ppermute | solution.py:35
  163.0 4.2 %collective-permute-start.26 = (f32[1,3,1,67]{3,0,2,1:T(1,128)S(1)}, f32[1,3,1,67]{3,0,2,1:T(1,128)S(1)}, u32[]{:S(2)}, u32[]{:S(2)}) collective-permute-start(f32[1,3,1,67]{3,0,2,1:T(1,128)S(1)} %get-tuple-element.306), channel_id=1, source_target_pairs={{0,32},{32,64},{64,96},{96,128},{128,160},{160,192},{192,224},{224... | collective-permute-start | bytes 2420 | tf_op jit(solution)/shard_map/ppermute | solution.py:33
  163.1 4.3 %collective-permute-start.27 = (f32[1,3,1,67]{3,0,2,1:T(1,128)S(1)}, f32[1,3,1,67]{3,0,2,1:T(1,128)S(1)}, u32[]{:S(2)}, u32[]{:S(2)}) collective-permute-start(f32[1,3,1,67]{3,0,2,1:T(1,128)S(1)} %get-tuple-element.307), channel_id=1, source_target_pairs={{32,0},{64,32},{96,64},{128,96},{160,128},{192,160},{224,192},{0,2... | collective-permute-start | bytes 2420 | tf_op jit(solution)/shard_map/ppermute | solution.py:35
  167.5 5.9 %collective-permute-start.29 = (f32[1,1,11,67]{3,1,2,0:T(1,128)S(1)}, f32[1,1,11,67]{3,1,2,0:T(1,128)S(1)}, u32[]{:S(2)}, u32[]{:S(2)}) collective-permute-start(f32[1,1,11,67]{3,1,2,0:T(1,128)S(1)} %copy.839), channel_id=1, source_target_pairs={{1,0},{2,1},{3,2},{4,3},{5,4},{6,5},{7,6},{8,7},{9,8},{10,9},{11,1... | collective-permute-start | bytes 8852 | tf_op jit(solution)/shard_map/ppermute | solution.py:35
  170.2 6.7 %collective-permute-start.28 = (f32[1,1,11,67]{3,1,2,0:T(1,128)S(1)}, f32[1,1,11,67]{3,1,2,0:T(1,128)S(1)}, u32[]{:S(2)}, u32[]{:S(2)}) collective-permute-start(f32[1,1,11,67]{3,1,2,0:T(1,128)S(1)} %copy.840), channel_id=1, source_target_pairs={{0,1},{1,2},{2,3},{3,4},{4,5},{5,6},{6,7},{7,8},{8,9},{9,10},{10,1... | collective-permute-start | bytes 8852 | tf_op jit(solution)/shard_map/ppermute | solution.py:33
  179.1 5.9 %collective-permute-start.30 = (f32[1,3,9,1]{3,1,2,0:T(4,128)S(1)}, f32[1,3,9,1]{3,1,2,0:T(4,128)S(1)}, u32[]{:S(2)}, u32[]{:S(2)}) collective-permute-start(f32[1,3,9,1]{3,1,2,0:T(4,128)S(1)} %get-tuple-element.343), channel_id=1, source_target_pairs={{0,256},{256,512},{512,768},{768,0},{1,257},{257,513},{513,769},{7... | collective-permute-start | bytes 332 | tf_op jit(solution)/shard_map/ppermute | solution.py:33
  181.9 6.9 %collective-permute-start.31 = (f32[1,3,9,1]{3,1,2,0:T(4,128)S(1)}, f32[1,3,9,1]{3,1,2,0:T(4,128)S(1)}, u32[]{:S(2)}, u32[]{:S(2)}) collective-permute-start(f32[1,3,9,1]{3,1,2,0:T(4,128)S(1)} %get-tuple-element.344), channel_id=1, source_target_pairs={{256,0},{512,256},{768,512},{0,768},{257,1},{513,257},{769,513},{1... | collective-permute-start | bytes 332 | tf_op jit(solution)/shard_map/ppermute | solution.py:35
  188.8 4.2 %collective-permute-start.32 = (f32[1,3,1,67]{3,0,2,1:T(1,128)S(1)}, f32[1,3,1,67]{3,0,2,1:T(1,128)S(1)}, u32[]{:S(2)}, u32[]{:S(2)}) collective-permute-start(f32[1,3,1,67]{3,0,2,1:T(1,128)S(1)} %get-tuple-element.304), channel_id=1, source_target_pairs={{0,32},{32,64},{64,96},{96,128},{128,160},{160,192},{192,224},{224... | collective-permute-start | bytes 2420 | tf_op jit(solution)/shard_map/ppermute | solution.py:33
  188.8 4.3 %collective-permute-start.33 = (f32[1,3,1,67]{3,0,2,1:T(1,128)S(1)}, f32[1,3,1,67]{3,0,2,1:T(1,128)S(1)}, u32[]{:S(2)}, u32[]{:S(2)}) collective-permute-start(f32[1,3,1,67]{3,0,2,1:T(1,128)S(1)} %get-tuple-element.305), channel_id=1, source_target_pairs={{32,0},{64,32},{96,64},{128,96},{160,128},{192,160},{224,192},{0,2... | collective-permute-start | bytes 2420 | tf_op jit(solution)/shard_map/ppermute | solution.py:35
  193.3 5.9 %collective-permute-start.35 = (f32[1,1,11,67]{3,1,2,0:T(1,128)S(1)}, f32[1,1,11,67]{3,1,2,0:T(1,128)S(1)}, u32[]{:S(2)}, u32[]{:S(2)}) collective-permute-start(f32[1,1,11,67]{3,1,2,0:T(1,128)S(1)} %copy.841), channel_id=1, source_target_pairs={{1,0},{2,1},{3,2},{4,3},{5,4},{6,5},{7,6},{8,7},{9,8},{10,9},{11,1... | collective-permute-start | bytes 8852 | tf_op jit(solution)/shard_map/ppermute | solution.py:35
  196.0 6.7 %collective-permute-start.34 = (f32[1,1,11,67]{3,1,2,0:T(1,128)S(1)}, f32[1,1,11,67]{3,1,2,0:T(1,128)S(1)}, u32[]{:S(2)}, u32[]{:S(2)}) collective-permute-start(f32[1,1,11,67]{3,1,2,0:T(1,128)S(1)} %copy.842), channel_id=1, source_target_pairs={{0,1},{1,2},{2,3},{3,4},{4,5},{5,6},{6,7},{7,8},{8,9},{9,10},{10,1... | collective-permute-start | bytes 8852 | tf_op jit(solution)/shard_map/ppermute | solution.py:33

commit v3 on v1

--- a/solution.py
+++ b/solution.py
@@ -64,8 +64,18 @@
 def spread(node_field):
     length_x = node_field.shape[2]
     elements_x = (length_x - 1) // 2
-    even_x = lax.slice_in_dim(node_field, 0, length_x, 2, axis=2)
-    odd_x = lax.slice_in_dim(node_field, 1, length_x, 2, axis=2)
+    if node_field.shape[0] * node_field.shape[1] > 128:
+        order = np.concatenate([np.arange(0, length_x, 2), np.arange(1, length_x, 2)])
+        chooser = np.zeros((length_x, length_x), np.float32)
+        chooser[order, np.arange(length_x)] = 1.0
+        sorted_x = jnp.einsum(
+            "zyx,xk->zyk", node_field, jnp.asarray(chooser), precision=lax.Precision.HIGHEST
+        )
+        even_x = lax.slice_in_dim(sorted_x, 0, elements_x + 1, axis=2)
+        odd_x = lax.slice_in_dim(sorted_x, elements_x + 1, length_x, axis=2)
+    else:
+        even_x = lax.slice_in_dim(node_field, 0, length_x, 2, axis=2)
+        odd_x = lax.slice_in_dim(node_field, 1, length_x, 2, axis=2)
     along_x = jnp.stack(
         [
             lax.slice_in_dim(even_x, 0, elements_x, axis=2),

time: 202 us -> 199 us (0.985)
  local copies, waits for them, and re-layouts: 26.5 us -> 23 us
    slice x6 -> x5, local copies, waits for them, and re-layouts: 4.05 us -> 2.29 us  [spread(): even_x = lax.slice_in_dim(node_field, 0, length_x, 2, axis=2)]
    unnamed x24 -> x26, local copies, waits for them, and re-layouts: 5.25 us -> 5.26 us
where the time goes in v3:
time: 199 us; the launch traced here: 198 us
  starting transfers between devices  105 us (53%)
  waiting for transfers between devices  54 us (27%)
  local copies, waits for them, and re-layouts  23 us (12%)
  other arithmetic  13 us (7%)
  between operations  2.58 us (1%)
    ppermute x15, starting transfers between devices, padded(): lax.ppermute(head, axis, [((i + 1) % count, i) for i in range(count)])  58.3 us
    ppermute x15, waiting for transfers between devices, padded(): lax.ppermute(head, axis, [((i + 1) % count, i) for i in range(count)])  25.3 us
    ppermute x15, starting transfers between devices, padded(): lax.ppermute(tail, axis, [(i, (i + 1) % count) for i in range(count)])  23.9 us
    ppermute x3, waiting for transfers between devices, widened(): lax.ppermute(tail, axis, [(i, (i + 1) % count) for i in range(count)])  17 us
    ppermute x3, starting transfers between devices, widened(): lax.ppermute(tail, axis, [(i, (i + 1) % count) for i in range(count)])  16.4 us
    ppermute x3, starting transfers between devices, widened(): lax.ppermute(head, axis, [((i + 1) % count, i) for i in range(count)])  6.59 us
    ppermute x15, waiting for transfers between devices, padded(): lax.ppermute(tail, axis, [(i, (i + 1) % count) for i in range(count)])  6.21 us
    ppermute x3, waiting for transfers between devices, widened(): lax.ppermute(head, axis, [((i + 1) % count, i) for i in range(count)])  5.47 us
  transfers between devices with their start and end apart: 36, of which 22 were waited for; matrix products, arithmetic and copies ran while one was open for 1% of the time, Pallas kernels for 0%

profile of v3, /device:TPU:24, one launch (start us, length us, event | category | flops | bytes accessed | tf_op | source)
XLA Modules:
  0.0 198.1 jit_solution(13067369794472022653)
XLA Ops:
  0.0 0.7 copy-done.8
  0.7 0.8 multiply_add_fusion.24
  2.0 0.6 copy-done.2
  3.3 0.7 copy-done.1
  4.1 2.7 %collective-permute-start.1 = (f32[3,5,17,3]{3,2,1,0:T(8,128)S(1)}, f32[3,5,17,3]{3,2,1,0:T(8,128)S(1)}, u32[]{:S(2)}, u32[]{:S(2)}) collective-permute-start(f32[3,5,17,3]{3,2,1,0:T(8,128)S(1)} %get-tuple-element.58), channel_id=1, source_target_pairs={{256,0},{512,256},{768,512},{0,768},{257,1},{513,257},{769,513},{1... | collective-permute-start | bytes 9188 | tf_op jit(solution)/shard_map/ppermute | solution.py:256
  6.8 14.0 %collective-permute-start = (f32[3,5,17,3]{3,2,1,0:T(8,128)S(1)}, f32[3,5,17,3]{3,2,1,0:T(8,128)S(1)}, u32[]{:S(2)}, u32[]{:S(2)}) collective-permute-start(f32[3,5,17,3]{3,2,1,0:T(8,128)S(1)} %get-tuple-element.59), channel_id=1, source_target_pairs={{0,256},{256,512},{512,768},{768,0},{1,257},{257,513},{513,769},{7... | collective-permute-start | bytes 9188 | tf_op jit(solution)/shard_map/ppermute | solution.py:255
  22.5 1.3 collective-permute-done
  24.9 1.3 collective-permute-done.3
  26.2 3.0 %collective-permute-done.2 = f32[3,5,3,133]{3,2,1,0:T(4,128)S(1)} collective-permute-done((f32[3,5,3,133]{3,2,1,0:T(4,128)S(1)}, f32[3,5,3,133]{3,2,1,0:T(4,128)S(1)}, u32[]{:S(2)}, u32[]{:S(2)}) %collective-permute-start.2) | collective-permute-done | bytes 23972 | tf_op jit(solution)/shard_map/ppermute | solution.py:255
  29.7 1.9 collective-permute-start.4
  31.7 12.6 %collective-permute-done.4 = f32[3,3,21,133]{3,2,1,0:T(8,128)S(1)} collective-permute-done((f32[3,3,21,133]{3,2,1,0:T(8,128)S(1)}, f32[3,3,21,133]{3,2,1,0:T(8,128)S(1)}, u32[]{:S(2)}, u32[]{:S(2)}) %collective-permute-start.4) | collective-permute-done | bytes 100580 | tf_op jit(solution)/shard_map/ppermute | solution.py:255
  44.4 3.9 %collective-permute-start.5 = (f32[3,3,21,133]{3,2,1,0:T(8,128)S(1)}, f32[3,3,21,133]{3,2,1,0:T(8,128)S(1)}, u32[]{:S(2)}, u32[]{:S(2)}) collective-permute-start(f32[3,3,21,133]{3,2,1,0:T(8,128)S(1)} %get-tuple-element.51), channel_id=1, source_target_pairs={{1,0},{2,1},{3,2},{4,3},{5,4},{6,5},{7,6},{8,7},{9,8},{10,9},{11,1... | collective-permute-start | bytes 301652 | tf_op jit(solution)/shard_map/ppermute | solution.py:256
  48.4 3.8 %collective-permute-done.5 = f32[3,3,21,133]{3,2,1,0:T(8,128)S(1)} collective-permute-done((f32[3,3,21,133]{3,2,1,0:T(8,128)S(1)}, f32[3,3,21,133]{3,2,1,0:T(8,128)S(1)}, u32[]{:S(2)}, u32[]{:S(2)}) %collective-permute-start.5) | collective-permute-done | bytes 100580 | tf_op jit(solution)/shard_map/ppermute | solution.py:256
  52.3 0.9 slice.1356
  59.4 0.8 slice.1403
  60.3 0.8 slice.1401
  63.2 5.6 %collective-permute-start.6 = (f32[1,5,17,1]{3,2,1,0:T(8,128)S(1)}, f32[1,5,17,1]{3,2,1,0:T(8,128)S(1)}, u32[]{:S(2)}, u32[]{:S(2)}) collective-permute-start(f32[1,5,17,1]{3,2,1,0:T(8,128)S(1)} %get-tuple-element.168), channel_id=1, source_target_pairs={{0,256},{256,512},{512,768},{768,0},{1,257},{257,513},{513,769},{7... | collective-permute-start | bytes 1028 | tf_op jit(solution)/shard_map/ppermute | solution.py:33
  68.8 1.9 collective-permute-start.7
  70.8 5.4 %collective-permute-done.7 = f32[1,5,17,1]{3,2,1,0:T(8,128)S(1)} collective-permute-done((f32[1,5,17,1]{3,2,1,0:T(8,128)S(1)}, f32[1,5,17,1]{3,2,1,0:T(8,128)S(1)}, u32[]{:S(2)}, u32[]{:S(2)}) %collective-permute-start.7) | collective-permute-done | bytes 372 | tf_op jit(solution)/shard_map/ppermute | solution.py:35
  76.3 2.9 %collective-permute-start.9 = (f32[1,5,1,131]{3,2,1,0:T(1,128)S(1)}, f32[1,5,1,131]{3,2,1,0:T(1,128)S(1)}, u32[]{:S(2)}, u32[]{:S(2)}) collective-permute-start(f32[1,5,1,131]{3,2,1,0:T(1,128)S(1)} %get-tuple-element.64), channel_id=1, source_target_pairs={{32,0},{64,32},{96,64},{128,96},{160,128},{192,160},{224,192},{0,2... | collective-permute-start | bytes 7868 | tf_op jit(solution)/shard_map/ppermute | solution.py:35
  79.5 1.0 collective-permute-done.8
  80.7 1.9 collective-permute-start.10
  82.6 5.3 %collective-permute-start.11 = (f32[1,1,19,131]{3,2,1,0:T(8,128)S(1)}, f32[1,1,19,131]{3,2,1,0:T(8,128)S(1)}, u32[]{:S(2)}, u32[]{:S(2)}) collective-permute-start(f32[1,1,19,131]{3,2,1,0:T(8,128)S(1)} %get-tuple-element.167), channel_id=1, source_target_pairs={{1,0},{2,1},{3,2},{4,3},{5,4},{6,5},{7,6},{8,7},{9,8},{10,9},{11,1... | collective-permute-start | bytes 29876 | tf_op jit(solution)/shard_map/ppermute | solution.py:35
  88.0 1.2 collective-permute-done.11
  89.4 0.6 copy-done.10
  90.2 0.6 copy-done.9
  91.0 0.8 slice.1458
  91.8 0.8 slice.1456
  96.3 0.6 slice-done
  97.1 1.9 collective-permute-start.12
  99.0 3.9 %collective-permute-start.13 = (f32[2,3,9,1]{3,2,1,0:T(8,128)S(1)}, f32[2,3,9,1]{3,2,1,0:T(8,128)S(1)}, u32[]{:S(2)}, u32[]{:S(2)}) collective-permute-start(f32[2,3,9,1]{3,2,1,0:T(8,128)S(1)} %get-tuple-element.297), channel_id=1, source_target_pairs={{256,0},{512,256},{768,512},{0,768},{257,1},{513,257},{769,513},{1... | collective-permute-start | bytes 656 | tf_op jit(solution)/shard_map/ppermute | solution.py:35
  103.1 3.1 %collective-permute-done.13 = f32[2,3,9,1]{3,2,1,0:T(8,128)S(1)} collective-permute-done((f32[2,3,9,1]{3,2,1,0:T(8,128)S(1)}, f32[2,3,9,1]{3,2,1,0:T(8,128)S(1)}, u32[]{:S(2)}, u32[]{:S(2)}) %collective-permute-start.13) | collective-permute-done | bytes 248 | tf_op jit(solution)/shard_map/ppermute | solution.py:35
  106.3 2.9 %collective-permute-start.15 = (f32[2,3,1,67]{3,2,1,0:T(1,128)S(1)}, f32[2,3,1,67]{3,2,1,0:T(1,128)S(1)}, u32[]{:S(2)}, u32[]{:S(2)}) collective-permute-start(f32[2,3,1,67]{3,2,1,0:T(1,128)S(1)} %get-tuple-element.152), channel_id=1, source_target_pairs={{32,0},{64,32},{96,64},{128,96},{160,128},{192,160},{224,192},{0,2... | collective-permute-start | bytes 4832 | tf_op jit(solution)/shard_map/ppermute | solution.py:35
  109.3 1.3 collective-permute-done.14
  110.7 1.9 collective-permute-start.16
  112.6 5.4 %collective-permute-start.17 = (f32[2,1,11,67]{3,2,1,0:T(8,128)S(1)}, f32[2,1,11,67]{3,2,1,0:T(8,128)S(1)}, u32[]{:S(2)}, u32[]{:S(2)}) collective-permute-start(f32[2,1,11,67]{3,2,1,0:T(8,128)S(1)} %get-tuple-element.295), channel_id=1, source_target_pairs={{1,0},{2,1},{3,2},{4,3},{5,4},{6,5},{7,6},{8,7},{9,8},{10,9},{11,1... | collective-permute-start | bytes 17696 | tf_op jit(solution)/shard_map/ppermute | solution.py:35
  118.1 1.4 collective-permute-done.17
  119.6 0.6 copy-done.4
  120.4 0.6 copy-done.3
  123.2 1.9 collective-permute-start.18
  125.1 3.9 %collective-permute-start.19 = (f32[1,3,9,1]{3,2,1,0:T(8,128)S(1)}, f32[1,3,9,1]{3,2,1,0:T(8,128)S(1)}, u32[]{:S(2)}, u32[]{:S(2)}) collective-permute-start(f32[1,3,9,1]{3,2,1,0:T(8,128)S(1)} %get-tuple-element.345), channel_id=1, source_target_pairs={{256,0},{512,256},{768,512},{0,768},{257,1},{513,257},{769,513},{1... | collective-permute-start | bytes 332 | tf_op jit(solution)/shard_map/ppermute | solution.py:35
  129.1 3.0 %collective-permute-done.19 = f32[1,3,9,1]{3,2,1,0:T(8,128)S(1)} collective-permute-done((f32[1,3,9,1]{3,2,1,0:T(8,128)S(1)}, f32[1,3,9,1]{3,2,1,0:T(8,128)S(1)}, u32[]{:S(2)}, u32[]{:S(2)}) %collective-permute-start.19) | collective-permute-done | bytes 140 | tf_op jit(solution)/shard_map/ppermute | solution.py:35
  132.1 3.0 %collective-permute-start.21 = (f32[1,3,1,67]{3,2,1,0:T(1,128)S(1)}, f32[1,3,1,67]{3,2,1,0:T(1,128)S(1)}, u32[]{:S(2)}, u32[]{:S(2)}) collective-permute-start(f32[1,3,1,67]{3,2,1,0:T(1,128)S(1)} %get-tuple-element.175), channel_id=1, source_target_pairs={{32,0},{64,32},{96,64},{128,96},{160,128},{192,160},{224,192},{0,2... | collective-permute-start | bytes 2420 | tf_op jit(solution)/shard_map/ppermute | solution.py:35
  135.1 1.3 collective-permute-done.20
  136.5 1.9 collective-permute-start.22
  138.4 5.4 %collective-permute-start.23 = (f32[1,1,11,67]{3,2,1,0:T(8,128)S(1)}, f32[1,1,11,67]{3,2,1,0:T(8,128)S(1)}, u32[]{:S(2)}, u32[]{:S(2)}) collective-permute-start(f32[1,1,11,67]{3,2,1,0:T(8,128)S(1)} %get-tuple-element.343), channel_id=1, source_target_pairs={{1,0},{2,1},{3,2},{4,3},{5,4},{6,5},{7,6},{8,7},{9,8},{10,9},{11,1... | collective-permute-start | bytes 8852 | tf_op jit(solution)/shard_map/ppermute | solution.py:35
  143.8 1.3 collective-permute-done.23
  147.6 2.1 %collective-permute-start.24 = (f32[1,3,9,1]{3,2,1,0:T(8,128)S(1)}, f32[1,3,9,1]{3,2,1,0:T(8,128)S(1)}, u32[]{:S(2)}, u32[]{:S(2)}) collective-permute-start(f32[1,3,9,1]{3,2,1,0:T(8,128)S(1)} %get-tuple-element.338), channel_id=1, source_target_pairs={{0,256},{256,512},{512,768},{768,0},{1,257},{257,513},{513,769},{7... | collective-permute-start | bytes 332 | tf_op jit(solution)/shard_map/ppermute | solution.py:33
  149.8 3.7 %collective-permute-start.25 = (f32[1,3,9,1]{3,2,1,0:T(8,128)S(1)}, f32[1,3,9,1]{3,2,1,0:T(8,128)S(1)}, u32[]{:S(2)}, u32[]{:S(2)}) collective-permute-start(f32[1,3,9,1]{3,2,1,0:T(8,128)S(1)} %get-tuple-element.339), channel_id=1, source_target_pairs={{256,0},{512,256},{768,512},{0,768},{257,1},{513,257},{769,513},{1... | collective-permute-start | bytes 332 | tf_op jit(solution)/shard_map/ppermute | solution.py:35
  153.5 3.2 %collective-permute-done.25 = f32[1,3,9,1]{3,2,1,0:T(8,128)S(1)} collective-permute-done((f32[1,3,9,1]{3,2,1,0:T(8,128)S(1)}, f32[1,3,9,1]{3,2,1,0:T(8,128)S(1)}, u32[]{:S(2)}, u32[]{:S(2)}) %collective-permute-start.25) | collective-permute-done | bytes 140 | tf_op jit(solution)/shard_map/ppermute | solution.py:35
  156.8 3.0 %collective-permute-start.27 = (f32[1,3,1,67]{3,2,1,0:T(1,128)S(1)}, f32[1,3,1,67]{3,2,1,0:T(1,128)S(1)}, u32[]{:S(2)}, u32[]{:S(2)}) collective-permute-start(f32[1,3,1,67]{3,2,1,0:T(1,128)S(1)} %get-tuple-element.173), channel_id=1, source_target_pairs={{32,0},{64,32},{96,64},{128,96},{160,128},{192,160},{224,192},{0,2... | collective-permute-start | bytes 2420 | tf_op jit(solution)/shard_map/ppermute | solution.py:35
  159.7 1.3 collective-permute-done.26
  161.1 1.9 collective-permute-start.28
  163.1 5.4 %collective-permute-start.29 = (f32[1,1,11,67]{3,2,1,0:T(8,128)S(1)}, f32[1,1,11,67]{3,2,1,0:T(8,128)S(1)}, u32[]{:S(2)}, u32[]{:S(2)}) collective-permute-start(f32[1,1,11,67]{3,2,1,0:T(8,128)S(1)} %get-tuple-element.337), channel_id=1, source_target_pairs={{1,0},{2,1},{3,2},{4,3},{5,4},{6,5},{7,6},{8,7},{9,8},{10,9},{11,1... | collective-permute-start | bytes 8852 | tf_op jit(solution)/shard_map/ppermute | solution.py:35
  168.5 1.3 collective-permute-done.29
  172.3 2.7 %collective-permute-start.30 = (f32[1,3,9,1]{3,2,1,0:T(8,128)S(1)}, f32[1,3,9,1]{3,2,1,0:T(8,128)S(1)}, u32[]{:S(2)}, u32[]{:S(2)}) collective-permute-start(f32[1,3,9,1]{3,2,1,0:T(8,128)S(1)} %get-tuple-element.332), channel_id=1, source_target_pairs={{0,256},{256,512},{512,768},{768,0},{1,257},{257,513},{513,769},{7... | collective-permute-start | bytes 332 | tf_op jit(solution)/shard_map/ppermute | solution.py:33
  175.0 3.1 %collective-permute-start.31 = (f32[1,3,9,1]{3,2,1,0:T(8,128)S(1)}, f32[1,3,9,1]{3,2,1,0:T(8,128)S(1)}, u32[]{:S(2)}, u32[]{:S(2)}) collective-permute-start(f32[1,3,9,1]{3,2,1,0:T(8,128)S(1)} %get-tuple-element.333), channel_id=1, source_target_pairs={{256,0},{512,256},{768,512},{0,768},{257,1},{513,257},{769,513},{1... | collective-permute-start | bytes 332 | tf_op jit(solution)/shard_map/ppermute | solution.py:35
  178.1 3.8 %collective-permute-done.31 = f32[1,3,9,1]{3,2,1,0:T(8,128)S(1)} collective-permute-done((f32[1,3,9,1]{3,2,1,0:T(8,128)S(1)}, f32[1,3,9,1]{3,2,1,0:T(8,128)S(1)}, u32[]{:S(2)}, u32[]{:S(2)}) %collective-permute-start.31) | collective-permute-done | bytes 140 | tf_op jit(solution)/shard_map/ppermute | solution.py:35
  182.0 3.0 %collective-permute-start.33 = (f32[1,3,1,67]{3,2,1,0:T(1,128)S(1)}, f32[1,3,1,67]{3,2,1,0:T(1,128)S(1)}, u32[]{:S(2)}, u32[]{:S(2)}) collective-permute-start(f32[1,3,1,67]{3,2,1,0:T(1,128)S(1)} %get-tuple-element.171), channel_id=1, source_target_pairs={{32,0},{64,32},{96,64},{128,96},{160,128},{192,160},{224,192},{0,2... | collective-permute-start | bytes 2420 | tf_op jit(solution)/shard_map/ppermute | solution.py:35
  185.0 1.3 collective-permute-done.32
  186.4 1.9 collective-permute-start.34
  188.3 5.4 %collective-permute-start.35 = (f32[1,1,11,67]{3,2,1,0:T(8,128)S(1)}, f32[1,1,11,67]{3,2,1,0:T(8,128)S(1)}, u32[]{:S(2)}, u32[]{:S(2)}) collective-permute-start(f32[1,1,11,67]{3,2,1,0:T(8,128)S(1)} %get-tuple-element.331), channel_id=1, source_target_pairs={{1,0},{2,1},{3,2},{4,3},{5,4},{6,5},{7,6},{8,7},{9,8},{10,9},{11,1... | collective-permute-start | bytes 8852 | tf_op jit(solution)/shard_map/ppermute | solution.py:35
  193.7 1.3 collective-permute-done.35
  197.5 0.7 slice_add_fusion.4
  (416 shorter events, 26.9 us)
Async XLA Ops:
  0.0 0.7 copy-start.8
  0.0 0.7 copy-start.7
  1.9 0.7 copy-start.2
  3.1 0.8 copy-start.1
  4.1 18.3 %collective-permute-start.1 = (f32[3,5,17,3]{3,2,1,0:T(8,128)S(1)}, f32[3,5,17,3]{3,2,1,0:T(8,128)S(1)}, u32[]{:S(2)}, u32[]{:S(2)}) collective-permute-start(f32[3,5,17,3]{3,2,1,0:T(8,128)S(1)} %get-tuple-element.58), channel_id=1, source_target_pairs={{256,0},{512,256},{768,512},{0,768},{257,1},{513,257},{769,513},{1... | collective-permute-start | bytes 9188 | tf_op jit(solution)/shard_map/ppermute | solution.py:256
  6.8 17.1 %collective-permute-start = (f32[3,5,17,3]{3,2,1,0:T(8,128)S(1)}, f32[3,5,17,3]{3,2,1,0:T(8,128)S(1)}, u32[]{:S(2)}, u32[]{:S(2)}) collective-permute-start(f32[3,5,17,3]{3,2,1,0:T(8,128)S(1)} %get-tuple-element.59), channel_id=1, source_target_pairs={{0,256},{256,512},{512,768},{768,0},{1,257},{257,513},{513,769},{7... | collective-permute-start | bytes 9188 | tf_op jit(solution)/shard_map/ppermute | solution.py:255
  21.0 0.7 copy-start.5
  21.0 0.7 copy-start.6
  24.3 1.9 collective-permute-start.3
  24.4 4.9 %collective-permute-start.2 = (f32[3,5,3,133]{3,2,1,0:T(4,128)S(1)}, f32[3,5,3,133]{3,2,1,0:T(4,128)S(1)}, u32[]{:S(2)}, u32[]{:S(2)}) collective-permute-start(f32[3,5,3,133]{3,2,1,0:T(4,128)S(1)} %get-tuple-element.55), channel_id=1, source_target_pairs={{0,32},{32,64},{64,96},{96,128},{128,160},{160,192},{192,224},{224... | collective-permute-start | bytes 71828 | tf_op jit(solution)/shard_map/ppermute | solution.py:255
  29.7 14.6 %collective-permute-start.4 = (f32[3,3,21,133]{3,2,1,0:T(8,128)S(1)}, f32[3,3,21,133]{3,2,1,0:T(8,128)S(1)}, u32[]{:S(2)}, u32[]{:S(2)}) collective-permute-start(f32[3,3,21,133]{3,2,1,0:T(8,128)S(1)} %slice.1761), channel_id=1, source_target_pairs={{0,1},{1,2},{2,3},{3,4},{4,5},{5,6},{6,7},{7,8},{8,9},{9,10},{10,1... | collective-permute-start | bytes 301652 | tf_op jit(solution)/shard_map/ppermute | solution.py:255
  44.4 7.8 %collective-permute-start.5 = (f32[3,3,21,133]{3,2,1,0:T(8,128)S(1)}, f32[3,3,21,133]{3,2,1,0:T(8,128)S(1)}, u32[]{:S(2)}, u32[]{:S(2)}) collective-permute-start(f32[3,3,21,133]{3,2,1,0:T(8,128)S(1)} %get-tuple-element.51), channel_id=1, source_target_pairs={{1,0},{2,1},{3,2},{4,3},{5,4},{6,5},{7,6},{8,7},{9,8},{10,9},{11,1... | collective-permute-start | bytes 301652 | tf_op jit(solution)/shard_map/ppermute | solution.py:256
  52.2 0.9 copy-start.11
  63.2 7.6 %collective-permute-start.6 = (f32[1,5,17,1]{3,2,1,0:T(8,128)S(1)}, f32[1,5,17,1]{3,2,1,0:T(8,128)S(1)}, u32[]{:S(2)}, u32[]{:S(2)}) collective-permute-start(f32[1,5,17,1]{3,2,1,0:T(8,128)S(1)} %get-tuple-element.168), channel_id=1, source_target_pairs={{0,256},{256,512},{512,768},{768,0},{1,257},{257,513},{513,769},{7... | collective-permute-start | bytes 1028 | tf_op jit(solution)/shard_map/ppermute | solution.py:33
  68.8 7.3 %collective-permute-start.7 = (f32[1,5,17,1]{3,2,1,0:T(8,128)S(1)}, f32[1,5,17,1]{3,2,1,0:T(8,128)S(1)}, u32[]{:S(2)}, u32[]{:S(2)}) collective-permute-start(f32[1,5,17,1]{3,2,1,0:T(8,128)S(1)} %get-tuple-element.169), channel_id=1, source_target_pairs={{256,0},{512,256},{768,512},{0,768},{257,1},{513,257},{769,513},{1... | collective-permute-start | bytes 1028 | tf_op jit(solution)/shard_map/ppermute | solution.py:35
  76.2 4.3 %collective-permute-start.8 = (f32[1,5,1,131]{3,2,1,0:T(1,128)S(1)}, f32[1,5,1,131]{3,2,1,0:T(1,128)S(1)}, u32[]{:S(2)}, u32[]{:S(2)}) collective-permute-start(f32[1,5,1,131]{3,2,1,0:T(1,128)S(1)} %get-tuple-element.63), channel_id=1, source_target_pairs={{0,32},{32,64},{64,96},{96,128},{128,160},{160,192},{192,224},{224... | collective-permute-start | bytes 7868 | tf_op jit(solution)/shard_map/ppermute | solution.py:33
  76.3 4.3 %collective-permute-start.9 = (f32[1,5,1,131]{3,2,1,0:T(1,128)S(1)}, f32[1,5,1,131]{3,2,1,0:T(1,128)S(1)}, u32[]{:S(2)}, u32[]{:S(2)}) collective-permute-start(f32[1,5,1,131]{3,2,1,0:T(1,128)S(1)} %get-tuple-element.64), channel_id=1, source_target_pairs={{32,0},{64,32},{96,64},{128,96},{160,128},{192,160},{224,192},{0,2... | collective-permute-start | bytes 7868 | tf_op jit(solution)/shard_map/ppermute | solution.py:35
  80.7 7.3 %collective-permute-start.10 = (f32[1,1,19,131]{3,2,1,0:T(8,128)S(1)}, f32[1,1,19,131]{3,2,1,0:T(8,128)S(1)}, u32[]{:S(2)}, u32[]{:S(2)}) collective-permute-start(f32[1,1,19,131]{3,2,1,0:T(8,128)S(1)} %get-tuple-element.166), channel_id=1, source_target_pairs={{0,1},{1,2},{2,3},{3,4},{4,5},{5,6},{6,7},{7,8},{8,9},{9,10},{10,1... | collective-permute-start | bytes 29876 | tf_op jit(solution)/shard_map/ppermute | solution.py:33
  82.6 6.6 %collective-permute-start.11 = (f32[1,1,19,131]{3,2,1,0:T(8,128)S(1)}, f32[1,1,19,131]{3,2,1,0:T(8,128)S(1)}, u32[]{:S(2)}, u32[]{:S(2)}) collective-permute-start(f32[1,1,19,131]{3,2,1,0:T(8,128)S(1)} %get-tuple-element.167), channel_id=1, source_target_pairs={{1,0},{2,1},{3,2},{4,3},{5,4},{6,5},{7,6},{8,7},{9,8},{10,9},{11,1... | collective-permute-start | bytes 29876 | tf_op jit(solution)/shard_map/ppermute | solution.py:35
  89.4 0.7 copy-start.10
  90.1 0.7 copy-start.9
  95.0 0.7 copy-start
  96.2 0.7 slice-start
  97.1 6.0 %collective-permute-start.12 = (f32[2,3,9,1]{3,2,1,0:T(8,128)S(1)}, f32[2,3,9,1]{3,2,1,0:T(8,128)S(1)}, u32[]{:S(2)}, u32[]{:S(2)}) collective-permute-start(f32[2,3,9,1]{3,2,1,0:T(8,128)S(1)} %get-tuple-element.296), channel_id=1, source_target_pairs={{0,256},{256,512},{512,768},{768,0},{1,257},{257,513},{513,769},{7... | collective-permute-start | bytes 656 | tf_op jit(solution)/shard_map/ppermute | solution.py:33
  99.0 7.2 %collective-permute-start.13 = (f32[2,3,9,1]{3,2,1,0:T(8,128)S(1)}, f32[2,3,9,1]{3,2,1,0:T(8,128)S(1)}, u32[]{:S(2)}, u32[]{:S(2)}) collective-permute-start(f32[2,3,9,1]{3,2,1,0:T(8,128)S(1)} %get-tuple-element.297), channel_id=1, source_target_pairs={{256,0},{512,256},{768,512},{0,768},{257,1},{513,257},{769,513},{1... | collective-permute-start | bytes 656 | tf_op jit(solution)/shard_map/ppermute | solution.py:35
  106.3 4.2 %collective-permute-start.14 = (f32[2,3,1,67]{3,2,1,0:T(1,128)S(1)}, f32[2,3,1,67]{3,2,1,0:T(1,128)S(1)}, u32[]{:S(2)}, u32[]{:S(2)}) collective-permute-start(f32[2,3,1,67]{3,2,1,0:T(1,128)S(1)} %get-tuple-element.151), channel_id=1, source_target_pairs={{0,32},{32,64},{64,96},{96,128},{128,160},{160,192},{192,224},{224... | collective-permute-start | bytes 4832 | tf_op jit(solution)/shard_map/ppermute | solution.py:33
  106.3 4.3 %collective-permute-start.15 = (f32[2,3,1,67]{3,2,1,0:T(1,128)S(1)}, f32[2,3,1,67]{3,2,1,0:T(1,128)S(1)}, u32[]{:S(2)}, u32[]{:S(2)}) collective-permute-start(f32[2,3,1,67]{3,2,1,0:T(1,128)S(1)} %get-tuple-element.152), channel_id=1, source_target_pairs={{32,0},{64,32},{96,64},{128,96},{160,128},{192,160},{224,192},{0,2... | collective-permute-start | bytes 4832 | tf_op jit(solution)/shard_map/ppermute | solution.py:35
  110.7 7.4 %collective-permute-start.16 = (f32[2,1,11,67]{3,2,1,0:T(8,128)S(1)}, f32[2,1,11,67]{3,2,1,0:T(8,128)S(1)}, u32[]{:S(2)}, u32[]{:S(2)}) collective-permute-start(f32[2,1,11,67]{3,2,1,0:T(8,128)S(1)} %get-tuple-element.294), channel_id=1, source_target_pairs={{0,1},{1,2},{2,3},{3,4},{4,5},{5,6},{6,7},{7,8},{8,9},{9,10},{10,1... | collective-permute-start | bytes 17696 | tf_op jit(solution)/shard_map/ppermute | solution.py:33
  112.6 6.9 %collective-permute-start.17 = (f32[2,1,11,67]{3,2,1,0:T(8,128)S(1)}, f32[2,1,11,67]{3,2,1,0:T(8,128)S(1)}, u32[]{:S(2)}, u32[]{:S(2)}) collective-permute-start(f32[2,1,11,67]{3,2,1,0:T(8,128)S(1)} %get-tuple-element.295), channel_id=1, source_target_pairs={{1,0},{2,1},{3,2},{4,3},{5,4},{6,5},{7,6},{8,7},{9,8},{10,9},{11,1... | collective-permute-start | bytes 17696 | tf_op jit(solution)/shard_map/ppermute | solution.py:35
  119.6 0.7 copy-start.4
  120.3 0.7 copy-start.3
  123.2 5.9 %collective-permute-start.18 = (f32[1,3,9,1]{3,2,1,0:T(8,128)S(1)}, f32[1,3,9,1]{3,2,1,0:T(8,128)S(1)}, u32[]{:S(2)}, u32[]{:S(2)}) collective-permute-start(f32[1,3,9,1]{3,2,1,0:T(8,128)S(1)} %get-tuple-element.344), channel_id=1, source_target_pairs={{0,256},{256,512},{512,768},{768,0},{1,257},{257,513},{513,769},{7... | collective-permute-start | bytes 332 | tf_op jit(solution)/shard_map/ppermute | solution.py:33
  125.1 6.9 %collective-permute-start.19 = (f32[1,3,9,1]{3,2,1,0:T(8,128)S(1)}, f32[1,3,9,1]{3,2,1,0:T(8,128)S(1)}, u32[]{:S(2)}, u32[]{:S(2)}) collective-permute-start(f32[1,3,9,1]{3,2,1,0:T(8,128)S(1)} %get-tuple-element.345), channel_id=1, source_target_pairs={{256,0},{512,256},{768,512},{0,768},{257,1},{513,257},{769,513},{1... | collective-permute-start | bytes 332 | tf_op jit(solution)/shard_map/ppermute | solution.py:35
  132.1 4.2 %collective-permute-start.20 = (f32[1,3,1,67]{3,2,1,0:T(1,128)S(1)}, f32[1,3,1,67]{3,2,1,0:T(1,128)S(1)}, u32[]{:S(2)}, u32[]{:S(2)}) collective-permute-start(f32[1,3,1,67]{3,2,1,0:T(1,128)S(1)} %get-tuple-element.174), channel_id=1, source_target_pairs={{0,32},{32,64},{64,96},{96,128},{128,160},{160,192},{192,224},{224... | collective-permute-start | bytes 2420 | tf_op jit(solution)/shard_map/ppermute | solution.py:33
  132.1 4.3 %collective-permute-start.21 = (f32[1,3,1,67]{3,2,1,0:T(1,128)S(1)}, f32[1,3,1,67]{3,2,1,0:T(1,128)S(1)}, u32[]{:S(2)}, u32[]{:S(2)}) collective-permute-start(f32[1,3,1,67]{3,2,1,0:T(1,128)S(1)} %get-tuple-element.175), channel_id=1, source_target_pairs={{32,0},{64,32},{96,64},{128,96},{160,128},{192,160},{224,192},{0,2... | collective-permute-start | bytes 2420 | tf_op jit(solution)/shard_map/ppermute | solution.py:35
  136.5 7.3 %collective-permute-start.22 = (f32[1,1,11,67]{3,2,1,0:T(8,128)S(1)}, f32[1,1,11,67]{3,2,1,0:T(8,128)S(1)}, u32[]{:S(2)}, u32[]{:S(2)}) collective-permute-start(f32[1,1,11,67]{3,2,1,0:T(8,128)S(1)} %get-tuple-element.342), channel_id=1, source_target_pairs={{0,1},{1,2},{2,3},{3,4},{4,5},{5,6},{6,7},{7,8},{8,9},{9,10},{10,1... | collective-permute-start | bytes 8852 | tf_op jit(solution)/shard_map/ppermute | solution.py:33
  138.4 6.8 %collective-permute-start.23 = (f32[1,1,11,67]{3,2,1,0:T(8,128)S(1)}, f32[1,1,11,67]{3,2,1,0:T(8,128)S(1)}, u32[]{:S(2)}, u32[]{:S(2)}) collective-permute-start(f32[1,1,11,67]{3,2,1,0:T(8,128)S(1)} %get-tuple-element.343), channel_id=1, source_target_pairs={{1,0},{2,1},{3,2},{4,3},{5,4},{6,5},{7,6},{8,7},{9,8},{10,9},{11,1... | collective-permute-start | bytes 8852 | tf_op jit(solution)/shard_map/ppermute | solution.py:35
  147.6 5.9 %collective-permute-start.24 = (f32[1,3,9,1]{3,2,1,0:T(8,128)S(1)}, f32[1,3,9,1]{3,2,1,0:T(8,128)S(1)}, u32[]{:S(2)}, u32[]{:S(2)}) collective-permute-start(f32[1,3,9,1]{3,2,1,0:T(8,128)S(1)} %get-tuple-element.338), channel_id=1, source_target_pairs={{0,256},{256,512},{512,768},{768,0},{1,257},{257,513},{513,769},{7... | collective-permute-start | bytes 332 | tf_op jit(solution)/shard_map/ppermute | solution.py:33
  149.8 6.9 %collective-permute-start.25 = (f32[1,3,9,1]{3,2,1,0:T(8,128)S(1)}, f32[1,3,9,1]{3,2,1,0:T(8,128)S(1)}, u32[]{:S(2)}, u32[]{:S(2)}) collective-permute-start(f32[1,3,9,1]{3,2,1,0:T(8,128)S(1)} %get-tuple-element.339), channel_id=1, source_target_pairs={{256,0},{512,256},{768,512},{0,768},{257,1},{513,257},{769,513},{1... | collective-permute-start | bytes 332 | tf_op jit(solution)/shard_map/ppermute | solution.py:35
  156.8 4.2 %collective-permute-start.26 = (f32[1,3,1,67]{3,2,1,0:T(1,128)S(1)}, f32[1,3,1,67]{3,2,1,0:T(1,128)S(1)}, u32[]{:S(2)}, u32[]{:S(2)}) collective-permute-start(f32[1,3,1,67]{3,2,1,0:T(1,128)S(1)} %get-tuple-element.172), channel_id=1, source_target_pairs={{0,32},{32,64},{64,96},{96,128},{128,160},{160,192},{192,224},{224... | collective-permute-start | bytes 2420 | tf_op jit(solution)/shard_map/ppermute | solution.py:33
  156.8 4.3 %collective-permute-start.27 = (f32[1,3,1,67]{3,2,1,0:T(1,128)S(1)}, f32[1,3,1,67]{3,2,1,0:T(1,128)S(1)}, u32[]{:S(2)}, u32[]{:S(2)}) collective-permute-start(f32[1,3,1,67]{3,2,1,0:T(1,128)S(1)} %get-tuple-element.173), channel_id=1, source_target_pairs={{32,0},{64,32},{96,64},{128,96},{160,128},{192,160},{224,192},{0,2... | collective-permute-start | bytes 2420 | tf_op jit(solution)/shard_map/ppermute | solution.py:35
  161.1 7.3 %collective-permute-start.28 = (f32[1,1,11,67]{3,2,1,0:T(8,128)S(1)}, f32[1,1,11,67]{3,2,1,0:T(8,128)S(1)}, u32[]{:S(2)}, u32[]{:S(2)}) collective-permute-start(f32[1,1,11,67]{3,2,1,0:T(8,128)S(1)} %get-tuple-element.336), channel_id=1, source_target_pairs={{0,1},{1,2},{2,3},{3,4},{4,5},{5,6},{6,7},{7,8},{8,9},{9,10},{10,1... | collective-permute-start | bytes 8852 | tf_op jit(solution)/shard_map/ppermute | solution.py:33
  163.1 6.8 %collective-permute-start.29 = (f32[1,1,11,67]{3,2,1,0:T(8,128)S(1)}, f32[1,1,11,67]{3,2,1,0:T(8,128)S(1)}, u32[]{:S(2)}, u32[]{:S(2)}) collective-permute-start(f32[1,1,11,67]{3,2,1,0:T(8,128)S(1)} %get-tuple-element.337), channel_id=1, source_target_pairs={{1,0},{2,1},{3,2},{4,3},{5,4},{6,5},{7,6},{8,7},{9,8},{10,9},{11,1... | collective-permute-start | bytes 8852 | tf_op jit(solution)/shard_map/ppermute | solution.py:35
  172.3 5.9 %collective-permute-start.30 = (f32[1,3,9,1]{3,2,1,0:T(8,128)S(1)}, f32[1,3,9,1]{3,2,1,0:T(8,128)S(1)}, u32[]{:S(2)}, u32[]{:S(2)}) collective-permute-start(f32[1,3,9,1]{3,2,1,0:T(8,128)S(1)} %get-tuple-element.332), channel_id=1, source_target_pairs={{0,256},{256,512},{512,768},{768,0},{1,257},{257,513},{513,769},{7... | collective-permute-start | bytes 332 | tf_op jit(solution)/shard_map/ppermute | solution.py:33
  175.0 6.9 %collective-permute-start.31 = (f32[1,3,9,1]{3,2,1,0:T(8,128)S(1)}, f32[1,3,9,1]{3,2,1,0:T(8,128)S(1)}, u32[]{:S(2)}, u32[]{:S(2)}) collective-permute-start(f32[1,3,9,1]{3,2,1,0:T(8,128)S(1)} %get-tuple-element.333), channel_id=1, source_target_pairs={{256,0},{512,256},{768,512},{0,768},{257,1},{513,257},{769,513},{1... | collective-permute-start | bytes 332 | tf_op jit(solution)/shard_map/ppermute | solution.py:35
  182.0 4.2 %collective-permute-start.32 = (f32[1,3,1,67]{3,2,1,0:T(1,128)S(1)}, f32[1,3,1,67]{3,2,1,0:T(1,128)S(1)}, u32[]{:S(2)}, u32[]{:S(2)}) collective-permute-start(f32[1,3,1,67]{3,2,1,0:T(1,128)S(1)} %get-tuple-element.170), channel_id=1, source_target_pairs={{0,32},{32,64},{64,96},{96,128},{128,160},{160,192},{192,224},{224... | collective-permute-start | bytes 2420 | tf_op jit(solution)/shard_map/ppermute | solution.py:33
  182.0 4.3 %collective-permute-start.33 = (f32[1,3,1,67]{3,2,1,0:T(1,128)S(1)}, f32[1,3,1,67]{3,2,1,0:T(1,128)S(1)}, u32[]{:S(2)}, u32[]{:S(2)}) collective-permute-start(f32[1,3,1,67]{3,2,1,0:T(1,128)S(1)} %get-tuple-element.171), channel_id=1, source_target_pairs={{32,0},{64,32},{96,64},{128,96},{160,128},{192,160},{224,192},{0,2... | collective-permute-start | bytes 2420 | tf_op jit(solution)/shard_map/ppermute | solution.py:35
  186.4 7.3 %collective-permute-start.34 = (f32[1,1,11,67]{3,2,1,0:T(8,128)S(1)}, f32[1,1,11,67]{3,2,1,0:T(8,128)S(1)}, u32[]{:S(2)}, u32[]{:S(2)}) collective-permute-start(f32[1,1,11,67]{3,2,1,0:T(8,128)S(1)} %get-tuple-element.330), channel_id=1, source_target_pairs={{0,1},{1,2},{2,3},{3,4},{4,5},{5,6},{6,7},{7,8},{8,9},{9,10},{10,1... | collective-permute-start | bytes 8852 | tf_op jit(solution)/shard_map/ppermute | solution.py:33
  188.3 6.8 %collective-permute-start.35 = (f32[1,1,11,67]{3,2,1,0:T(8,128)S(1)}, f32[1,1,11,67]{3,2,1,0:T(8,128)S(1)}, u32[]{:S(2)}, u32[]{:S(2)}) collective-permute-start(f32[1,1,11,67]{3,2,1,0:T(8,128)S(1)} %get-tuple-element.331), channel_id=1, source_target_pairs={{1,0},{2,1},{3,2},{4,3},{5,4},{6,5},{7,6},{8,7},{9,8},{10,9},{11,1... | collective-permute-start | bytes 8852 | tf_op jit(solution)/shard_map/ppermute | solution.py:35

commit v4 on v3

--- a/solution.py
+++ b/solution.py
@@ -284,7 +284,14 @@
     right_side = inner[0]
     diagonal = inner[1]
     cells = conductivity.shape
-    cond_wide = wide[2, : 2 * cells[0] + 3 : 2, : 2 * cells[1] + 3 : 2, : 2 * cells[2] + 3 : 2]
+    wide_x = wide.shape[3]
+    order = np.concatenate([np.arange(0, wide_x, 2), np.arange(1, wide_x, 2)])
+    chooser = np.zeros((wide_x, wide_x), np.float32)
+    chooser[order, np.arange(wide_x)] = 1.0
+    cond_even = jnp.einsum(
+        "zyx,xk->zyk", wide[2], jnp.asarray(chooser), precision=lax.Precision.HIGHEST
+    )
+    cond_wide = cond_even[: 2 * cells[0] + 3 : 2, : 2 * cells[1] + 3 : 2, : cells[2] + 2]
 
     def operate_fine(node_field):
         return faces_fine(apply_local(node_field, conductivity, 1.0, reaction_rate)[None])[0]

time: 199 us -> 200 us (level)
    unnamed x26 -> x24, local copies, waits for them, and re-layouts: 5.26 us -> 6.13 us
where the time goes in v4:
time: 200 us; the launch traced here: 198 us
  starting transfers between devices  105 us (52%)
  waiting for transfers between devices  54 us (27%)
  local copies, waits for them, and re-layouts  23.1 us (12%)
  other arithmetic  12.9 us (6%)
  between operations  2.55 us (1%)
    ppermute x15, starting transfers between devices, padded(): lax.ppermute(head, axis, [((i + 1) % count, i) for i in range(count)])  58.3 us
    ppermute x15, waiting for transfers between devices, padded(): lax.ppermute(head, axis, [((i + 1) % count, i) for i in range(count)])  25.3 us
    ppermute x15, starting transfers between devices, padded(): lax.ppermute(tail, axis, [(i, (i + 1) % count) for i in range(count)])  23.9 us
    ppermute x3, waiting for transfers between devices, widened(): lax.ppermute(tail, axis, [(i, (i + 1) % count) for i in range(count)])  17 us
    ppermute x3, starting transfers between devices, widened(): lax.ppermute(tail, axis, [(i, (i + 1) % count) for i in range(count)])  16.4 us
    ppermute x3, starting transfers between devices, widened(): lax.ppermute(head, axis, [((i + 1) % count, i) for i in range(count)])  6.59 us
    ppermute x15, waiting for transfers between devices, padded(): lax.ppermute(tail, axis, [(i, (i + 1) % count) for i in range(count)])  6.21 us
    unnamed x24, local copies, waits for them, and re-layouts  6.13 us
  transfers between devices with their start and end apart: 36, of which 22 were waited for; matrix products, arithmetic and copies ran while one was open for 1% of the time, Pallas kernels for 0%

profile of v4, /device:TPU:24, one launch (start us, length us, event | category | flops | bytes accessed | tf_op | source)
XLA Modules:
  0.0 198.5 jit_solution(17392873726160131232)
XLA Ops:
  0.0 0.7 copy-done.8
  0.7 0.8 multiply_add_fusion.24
  2.0 0.6 copy-done.2
  3.3 0.7 copy-done.1
  4.1 2.7 %collective-permute-start.1 = (f32[3,5,17,3]{3,2,1,0:T(8,128)S(1)}, f32[3,5,17,3]{3,2,1,0:T(8,128)S(1)}, u32[]{:S(2)}, u32[]{:S(2)}) collective-permute-start(f32[3,5,17,3]{3,2,1,0:T(8,128)S(1)} %get-tuple-element.58), channel_id=1, source_target_pairs={{256,0},{512,256},{768,512},{0,768},{257,1},{513,257},{769,513},{1... | collective-permute-start | bytes 9188 | tf_op jit(solution)/shard_map/ppermute | solution.py:256
  6.8 14.0 %collective-permute-start = (f32[3,5,17,3]{3,2,1,0:T(8,128)S(1)}, f32[3,5,17,3]{3,2,1,0:T(8,128)S(1)}, u32[]{:S(2)}, u32[]{:S(2)}) collective-permute-start(f32[3,5,17,3]{3,2,1,0:T(8,128)S(1)} %get-tuple-element.59), channel_id=1, source_target_pairs={{0,256},{256,512},{512,768},{768,0},{1,257},{257,513},{513,769},{7... | collective-permute-start | bytes 9188 | tf_op jit(solution)/shard_map/ppermute | solution.py:255
  21.1 0.6 copy-done.7
  22.5 1.3 collective-permute-done
  24.9 1.3 collective-permute-done.3
  26.2 3.0 %collective-permute-done.2 = f32[3,5,3,133]{3,2,1,0:T(4,128)S(1)} collective-permute-done((f32[3,5,3,133]{3,2,1,0:T(4,128)S(1)}, f32[3,5,3,133]{3,2,1,0:T(4,128)S(1)}, u32[]{:S(2)}, u32[]{:S(2)}) %collective-permute-start.2) | collective-permute-done | bytes 23972 | tf_op jit(solution)/shard_map/ppermute | solution.py:255
  29.7 1.9 collective-permute-start.4
  31.7 12.6 %collective-permute-done.4 = f32[3,3,21,133]{3,2,1,0:T(8,128)S(1)} collective-permute-done((f32[3,3,21,133]{3,2,1,0:T(8,128)S(1)}, f32[3,3,21,133]{3,2,1,0:T(8,128)S(1)}, u32[]{:S(2)}, u32[]{:S(2)}) %collective-permute-start.4) | collective-permute-done | bytes 100580 | tf_op jit(solution)/shard_map/ppermute | solution.py:255
  44.4 3.9 %collective-permute-start.5 = (f32[3,3,21,133]{3,2,1,0:T(8,128)S(1)}, f32[3,3,21,133]{3,2,1,0:T(8,128)S(1)}, u32[]{:S(2)}, u32[]{:S(2)}) collective-permute-start(f32[3,3,21,133]{3,2,1,0:T(8,128)S(1)} %get-tuple-element.51), channel_id=1, source_target_pairs={{1,0},{2,1},{3,2},{4,3},{5,4},{6,5},{7,6},{8,7},{9,8},{10,9},{11,1... | collective-permute-start | bytes 301652 | tf_op jit(solution)/shard_map/ppermute | solution.py:256
  48.4 3.8 %collective-permute-done.5 = f32[3,3,21,133]{3,2,1,0:T(8,128)S(1)} collective-permute-done((f32[3,3,21,133]{3,2,1,0:T(8,128)S(1)}, f32[3,3,21,133]{3,2,1,0:T(8,128)S(1)}, u32[]{:S(2)}, u32[]{:S(2)}) %collective-permute-start.5) | collective-permute-done | bytes 100580 | tf_op jit(solution)/shard_map/ppermute | solution.py:256
  52.3 0.9 copy-done.3
  59.9 0.8 slice.1407
  60.7 0.8 slice.1405
  63.6 5.6 %collective-permute-start.6 = (f32[1,5,17,1]{3,2,1,0:T(8,128)S(1)}, f32[1,5,17,1]{3,2,1,0:T(8,128)S(1)}, u32[]{:S(2)}, u32[]{:S(2)}) collective-permute-start(f32[1,5,17,1]{3,2,1,0:T(8,128)S(1)} %get-tuple-element.165), channel_id=1, source_target_pairs={{0,256},{256,512},{512,768},{768,0},{1,257},{257,513},{513,769},{7... | collective-permute-start | bytes 1028 | tf_op jit(solution)/shard_map/ppermute | solution.py:33
  69.2 1.9 collective-permute-start.7
  71.1 5.4 %collective-permute-done.7 = f32[1,5,17,1]{3,2,1,0:T(8,128)S(1)} collective-permute-done((f32[1,5,17,1]{3,2,1,0:T(8,128)S(1)}, f32[1,5,17,1]{3,2,1,0:T(8,128)S(1)}, u32[]{:S(2)}, u32[]{:S(2)}) %collective-permute-start.7) | collective-permute-done | bytes 372 | tf_op jit(solution)/shard_map/ppermute | solution.py:35
  76.6 2.9 %collective-permute-start.9 = (f32[1,5,1,131]{3,2,1,0:T(1,128)S(1)}, f32[1,5,1,131]{3,2,1,0:T(1,128)S(1)}, u32[]{:S(2)}, u32[]{:S(2)}) collective-permute-start(f32[1,5,1,131]{3,2,1,0:T(1,128)S(1)} %get-tuple-element.64), channel_id=1, source_target_pairs={{32,0},{64,32},{96,64},{128,96},{160,128},{192,160},{224,192},{0,2... | collective-permute-start | bytes 7868 | tf_op jit(solution)/shard_map/ppermute | solution.py:35
  79.9 1.0 collective-permute-done.8
  81.1 1.9 collective-permute-start.10
  83.0 5.3 %collective-permute-start.11 = (f32[1,1,19,131]{3,2,1,0:T(8,128)S(1)}, f32[1,1,19,131]{3,2,1,0:T(8,128)S(1)}, u32[]{:S(2)}, u32[]{:S(2)}) collective-permute-start(f32[1,1,19,131]{3,2,1,0:T(8,128)S(1)} %get-tuple-element.164), channel_id=1, source_target_pairs={{1,0},{2,1},{3,2},{4,3},{5,4},{6,5},{7,6},{8,7},{9,8},{10,9},{11,1... | collective-permute-start | bytes 29876 | tf_op jit(solution)/shard_map/ppermute | solution.py:35
  88.4 1.2 collective-permute-done.11
  89.8 0.6 copy-done.10
  91.3 0.8 slice.1462
  92.2 0.8 slice.1460
  96.7 0.6 slice-done
  97.5 1.9 collective-permute-start.12
  99.4 3.9 %collective-permute-start.13 = (f32[2,3,9,1]{3,2,1,0:T(8,128)S(1)}, f32[2,3,9,1]{3,2,1,0:T(8,128)S(1)}, u32[]{:S(2)}, u32[]{:S(2)}) collective-permute-start(f32[2,3,9,1]{3,2,1,0:T(8,128)S(1)} %get-tuple-element.294), channel_id=1, source_target_pairs={{256,0},{512,256},{768,512},{0,768},{257,1},{513,257},{769,513},{1... | collective-permute-start | bytes 656 | tf_op jit(solution)/shard_map/ppermute | solution.py:35
  103.4 3.1 %collective-permute-done.13 = f32[2,3,9,1]{3,2,1,0:T(8,128)S(1)} collective-permute-done((f32[2,3,9,1]{3,2,1,0:T(8,128)S(1)}, f32[2,3,9,1]{3,2,1,0:T(8,128)S(1)}, u32[]{:S(2)}, u32[]{:S(2)}) %collective-permute-start.13) | collective-permute-done | bytes 248 | tf_op jit(solution)/shard_map/ppermute | solution.py:35
  106.7 2.9 %collective-permute-start.15 = (f32[2,3,1,67]{3,2,1,0:T(1,128)S(1)}, f32[2,3,1,67]{3,2,1,0:T(1,128)S(1)}, u32[]{:S(2)}, u32[]{:S(2)}) collective-permute-start(f32[2,3,1,67]{3,2,1,0:T(1,128)S(1)} %get-tuple-element.149), channel_id=1, source_target_pairs={{32,0},{64,32},{96,64},{128,96},{160,128},{192,160},{224,192},{0,2... | collective-permute-start | bytes 4832 | tf_op jit(solution)/shard_map/ppermute | solution.py:35
  109.7 1.3 collective-permute-done.14
  111.1 1.9 collective-permute-start.16
  113.0 5.4 %collective-permute-start.17 = (f32[2,1,11,67]{3,2,1,0:T(8,128)S(1)}, f32[2,1,11,67]{3,2,1,0:T(8,128)S(1)}, u32[]{:S(2)}, u32[]{:S(2)}) collective-permute-start(f32[2,1,11,67]{3,2,1,0:T(8,128)S(1)} %get-tuple-element.292), channel_id=1, source_target_pairs={{1,0},{2,1},{3,2},{4,3},{5,4},{6,5},{7,6},{8,7},{9,8},{10,9},{11,1... | collective-permute-start | bytes 17696 | tf_op jit(solution)/shard_map/ppermute | solution.py:35
  118.5 1.4 collective-permute-done.17
  120.0 0.6 copy-done.6
  120.8 0.6 copy-done.5
  123.6 1.9 collective-permute-start.18
  125.5 3.9 %collective-permute-start.19 = (f32[1,3,9,1]{3,2,1,0:T(8,128)S(1)}, f32[1,3,9,1]{3,2,1,0:T(8,128)S(1)}, u32[]{:S(2)}, u32[]{:S(2)}) collective-permute-start(f32[1,3,9,1]{3,2,1,0:T(8,128)S(1)} %get-tuple-element.342), channel_id=1, source_target_pairs={{256,0},{512,256},{768,512},{0,768},{257,1},{513,257},{769,513},{1... | collective-permute-start | bytes 332 | tf_op jit(solution)/shard_map/ppermute | solution.py:35
  129.4 3.0 %collective-permute-done.19 = f32[1,3,9,1]{3,2,1,0:T(8,128)S(1)} collective-permute-done((f32[1,3,9,1]{3,2,1,0:T(8,128)S(1)}, f32[1,3,9,1]{3,2,1,0:T(8,128)S(1)}, u32[]{:S(2)}, u32[]{:S(2)}) %collective-permute-start.19) | collective-permute-done | bytes 140 | tf_op jit(solution)/shard_map/ppermute | solution.py:35
  132.5 3.0 %collective-permute-start.21 = (f32[1,3,1,67]{3,2,1,0:T(1,128)S(1)}, f32[1,3,1,67]{3,2,1,0:T(1,128)S(1)}, u32[]{:S(2)}, u32[]{:S(2)}) collective-permute-start(f32[1,3,1,67]{3,2,1,0:T(1,128)S(1)} %get-tuple-element.172), channel_id=1, source_target_pairs={{32,0},{64,32},{96,64},{128,96},{160,128},{192,160},{224,192},{0,2... | collective-permute-start | bytes 2420 | tf_op jit(solution)/shard_map/ppermute | solution.py:35
  135.5 1.3 collective-permute-done.20
  136.9 1.9 collective-permute-start.22
  138.8 5.4 %collective-permute-start.23 = (f32[1,1,11,67]{3,2,1,0:T(8,128)S(1)}, f32[1,1,11,67]{3,2,1,0:T(8,128)S(1)}, u32[]{:S(2)}, u32[]{:S(2)}) collective-permute-start(f32[1,1,11,67]{3,2,1,0:T(8,128)S(1)} %get-tuple-element.340), channel_id=1, source_target_pairs={{1,0},{2,1},{3,2},{4,3},{5,4},{6,5},{7,6},{8,7},{9,8},{10,9},{11,1... | collective-permute-start | bytes 8852 | tf_op jit(solution)/shard_map/ppermute | solution.py:35
  144.2 1.3 collective-permute-done.23
  148.0 2.1 %collective-permute-start.24 = (f32[1,3,9,1]{3,2,1,0:T(8,128)S(1)}, f32[1,3,9,1]{3,2,1,0:T(8,128)S(1)}, u32[]{:S(2)}, u32[]{:S(2)}) collective-permute-start(f32[1,3,9,1]{3,2,1,0:T(8,128)S(1)} %get-tuple-element.335), channel_id=1, source_target_pairs={{0,256},{256,512},{512,768},{768,0},{1,257},{257,513},{513,769},{7... | collective-permute-start | bytes 332 | tf_op jit(solution)/shard_map/ppermute | solution.py:33
  150.1 3.7 %collective-permute-start.25 = (f32[1,3,9,1]{3,2,1,0:T(8,128)S(1)}, f32[1,3,9,1]{3,2,1,0:T(8,128)S(1)}, u32[]{:S(2)}, u32[]{:S(2)}) collective-permute-start(f32[1,3,9,1]{3,2,1,0:T(8,128)S(1)} %get-tuple-element.336), channel_id=1, source_target_pairs={{256,0},{512,256},{768,512},{0,768},{257,1},{513,257},{769,513},{1... | collective-permute-start | bytes 332 | tf_op jit(solution)/shard_map/ppermute | solution.py:35
  153.9 3.2 %collective-permute-done.25 = f32[1,3,9,1]{3,2,1,0:T(8,128)S(1)} collective-permute-done((f32[1,3,9,1]{3,2,1,0:T(8,128)S(1)}, f32[1,3,9,1]{3,2,1,0:T(8,128)S(1)}, u32[]{:S(2)}, u32[]{:S(2)}) %collective-permute-start.25) | collective-permute-done | bytes 140 | tf_op jit(solution)/shard_map/ppermute | solution.py:35
  157.2 3.0 %collective-permute-start.27 = (f32[1,3,1,67]{3,2,1,0:T(1,128)S(1)}, f32[1,3,1,67]{3,2,1,0:T(1,128)S(1)}, u32[]{:S(2)}, u32[]{:S(2)}) collective-permute-start(f32[1,3,1,67]{3,2,1,0:T(1,128)S(1)} %get-tuple-element.170), channel_id=1, source_target_pairs={{32,0},{64,32},{96,64},{128,96},{160,128},{192,160},{224,192},{0,2... | collective-permute-start | bytes 2420 | tf_op jit(solution)/shard_map/ppermute | solution.py:35
  160.1 1.3 collective-permute-done.26
  161.5 1.9 collective-permute-start.28
  163.4 5.4 %collective-permute-start.29 = (f32[1,1,11,67]{3,2,1,0:T(8,128)S(1)}, f32[1,1,11,67]{3,2,1,0:T(8,128)S(1)}, u32[]{:S(2)}, u32[]{:S(2)}) collective-permute-start(f32[1,1,11,67]{3,2,1,0:T(8,128)S(1)} %get-tuple-element.334), channel_id=1, source_target_pairs={{1,0},{2,1},{3,2},{4,3},{5,4},{6,5},{7,6},{8,7},{9,8},{10,9},{11,1... | collective-permute-start | bytes 8852 | tf_op jit(solution)/shard_map/ppermute | solution.py:35
  168.9 1.3 collective-permute-done.29
  172.6 2.7 %collective-permute-start.30 = (f32[1,3,9,1]{3,2,1,0:T(8,128)S(1)}, f32[1,3,9,1]{3,2,1,0:T(8,128)S(1)}, u32[]{:S(2)}, u32[]{:S(2)}) collective-permute-start(f32[1,3,9,1]{3,2,1,0:T(8,128)S(1)} %get-tuple-element.329), channel_id=1, source_target_pairs={{0,256},{256,512},{512,768},{768,0},{1,257},{257,513},{513,769},{7... | collective-permute-start | bytes 332 | tf_op jit(solution)/shard_map/ppermute | solution.py:33
  175.4 3.1 %collective-permute-start.31 = (f32[1,3,9,1]{3,2,1,0:T(8,128)S(1)}, f32[1,3,9,1]{3,2,1,0:T(8,128)S(1)}, u32[]{:S(2)}, u32[]{:S(2)}) collective-permute-start(f32[1,3,9,1]{3,2,1,0:T(8,128)S(1)} %get-tuple-element.330), channel_id=1, source_target_pairs={{256,0},{512,256},{768,512},{0,768},{257,1},{513,257},{769,513},{1... | collective-permute-start | bytes 332 | tf_op jit(solution)/shard_map/ppermute | solution.py:35
  178.5 3.8 %collective-permute-done.31 = f32[1,3,9,1]{3,2,1,0:T(8,128)S(1)} collective-permute-done((f32[1,3,9,1]{3,2,1,0:T(8,128)S(1)}, f32[1,3,9,1]{3,2,1,0:T(8,128)S(1)}, u32[]{:S(2)}, u32[]{:S(2)}) %collective-permute-start.31) | collective-permute-done | bytes 140 | tf_op jit(solution)/shard_map/ppermute | solution.py:35
  182.4 3.0 %collective-permute-start.33 = (f32[1,3,1,67]{3,2,1,0:T(1,128)S(1)}, f32[1,3,1,67]{3,2,1,0:T(1,128)S(1)}, u32[]{:S(2)}, u32[]{:S(2)}) collective-permute-start(f32[1,3,1,67]{3,2,1,0:T(1,128)S(1)} %get-tuple-element.168), channel_id=1, source_target_pairs={{32,0},{64,32},{96,64},{128,96},{160,128},{192,160},{224,192},{0,2... | collective-permute-start | bytes 2420 | tf_op jit(solution)/shard_map/ppermute | solution.py:35
  185.3 1.3 collective-permute-done.32
  186.7 1.9 collective-permute-start.34
  188.7 5.4 %collective-permute-start.35 = (f32[1,1,11,67]{3,2,1,0:T(8,128)S(1)}, f32[1,1,11,67]{3,2,1,0:T(8,128)S(1)}, u32[]{:S(2)}, u32[]{:S(2)}) collective-permute-start(f32[1,1,11,67]{3,2,1,0:T(8,128)S(1)} %get-tuple-element.328), channel_id=1, source_target_pairs={{1,0},{2,1},{3,2},{4,3},{5,4},{6,5},{7,6},{8,7},{9,8},{10,9},{11,1... | collective-permute-start | bytes 8852 | tf_op jit(solution)/shard_map/ppermute | solution.py:35
  194.1 1.3 collective-permute-done.35
  197.8 0.7 slice_add_fusion.4
  (413 shorter events, 27.4 us)
Async XLA Ops:
  0.0 0.7 copy-start.8
  0.0 0.7 copy-start.4
  1.9 0.7 copy-start.2
  3.1 0.8 copy-start.1
  4.1 18.3 %collective-permute-start.1 = (f32[3,5,17,3]{3,2,1,0:T(8,128)S(1)}, f32[3,5,17,3]{3,2,1,0:T(8,128)S(1)}, u32[]{:S(2)}, u32[]{:S(2)}) collective-permute-start(f32[3,5,17,3]{3,2,1,0:T(8,128)S(1)} %get-tuple-element.58), channel_id=1, source_target_pairs={{256,0},{512,256},{768,512},{0,768},{257,1},{513,257},{769,513},{1... | collective-permute-start | bytes 9188 | tf_op jit(solution)/shard_map/ppermute | solution.py:256
  6.8 17.1 %collective-permute-start = (f32[3,5,17,3]{3,2,1,0:T(8,128)S(1)}, f32[3,5,17,3]{3,2,1,0:T(8,128)S(1)}, u32[]{:S(2)}, u32[]{:S(2)}) collective-permute-start(f32[3,5,17,3]{3,2,1,0:T(8,128)S(1)} %get-tuple-element.59), channel_id=1, source_target_pairs={{0,256},{256,512},{512,768},{768,0},{1,257},{257,513},{513,769},{7... | collective-permute-start | bytes 9188 | tf_op jit(solution)/shard_map/ppermute | solution.py:255
  21.0 0.7 copy-start.7
  24.3 1.9 collective-permute-start.3
  24.4 4.9 %collective-permute-start.2 = (f32[3,5,3,133]{3,2,1,0:T(4,128)S(1)}, f32[3,5,3,133]{3,2,1,0:T(4,128)S(1)}, u32[]{:S(2)}, u32[]{:S(2)}) collective-permute-start(f32[3,5,3,133]{3,2,1,0:T(4,128)S(1)} %get-tuple-element.55), channel_id=1, source_target_pairs={{0,32},{32,64},{64,96},{96,128},{128,160},{160,192},{192,224},{224... | collective-permute-start | bytes 71828 | tf_op jit(solution)/shard_map/ppermute | solution.py:255
  29.7 14.6 %collective-permute-start.4 = (f32[3,3,21,133]{3,2,1,0:T(8,128)S(1)}, f32[3,3,21,133]{3,2,1,0:T(8,128)S(1)}, u32[]{:S(2)}, u32[]{:S(2)}) collective-permute-start(f32[3,3,21,133]{3,2,1,0:T(8,128)S(1)} %slice.1767), channel_id=1, source_target_pairs={{0,1},{1,2},{2,3},{3,4},{4,5},{5,6},{6,7},{7,8},{8,9},{9,10},{10,1... | collective-permute-start | bytes 301652 | tf_op jit(solution)/shard_map/ppermute | solution.py:255
  44.4 7.8 %collective-permute-start.5 = (f32[3,3,21,133]{3,2,1,0:T(8,128)S(1)}, f32[3,3,21,133]{3,2,1,0:T(8,128)S(1)}, u32[]{:S(2)}, u32[]{:S(2)}) collective-permute-start(f32[3,3,21,133]{3,2,1,0:T(8,128)S(1)} %get-tuple-element.51), channel_id=1, source_target_pairs={{1,0},{2,1},{3,2},{4,3},{5,4},{6,5},{7,6},{8,7},{9,8},{10,9},{11,1... | collective-permute-start | bytes 301652 | tf_op jit(solution)/shard_map/ppermute | solution.py:256
  52.2 0.9 copy-start.3
  63.6 7.6 %collective-permute-start.6 = (f32[1,5,17,1]{3,2,1,0:T(8,128)S(1)}, f32[1,5,17,1]{3,2,1,0:T(8,128)S(1)}, u32[]{:S(2)}, u32[]{:S(2)}) collective-permute-start(f32[1,5,17,1]{3,2,1,0:T(8,128)S(1)} %get-tuple-element.165), channel_id=1, source_target_pairs={{0,256},{256,512},{512,768},{768,0},{1,257},{257,513},{513,769},{7... | collective-permute-start | bytes 1028 | tf_op jit(solution)/shard_map/ppermute | solution.py:33
  69.2 7.3 %collective-permute-start.7 = (f32[1,5,17,1]{3,2,1,0:T(8,128)S(1)}, f32[1,5,17,1]{3,2,1,0:T(8,128)S(1)}, u32[]{:S(2)}, u32[]{:S(2)}) collective-permute-start(f32[1,5,17,1]{3,2,1,0:T(8,128)S(1)} %get-tuple-element.166), channel_id=1, source_target_pairs={{256,0},{512,256},{768,512},{0,768},{257,1},{513,257},{769,513},{1... | collective-permute-start | bytes 1028 | tf_op jit(solution)/shard_map/ppermute | solution.py:35
  76.6 4.3 %collective-permute-start.8 = (f32[1,5,1,131]{3,2,1,0:T(1,128)S(1)}, f32[1,5,1,131]{3,2,1,0:T(1,128)S(1)}, u32[]{:S(2)}, u32[]{:S(2)}) collective-permute-start(f32[1,5,1,131]{3,2,1,0:T(1,128)S(1)} %get-tuple-element.63), channel_id=1, source_target_pairs={{0,32},{32,64},{64,96},{96,128},{128,160},{160,192},{192,224},{224... | collective-permute-start | bytes 7868 | tf_op jit(solution)/shard_map/ppermute | solution.py:33
  76.6 4.3 %collective-permute-start.9 = (f32[1,5,1,131]{3,2,1,0:T(1,128)S(1)}, f32[1,5,1,131]{3,2,1,0:T(1,128)S(1)}, u32[]{:S(2)}, u32[]{:S(2)}) collective-permute-start(f32[1,5,1,131]{3,2,1,0:T(1,128)S(1)} %get-tuple-element.64), channel_id=1, source_target_pairs={{32,0},{64,32},{96,64},{128,96},{160,128},{192,160},{224,192},{0,2... | collective-permute-start | bytes 7868 | tf_op jit(solution)/shard_map/ppermute | solution.py:35
  81.1 7.3 %collective-permute-start.10 = (f32[1,1,19,131]{3,2,1,0:T(8,128)S(1)}, f32[1,1,19,131]{3,2,1,0:T(8,128)S(1)}, u32[]{:S(2)}, u32[]{:S(2)}) collective-permute-start(f32[1,1,19,131]{3,2,1,0:T(8,128)S(1)} %get-tuple-element.163), channel_id=1, source_target_pairs={{0,1},{1,2},{2,3},{3,4},{4,5},{5,6},{6,7},{7,8},{8,9},{9,10},{10,1... | collective-permute-start | bytes 29876 | tf_op jit(solution)/shard_map/ppermute | solution.py:33
  83.0 6.6 %collective-permute-start.11 = (f32[1,1,19,131]{3,2,1,0:T(8,128)S(1)}, f32[1,1,19,131]{3,2,1,0:T(8,128)S(1)}, u32[]{:S(2)}, u32[]{:S(2)}) collective-permute-start(f32[1,1,19,131]{3,2,1,0:T(8,128)S(1)} %get-tuple-element.164), channel_id=1, source_target_pairs={{1,0},{2,1},{3,2},{4,3},{5,4},{6,5},{7,6},{8,7},{9,8},{10,9},{11,1... | collective-permute-start | bytes 29876 | tf_op jit(solution)/shard_map/ppermute | solution.py:35
  89.7 0.7 copy-start.10
  90.5 0.7 copy-start.9
  95.4 0.7 copy-start
  96.6 0.7 slice-start
  97.5 6.0 %collective-permute-start.12 = (f32[2,3,9,1]{3,2,1,0:T(8,128)S(1)}, f32[2,3,9,1]{3,2,1,0:T(8,128)S(1)}, u32[]{:S(2)}, u32[]{:S(2)}) collective-permute-start(f32[2,3,9,1]{3,2,1,0:T(8,128)S(1)} %get-tuple-element.293), channel_id=1, source_target_pairs={{0,256},{256,512},{512,768},{768,0},{1,257},{257,513},{513,769},{7... | collective-permute-start | bytes 656 | tf_op jit(solution)/shard_map/ppermute | solution.py:33
  99.4 7.2 %collective-permute-start.13 = (f32[2,3,9,1]{3,2,1,0:T(8,128)S(1)}, f32[2,3,9,1]{3,2,1,0:T(8,128)S(1)}, u32[]{:S(2)}, u32[]{:S(2)}) collective-permute-start(f32[2,3,9,1]{3,2,1,0:T(8,128)S(1)} %get-tuple-element.294), channel_id=1, source_target_pairs={{256,0},{512,256},{768,512},{0,768},{257,1},{513,257},{769,513},{1... | collective-permute-start | bytes 656 | tf_op jit(solution)/shard_map/ppermute | solution.py:35
  106.7 4.2 %collective-permute-start.14 = (f32[2,3,1,67]{3,2,1,0:T(1,128)S(1)}, f32[2,3,1,67]{3,2,1,0:T(1,128)S(1)}, u32[]{:S(2)}, u32[]{:S(2)}) collective-permute-start(f32[2,3,1,67]{3,2,1,0:T(1,128)S(1)} %get-tuple-element.148), channel_id=1, source_target_pairs={{0,32},{32,64},{64,96},{96,128},{128,160},{160,192},{192,224},{224... | collective-permute-start | bytes 4832 | tf_op jit(solution)/shard_map/ppermute | solution.py:33
  106.7 4.3 %collective-permute-start.15 = (f32[2,3,1,67]{3,2,1,0:T(1,128)S(1)}, f32[2,3,1,67]{3,2,1,0:T(1,128)S(1)}, u32[]{:S(2)}, u32[]{:S(2)}) collective-permute-start(f32[2,3,1,67]{3,2,1,0:T(1,128)S(1)} %get-tuple-element.149), channel_id=1, source_target_pairs={{32,0},{64,32},{96,64},{128,96},{160,128},{192,160},{224,192},{0,2... | collective-permute-start | bytes 4832 | tf_op jit(solution)/shard_map/ppermute | solution.py:35
  111.1 7.4 %collective-permute-start.16 = (f32[2,1,11,67]{3,2,1,0:T(8,128)S(1)}, f32[2,1,11,67]{3,2,1,0:T(8,128)S(1)}, u32[]{:S(2)}, u32[]{:S(2)}) collective-permute-start(f32[2,1,11,67]{3,2,1,0:T(8,128)S(1)} %get-tuple-element.291), channel_id=1, source_target_pairs={{0,1},{1,2},{2,3},{3,4},{4,5},{5,6},{6,7},{7,8},{8,9},{9,10},{10,1... | collective-permute-start | bytes 17696 | tf_op jit(solution)/shard_map/ppermute | solution.py:33
  113.0 6.9 %collective-permute-start.17 = (f32[2,1,11,67]{3,2,1,0:T(8,128)S(1)}, f32[2,1,11,67]{3,2,1,0:T(8,128)S(1)}, u32[]{:S(2)}, u32[]{:S(2)}) collective-permute-start(f32[2,1,11,67]{3,2,1,0:T(8,128)S(1)} %get-tuple-element.292), channel_id=1, source_target_pairs={{1,0},{2,1},{3,2},{4,3},{5,4},{6,5},{7,6},{8,7},{9,8},{10,9},{11,1... | collective-permute-start | bytes 17696 | tf_op jit(solution)/shard_map/ppermute | solution.py:35
  120.0 0.7 copy-start.6
  120.7 0.7 copy-start.5
  123.6 5.9 %collective-permute-start.18 = (f32[1,3,9,1]{3,2,1,0:T(8,128)S(1)}, f32[1,3,9,1]{3,2,1,0:T(8,128)S(1)}, u32[]{:S(2)}, u32[]{:S(2)}) collective-permute-start(f32[1,3,9,1]{3,2,1,0:T(8,128)S(1)} %get-tuple-element.341), channel_id=1, source_target_pairs={{0,256},{256,512},{512,768},{768,0},{1,257},{257,513},{513,769},{7... | collective-permute-start | bytes 332 | tf_op jit(solution)/shard_map/ppermute | solution.py:33
  125.5 6.9 %collective-permute-start.19 = (f32[1,3,9,1]{3,2,1,0:T(8,128)S(1)}, f32[1,3,9,1]{3,2,1,0:T(8,128)S(1)}, u32[]{:S(2)}, u32[]{:S(2)}) collective-permute-start(f32[1,3,9,1]{3,2,1,0:T(8,128)S(1)} %get-tuple-element.342), channel_id=1, source_target_pairs={{256,0},{512,256},{768,512},{0,768},{257,1},{513,257},{769,513},{1... | collective-permute-start | bytes 332 | tf_op jit(solution)/shard_map/ppermute | solution.py:35
  132.5 4.2 %collective-permute-start.20 = (f32[1,3,1,67]{3,2,1,0:T(1,128)S(1)}, f32[1,3,1,67]{3,2,1,0:T(1,128)S(1)}, u32[]{:S(2)}, u32[]{:S(2)}) collective-permute-start(f32[1,3,1,67]{3,2,1,0:T(1,128)S(1)} %get-tuple-element.171), channel_id=1, source_target_pairs={{0,32},{32,64},{64,96},{96,128},{128,160},{160,192},{192,224},{224... | collective-permute-start | bytes 2420 | tf_op jit(solution)/shard_map/ppermute | solution.py:33
  132.5 4.3 %collective-permute-start.21 = (f32[1,3,1,67]{3,2,1,0:T(1,128)S(1)}, f32[1,3,1,67]{3,2,1,0:T(1,128)S(1)}, u32[]{:S(2)}, u32[]{:S(2)}) collective-permute-start(f32[1,3,1,67]{3,2,1,0:T(1,128)S(1)} %get-tuple-element.172), channel_id=1, source_target_pairs={{32,0},{64,32},{96,64},{128,96},{160,128},{192,160},{224,192},{0,2... | collective-permute-start | bytes 2420 | tf_op jit(solution)/shard_map/ppermute | solution.py:35
  136.9 7.3 %collective-permute-start.22 = (f32[1,1,11,67]{3,2,1,0:T(8,128)S(1)}, f32[1,1,11,67]{3,2,1,0:T(8,128)S(1)}, u32[]{:S(2)}, u32[]{:S(2)}) collective-permute-start(f32[1,1,11,67]{3,2,1,0:T(8,128)S(1)} %get-tuple-element.339), channel_id=1, source_target_pairs={{0,1},{1,2},{2,3},{3,4},{4,5},{5,6},{6,7},{7,8},{8,9},{9,10},{10,1... | collective-permute-start | bytes 8852 | tf_op jit(solution)/shard_map/ppermute | solution.py:33
  138.8 6.8 %collective-permute-start.23 = (f32[1,1,11,67]{3,2,1,0:T(8,128)S(1)}, f32[1,1,11,67]{3,2,1,0:T(8,128)S(1)}, u32[]{:S(2)}, u32[]{:S(2)}) collective-permute-start(f32[1,1,11,67]{3,2,1,0:T(8,128)S(1)} %get-tuple-element.340), channel_id=1, source_target_pairs={{1,0},{2,1},{3,2},{4,3},{5,4},{6,5},{7,6},{8,7},{9,8},{10,9},{11,1... | collective-permute-start | bytes 8852 | tf_op jit(solution)/shard_map/ppermute | solution.py:35
  148.0 5.9 %collective-permute-start.24 = (f32[1,3,9,1]{3,2,1,0:T(8,128)S(1)}, f32[1,3,9,1]{3,2,1,0:T(8,128)S(1)}, u32[]{:S(2)}, u32[]{:S(2)}) collective-permute-start(f32[1,3,9,1]{3,2,1,0:T(8,128)S(1)} %get-tuple-element.335), channel_id=1, source_target_pairs={{0,256},{256,512},{512,768},{768,0},{1,257},{257,513},{513,769},{7... | collective-permute-start | bytes 332 | tf_op jit(solution)/shard_map/ppermute | solution.py:33
  150.1 6.9 %collective-permute-start.25 = (f32[1,3,9,1]{3,2,1,0:T(8,128)S(1)}, f32[1,3,9,1]{3,2,1,0:T(8,128)S(1)}, u32[]{:S(2)}, u32[]{:S(2)}) collective-permute-start(f32[1,3,9,1]{3,2,1,0:T(8,128)S(1)} %get-tuple-element.336), channel_id=1, source_target_pairs={{256,0},{512,256},{768,512},{0,768},{257,1},{513,257},{769,513},{1... | collective-permute-start | bytes 332 | tf_op jit(solution)/shard_map/ppermute | solution.py:35
  157.1 4.2 %collective-permute-start.26 = (f32[1,3,1,67]{3,2,1,0:T(1,128)S(1)}, f32[1,3,1,67]{3,2,1,0:T(1,128)S(1)}, u32[]{:S(2)}, u32[]{:S(2)}) collective-permute-start(f32[1,3,1,67]{3,2,1,0:T(1,128)S(1)} %get-tuple-element.169), channel_id=1, source_target_pairs={{0,32},{32,64},{64,96},{96,128},{128,160},{160,192},{192,224},{224... | collective-permute-start | bytes 2420 | tf_op jit(solution)/shard_map/ppermute | solution.py:33
  157.2 4.3 %collective-permute-start.27 = (f32[1,3,1,67]{3,2,1,0:T(1,128)S(1)}, f32[1,3,1,67]{3,2,1,0:T(1,128)S(1)}, u32[]{:S(2)}, u32[]{:S(2)}) collective-permute-start(f32[1,3,1,67]{3,2,1,0:T(1,128)S(1)} %get-tuple-element.170), channel_id=1, source_target_pairs={{32,0},{64,32},{96,64},{128,96},{160,128},{192,160},{224,192},{0,2... | collective-permute-start | bytes 2420 | tf_op jit(solution)/shard_map/ppermute | solution.py:35
  161.5 7.3 %collective-permute-start.28 = (f32[1,1,11,67]{3,2,1,0:T(8,128)S(1)}, f32[1,1,11,67]{3,2,1,0:T(8,128)S(1)}, u32[]{:S(2)}, u32[]{:S(2)}) collective-permute-start(f32[1,1,11,67]{3,2,1,0:T(8,128)S(1)} %get-tuple-element.333), channel_id=1, source_target_pairs={{0,1},{1,2},{2,3},{3,4},{4,5},{5,6},{6,7},{7,8},{8,9},{9,10},{10,1... | collective-permute-start | bytes 8852 | tf_op jit(solution)/shard_map/ppermute | solution.py:33
  163.4 6.8 %collective-permute-start.29 = (f32[1,1,11,67]{3,2,1,0:T(8,128)S(1)}, f32[1,1,11,67]{3,2,1,0:T(8,128)S(1)}, u32[]{:S(2)}, u32[]{:S(2)}) collective-permute-start(f32[1,1,11,67]{3,2,1,0:T(8,128)S(1)} %get-tuple-element.334), channel_id=1, source_target_pairs={{1,0},{2,1},{3,2},{4,3},{5,4},{6,5},{7,6},{8,7},{9,8},{10,9},{11,1... | collective-permute-start | bytes 8852 | tf_op jit(solution)/shard_map/ppermute | solution.py:35
  172.6 5.9 %collective-permute-start.30 = (f32[1,3,9,1]{3,2,1,0:T(8,128)S(1)}, f32[1,3,9,1]{3,2,1,0:T(8,128)S(1)}, u32[]{:S(2)}, u32[]{:S(2)}) collective-permute-start(f32[1,3,9,1]{3,2,1,0:T(8,128)S(1)} %get-tuple-element.329), channel_id=1, source_target_pairs={{0,256},{256,512},{512,768},{768,0},{1,257},{257,513},{513,769},{7... | collective-permute-start | bytes 332 | tf_op jit(solution)/shard_map/ppermute | solution.py:33
  175.4 6.9 %collective-permute-start.31 = (f32[1,3,9,1]{3,2,1,0:T(8,128)S(1)}, f32[1,3,9,1]{3,2,1,0:T(8,128)S(1)}, u32[]{:S(2)}, u32[]{:S(2)}) collective-permute-start(f32[1,3,9,1]{3,2,1,0:T(8,128)S(1)} %get-tuple-element.330), channel_id=1, source_target_pairs={{256,0},{512,256},{768,512},{0,768},{257,1},{513,257},{769,513},{1... | collective-permute-start | bytes 332 | tf_op jit(solution)/shard_map/ppermute | solution.py:35
  182.4 4.2 %collective-permute-start.32 = (f32[1,3,1,67]{3,2,1,0:T(1,128)S(1)}, f32[1,3,1,67]{3,2,1,0:T(1,128)S(1)}, u32[]{:S(2)}, u32[]{:S(2)}) collective-permute-start(f32[1,3,1,67]{3,2,1,0:T(1,128)S(1)} %get-tuple-element.167), channel_id=1, source_target_pairs={{0,32},{32,64},{64,96},{96,128},{128,160},{160,192},{192,224},{224... | collective-permute-start | bytes 2420 | tf_op jit(solution)/shard_map/ppermute | solution.py:33
  182.4 4.3 %collective-permute-start.33 = (f32[1,3,1,67]{3,2,1,0:T(1,128)S(1)}, f32[1,3,1,67]{3,2,1,0:T(1,128)S(1)}, u32[]{:S(2)}, u32[]{:S(2)}) collective-permute-start(f32[1,3,1,67]{3,2,1,0:T(1,128)S(1)} %get-tuple-element.168), channel_id=1, source_target_pairs={{32,0},{64,32},{96,64},{128,96},{160,128},{192,160},{224,192},{0,2... | collective-permute-start | bytes 2420 | tf_op jit(solution)/shard_map/ppermute | solution.py:35
  186.7 7.3 %collective-permute-start.34 = (f32[1,1,11,67]{3,2,1,0:T(8,128)S(1)}, f32[1,1,11,67]{3,2,1,0:T(8,128)S(1)}, u32[]{:S(2)}, u32[]{:S(2)}) collective-permute-start(f32[1,1,11,67]{3,2,1,0:T(8,128)S(1)} %get-tuple-element.327), channel_id=1, source_target_pairs={{0,1},{1,2},{2,3},{3,4},{4,5},{5,6},{6,7},{7,8},{8,9},{9,10},{10,1... | collective-permute-start | bytes 8852 | tf_op jit(solution)/shard_map/ppermute | solution.py:33
  188.7 6.8 %collective-permute-start.35 = (f32[1,1,11,67]{3,2,1,0:T(8,128)S(1)}, f32[1,1,11,67]{3,2,1,0:T(8,128)S(1)}, u32[]{:S(2)}, u32[]{:S(2)}) collective-permute-start(f32[1,1,11,67]{3,2,1,0:T(8,128)S(1)} %get-tuple-element.328), channel_id=1, source_target_pairs={{1,0},{2,1},{3,2},{4,3},{5,4},{6,5},{7,6},{8,7},{9,8},{10,9},{11,1... | collective-permute-start | bytes 8852 | tf_op jit(solution)/shard_map/ppermute | solution.py:35
